TPU v7x, 512 devices: a whole 4x8x8 slice. The times are simulated.
512 devices in a mesh: seq: 64 (over z, x, y_lo), tensor: 8 (over y_hi, core).
Axes of the slice: x: 4, y: 8 (y_hi: 4, y_lo: 2; y = y_hi * 2 + y_lo), z: 8, core: 2. Of those that a mesh axis runs over, the one named last changes fastest.
Arguments:
- hidden_in: bfloat16 [8192, 2560], P('seq', 'tensor'), may hold values from -6 to 6
- norm_gain: float32 [2560], replicated, may hold values from 0.1 to 1.9
- w_query: bfloat16 [2560, 2048], P(None, 'tensor'), may hold values from -0.125 to 0.125
- w_key: bfloat16 [2560, 1024], P(None, 'tensor'), may hold values from -0.125 to 0.125
- w_value: bfloat16 [2560, 1024], P(None, 'tensor'), may hold values from -0.125 to 0.125
- w_out: bfloat16 [2048, 2560], P('tensor'), may hold values from -0.125 to 0.125
- q_gain: float32 [128], replicated, may hold values from 0.1 to 1.9
- k_gain: float32 [128], replicated, may hold values from 0.1 to 1.9
- lengths: int32 [16], replicated, may hold values from 1 to 6144, 8192 in all
Outputs:
- attn_out: bfloat16 [8192, 2560], P(('seq', 'tensor'))
- key_cache: bfloat16 [8192, 1024], P('seq', 'tensor')
- value_cache: bfloat16 [8192, 1024], P('seq', 'tensor')
Inputs may be any that keep to these rules, and one draw needn't show every extreme that they name: The lengths sum to 8192 and the largest is exactly 6144.
All inputs are finite; a program needn't handle non-finite values.
Results may differ from a plain program's by a relative error of at most 0.015.
Values may be sent and summed in bfloat16 or wider, within the bound.
No kernel may reach another device: no remote copies, remote signals or barrier semaphores. Data moves between devices by JAX's collectives and lax.ppermute only.
A program may use at most 64 MiB of HBM per device.

v0:
```python
import math

import jax
import jax.numpy as jnp
from jax import lax
from jax.sharding import PartitionSpec as P

rope_base = 1000000.0
norm_eps = 1e-06
masked = -1e30


def prompt_starts(lengths, token_pos):
    ends = jnp.cumsum(lengths)
    starts = ends - lengths
    before = (ends[None, :] <= token_pos[:, None]).astype(jnp.int32)
    segment = jnp.sum(before, axis=1)
    onehot = segment[:, None] == jnp.arange(lengths.shape[0], dtype=jnp.int32)[None, :]
    return jnp.sum(jnp.where(onehot, starts[None, :], 0), axis=1)


def head_norm_rope(values, gain, rel_pos):
    width = values.shape[-1]
    half = width // 2
    mean_sq = jnp.mean(values * values, axis=-1, keepdims=True)
    normed = values * lax.rsqrt(mean_sq + norm_eps) * gain
    freq = rope_base ** (-jnp.arange(half, dtype=jnp.float32) * 2.0 / width)
    angle = rel_pos.astype(jnp.float32)[:, None] * freq[None, :]
    cosine = jnp.cos(angle)[:, None, :]
    sine = jnp.sin(angle)[:, None, :]
    first = normed[..., :half]
    second = normed[..., half:]
    return jnp.concatenate(
        [first * cosine - second * sine, second * cosine + first * sine], axis=-1
    )


def on_device(hidden_in, norm_gain, w_query, w_key, w_value, w_out, q_gain, k_gain, lengths):
    tokens = hidden_in.shape[0]
    width = w_query.shape[0]
    head_dim = q_gain.shape[0]
    q_cols = w_query.shape[1]
    kv_cols = w_key.shape[1]
    kv_local = kv_cols // head_dim
    group = q_cols // kv_cols
    combined = jnp.concatenate([w_query, w_key, w_value], axis=1)
    piece = lax.all_gather(hidden_in, "tensor", axis=1, tiled=True)
    wide = piece.astype(jnp.float32)
    rows = combined
    scaled = (wide * norm_gain[None, :]).astype(jnp.bfloat16)
    acc = jnp.dot(scaled, rows, preferred_element_type=jnp.float32)
    acc, sumsq = (acc, jnp.sum(wide * wide, axis=1))
    proj = acc * lax.rsqrt(sumsq / width + norm_eps)[:, None]
    block_index = lax.axis_index("seq")
    token_pos = block_index * tokens + jnp.arange(tokens, dtype=jnp.int32)
    seg_start = prompt_starts(lengths, token_pos)
    rel_pos = token_pos - seg_start
    queries = head_norm_rope(
        proj[:, :q_cols].reshape(tokens, kv_local * group, head_dim), q_gain, rel_pos
    ).astype(jnp.bfloat16)
    keys = head_norm_rope(
        proj[:, q_cols : q_cols + kv_cols].reshape(tokens, kv_local, head_dim), k_gain, rel_pos
    ).astype(jnp.bfloat16)
    key_flat = keys.reshape(tokens, kv_cols)
    value_flat = proj[:, q_cols + kv_cols :].astype(jnp.bfloat16)
    query_grid = queries.reshape(tokens, kv_local, group, head_dim)
    inv_root = 1.0 / math.sqrt(head_dim)
    last_pos = jnp.max(token_pos)
    first_start = jnp.min(seg_start)

    def attend_block(carry, key_block, value_block, key_start):
        rows = key_block.shape[0]
        key_pos = key_start + jnp.arange(rows, dtype=jnp.int32)

        def compute(state):
            best, total, summed = state
            key_heads = key_block.reshape(rows, kv_local, head_dim)
            value_heads = value_block.reshape(rows, kv_local, head_dim)
            score = (
                jnp.einsum(
                    "qhgd,khd->hgqk", query_grid, key_heads, preferred_element_type=jnp.float32
                )
                * inv_root
            )
            visible = (key_pos[None, :] >= seg_start[:, None]) & (
                key_pos[None, :] <= token_pos[:, None]
            )
            score = jnp.where(visible[None, None], score, masked)
            fresh = jnp.maximum(best, jnp.max(score, axis=-1))
            weights = jnp.where(visible[None, None], jnp.exp(score - fresh[..., None]), 0.0)
            decay = jnp.exp(best - fresh)
            total = total * decay + jnp.sum(weights, axis=-1)
            summed = summed * decay[..., None] + jnp.einsum(
                "hgqk,khd->hgqd",
                weights.astype(jnp.bfloat16),
                value_heads,
                preferred_element_type=jnp.float32,
            )
            return (fresh, total, summed)

        seen = (key_start <= last_pos) & (key_start + rows - 1 >= first_start)
        return lax.cond(seen, compute, lambda state: state, carry)

    start_state = (
        jnp.full((kv_local, group, tokens), masked, jnp.float32),
        jnp.zeros((kv_local, group, tokens), jnp.float32),
        jnp.zeros((kv_local, group, tokens, head_dim), jnp.float32),
    )
    key_piece = lax.all_gather(key_flat, "seq", axis=0, tiled=True)
    value_piece = lax.all_gather(value_flat, "seq", axis=0, tiled=True)
    rows = key_piece.shape[0]
    size = math.gcd(rows, 512)
    count = rows // size

    def one_part(state, part):
        key_part, value_part, offset = part
        return (attend_block(state, key_part, value_part, offset), None)

    offsets = jnp.arange(count, dtype=jnp.int32) * size
    parts = (
        key_piece.reshape(count, size, kv_cols),
        value_piece.reshape(count, size, kv_cols),
        offsets,
    )
    state, unused = lax.scan(one_part, start_state, parts)
    best, total, summed = state
    attn = summed / total[..., None]
    attn = jnp.transpose(attn, (2, 0, 1, 3)).reshape(tokens, q_cols).astype(jnp.bfloat16)
    mixed = lax.psum_scatter(
        jnp.dot(attn, w_out, preferred_element_type=jnp.float32).astype(jnp.bfloat16),
        "tensor",
        scatter_dimension=0,
        tiled=True,
    )
    return (mixed, key_flat, value_flat)


def solution(mesh):
    placed = (
        P("seq", "tensor"),
        P(),
        P(None, "tensor"),
        P(None, "tensor"),
        P(None, "tensor"),
        P("tensor", None),
        P(),
        P(),
        P(),
    )
    return jax.shard_map(
        on_device,
        mesh=mesh,
        in_specs=placed,
        out_specs=(P(("seq", "tensor"), None), P("seq", "tensor"), P("seq", "tensor")),
        check_vma=False,
    )
```

profile of v0, /device:TPU:6, one launch (start us, length us, event | category | flops | bytes accessed | tf_op | source)
XLA Modules:
  0.0 771.4 jit_solution(8246726257521450109)
XLA Ops:
  7.2 0.8 copy.30
  8.2 0.7 sub.38
  9.1 0.7 subtract_convert_fusion.1
  9.8 18.2 %all_gather.9 = bf16[128,2560]{0,1:T(8,128)(2,1)S(1)} all-gather(bf16[128,320]{0,1:T(8,128)(2,1)} %param.13), channel_id=1, replica_groups=mesh['seq'=64,'tensor'=8] {'tensor'}, dimensions={1}, use_global_device_ids=true | all-gather | bytes 737280 | tf_op jit(solution)/shard_map/all_gather | solution.py:47
  28.4 3.1 fusion.29
  32.0 0.7 pad_maximum_fusion.1
  32.8 0.6 slice.64
  33.5 0.7 fusion.48
  35.2 295.3 %all-gather.3.cloned.1.call-done = bf16[8192,128]{1,0:T(8,128)(2,1)} async-done(((bf16[128,128]{1,0:T(8,128)(2,1)}), bf16[8192,128]{1,0:T(8,128)(2,1)}) %all-gather.3.cloned.1.call-update) | async-done | bytes 2097168 | tf_op jit(solution)/shard_map/all_gather | solution.py:109
  330.6 302.9 %all-gather.5.cloned.1.call-done = bf16[8192,128]{1,0:T(8,128)(2,1)} async-done(((bf16[128,128]{1,0:T(8,128)(2,1)}), bf16[8192,128]{1,0:T(8,128)(2,1)}) %all-gather.5.cloned.1.call-update) | async-done | bytes 2097168 | tf_op jit(solution)/shard_map/all_gather | solution.py:110
  633.5 52.3 %while.19 = (s32[]{:T(128)}, f32[1,2,128]{2,1,0:T(2,128)S(1)}, f32[1,2,128]{2,1,0:T(2,128)S(1)}, f32[1,2,128,128]{3,2,1,0:T(8,128)S(1)}, s32[16]{0:T(128)S(1)}, ...) while((s32[]{:T(128)}, f32[1,2,128]{2,1,0:T(2,128)S(1)}, ...), condition=%wide.region_13.14_spmd.clone, body=%wide.region_8.13_spmd.clone.sunk | while | flops 68552072 | bytes 2453335 | solution.py:125
  633.5 0.6 dynamic_slice.41
  636.6 0.6 dynamic_slice.41
  639.6 3.4 conditional.3
  640.4 1.2 fusion.49
  641.7 1.3 fusion.4
  643.0 0.6 dynamic_slice.41
  646.1 0.6 dynamic_slice.41
  649.1 0.6 dynamic_slice.41
  652.2 0.6 dynamic_slice.41
  655.3 0.6 dynamic_slice.41
  658.3 0.6 dynamic_slice.41
  661.4 0.6 dynamic_slice.41
  664.4 0.6 dynamic_slice.41
  667.5 0.6 dynamic_slice.41
  670.5 0.6 dynamic_slice.41
  673.6 0.6 dynamic_slice.41
  676.7 0.6 dynamic_slice.41
  679.7 0.6 dynamic_slice.41
  682.8 0.6 dynamic_slice.41
  686.0 1.2 convolution_convert_fusion
  687.2 77.6 %reduce-scatter.2.cloned.1.call-done = bf16[16,2560]{1,0:T(8,128)(2,1)} async-done(((bf16[128,2560]{1,0:T(8,128)(2,1)}), bf16[16,2560]{1,0:T(8,128)(2,1)}) %reduce-scatter.2.cloned.1.call-update) | async-done | bytes 81936 | tf_op jit(solution)/shard_map/reduce_scatter | solution.py:129
  (93 shorter events, 3.7 us)
Async XLA Ops:
  7.2 678.8 %copy-start = (bf16[256,2560]{1,0:T(8,128)(2,1)S(1)}, bf16[256,2560]{1,0:T(8,128)(2,1)}, u32[]{:S(2)}) copy-start(bf16[256,2560]{1,0:T(8,128)(2,1)} %param.18) | copy-start | bytes 3932164
  7.2 323.4 %all-gather.3.cloned.1.call-start = ((), (), s32[]{:S(2)}) async-start(), calls=%async_computation.1 | async-start | bytes 2129920 | tf_op jit(solution)/shard_map/all_gather | solution.py:109
  28.4 3.2 copy-start.1
  28.4 6.6 copy-start.2
  32.7 600.8 %all-gather.5.cloned.1.call-start = ((), (), s32[]{:S(2)}) async-start(), calls=%async_computation.2 | async-start | bytes 2129920 | tf_op jit(solution)/shard_map/all_gather | solution.py:110
  33.5 731.4 %reduce-scatter.2.cloned.1.call-start = ((), (), s32[]{:S(2)}) async-start(), calls=%async_computation.3 | async-start | bytes 737280 | tf_op jit(solution)/shard_map/reduce_scatter | solution.py:129
Sparse Core Ops, SparseCore 0:
  32.9 297.6 all-gather.2
  333.2 300.2 all-gather.4
  687.3 77.4 reduce-scatter.1
where the time goes:
time: 773 us; the launch traced here: 771 us
  waiting for transfers between devices  676 us (87%)
  loops' own time  39.7 us (5%)
  blocking collectives  18.2 us (2%)
  between operations  13.9 us (2%)
  local copies, waits for them, and re-layouts  11 us (1%)
    all_gather x1, waiting for transfers between devices, on_device(): value_piece = lax.all_gather(value_flat, 'seq', axis=0, tiled=True)  303 us
    all_gather x1, waiting for transfers between devices, on_device(): key_piece = lax.all_gather(key_flat, 'seq', axis=0, tiled=True)  295 us
    reduce_scatter x1, waiting for transfers between devices, on_device(): lax.psum_scatter(jnp.dot(attn, w_out, preferred_element_type=jnp.float32)...  77.6 us
    another operation x1, loops' own time, on_device(): state, unused = lax.scan(one_part, start_state, parts)  39.4 us
    all_gather x1, blocking collectives, on_device(): piece = lax.all_gather(hidden_in, 'tensor', axis=1, tiled=True)  18.2 us
  transfers between devices with their start and end apart: 3, of which 3 were waited for; matrix products, arithmetic and copies ran while one was open for 0% of the time, Pallas kernels for 0%

commit v1 on v0

v1 whole, which is shorter than its diff:
```python
import math

import jax
import jax.numpy as jnp
from jax import lax
from jax.sharding import Mesh
from jax.sharding import PartitionSpec as P

rope_base = 1000000.0
norm_eps = 1e-06
masked = -1e30
max_len = 6144

SEQ = ("z", "x", "ylo")
TEN = ("yhi", "core")


def prompt_starts(lengths, token_pos):
    ends = jnp.cumsum(lengths)
    starts = ends - lengths
    before = (ends[None, :] <= token_pos[:, None]).astype(jnp.int32)
    segment = jnp.sum(before, axis=1)
    onehot = segment[:, None] == jnp.arange(lengths.shape[0], dtype=jnp.int32)[None, :]
    return jnp.sum(jnp.where(onehot, starts[None, :], 0), axis=1)


def head_norm_rope(values, gain, rel_pos):
    width = values.shape[-1]
    half = width // 2
    mean_sq = jnp.mean(values * values, axis=-1, keepdims=True)
    normed = values * lax.rsqrt(mean_sq + norm_eps) * gain
    freq = rope_base ** (-jnp.arange(half, dtype=jnp.float32) * 2.0 / width)
    angle = rel_pos.astype(jnp.float32)[:, None] * freq[None, :]
    cosine = jnp.cos(angle)[:, None, :]
    sine = jnp.sin(angle)[:, None, :]
    first = normed[..., :half]
    second = normed[..., half:]
    return jnp.concatenate(
        [first * cosine - second * sine, second * cosine + first * sine], axis=-1
    )


def on_device(hidden_in, norm_gain, w_query, w_key, w_value, w_out, q_gain, k_gain, lengths):
    tokens = hidden_in.shape[0]
    width = w_query.shape[0]
    head_dim = q_gain.shape[0]
    q_cols = w_query.shape[1]
    kv_cols = w_key.shape[1]
    kv_local = kv_cols // head_dim
    group = q_cols // kv_cols
    combined = jnp.concatenate([w_query, w_key, w_value], axis=1)
    piece = lax.all_gather(hidden_in, TEN, axis=1, tiled=True)
    wide = piece.astype(jnp.float32)
    scaled = (wide * norm_gain[None, :]).astype(jnp.bfloat16)
    acc = jnp.dot(scaled, combined, preferred_element_type=jnp.float32)
    sumsq = jnp.sum(wide * wide, axis=1)
    proj = acc * lax.rsqrt(sumsq / width + norm_eps)[:, None]
    block_index = lax.axis_index(SEQ)
    token_pos = block_index * tokens + jnp.arange(tokens, dtype=jnp.int32)
    seg_start = prompt_starts(lengths, token_pos)
    rel_pos = token_pos - seg_start
    queries = head_norm_rope(
        proj[:, :q_cols].reshape(tokens, kv_local * group, head_dim), q_gain, rel_pos
    ).astype(jnp.bfloat16)
    keys = head_norm_rope(
        proj[:, q_cols : q_cols + kv_cols].reshape(tokens, kv_local, head_dim), k_gain, rel_pos
    ).astype(jnp.bfloat16)
    key_flat = keys.reshape(tokens, kv_cols)
    value_flat = proj[:, q_cols + kv_cols :].astype(jnp.bfloat16)

    kv = jnp.concatenate([key_flat, value_flat], axis=1)
    kv = lax.all_gather(kv, "ylo", axis=0, tiled=True)
    kv = lax.all_gather(kv, "x", axis=0, tiled=True)
    kv = lax.all_gather(kv, "z", axis=0, tiled=True)
    rows = kv.shape[0]
    blocks = rows // tokens
    window = min(blocks, -(-(max_len - 1) // tokens) + 1)
    first_block = jnp.minimum(jnp.min(seg_start) // tokens, blocks - window)
    span = window * tokens
    kv_win = lax.dynamic_slice_in_dim(kv, first_block * tokens, span, 0)
    key_pos = first_block * tokens + jnp.arange(span, dtype=jnp.int32)
    key_heads = kv_win[:, :kv_cols].reshape(span, kv_local, head_dim)
    value_heads = kv_win[:, kv_cols:].reshape(span, kv_local, head_dim)
    query_grid = queries.reshape(tokens, kv_local, group, head_dim)
    inv_root = 1.0 / math.sqrt(head_dim)
    score = (
        jnp.einsum("qhgd,khd->hgqk", query_grid, key_heads, preferred_element_type=jnp.float32)
        * inv_root
    )
    visible = (key_pos[None, :] >= seg_start[:, None]) & (key_pos[None, :] <= token_pos[:, None])
    score = jnp.where(visible[None, None], score, masked)
    top = jnp.max(score, axis=-1, keepdims=True)
    weights = jnp.where(visible[None, None], jnp.exp(score - top), 0.0)
    denom = jnp.sum(weights, axis=-1)
    summed = jnp.einsum(
        "hgqk,khd->hgqd",
        weights.astype(jnp.bfloat16),
        value_heads,
        preferred_element_type=jnp.float32,
    )
    attn = summed / denom[..., None]
    attn = jnp.transpose(attn, (2, 0, 1, 3)).reshape(tokens, q_cols).astype(jnp.bfloat16)
    part = jnp.dot(attn, w_out, preferred_element_type=jnp.float32).astype(jnp.bfloat16)
    nyhi = lax.axis_size("yhi")
    ncore = lax.axis_size("core")
    chunk = tokens // (nyhi * ncore)
    part = part.reshape(nyhi, ncore, chunk, -1).transpose(1, 0, 2, 3).reshape(tokens, -1)
    part = lax.psum_scatter(part, "core", scatter_dimension=0, tiled=True)
    mixed = lax.psum_scatter(part, "yhi", scatter_dimension=0, tiled=True)
    return (mixed, key_flat, value_flat)


def solution(mesh):
    devices = mesh.devices
    nseq, nten = devices.shape
    nz = len({d.coords[2] for d in devices[:, 0]})
    nx = len({d.coords[0] for d in devices[:, 0]})
    ncore = len({d.core_on_chip for d in devices[0, :]})
    split = Mesh(devices.reshape(nz, nx, nseq // (nz * nx), nten // ncore, ncore), SEQ + TEN)
    seq, ten = SEQ, TEN
    placed = (
        P(seq, ten),
        P(),
        P(None, ten),
        P(None, ten),
        P(None, ten),
        P(ten, None),
        P(),
        P(),
        P(),
    )
    return jax.shard_map(
        on_device,
        mesh=split,
        in_specs=placed,
        out_specs=(P(seq + ten, None), P(seq, ten), P(seq, ten)),
        check_vma=False,
    )
```

time: 773 us -> 173 us (0.22)
  waiting for transfers between devices: 676 us -> 101 us
  loops' own time: 39.7 us -> 0 us
  blocking collectives: 18.2 us -> 36.9 us
  local copies, waits for them, and re-layouts: 11 us -> 1.16 us
    all_gather x2 -> x1, waiting for transfers between devices: 598 us -> 54.3 us  [on_device(): kv = lax.all_gather(kv, 'z', axis=0, tiled=True)]
    another operation x17 -> x0, loops' own time: 39.7 us -> none  [the longest x1 39.4 us: on_device(): state, unused = lax.scan(one_part, start_state, parts)]
    reduce_scatter x1 -> x2, waiting for transfers between devices: 77.6 us -> 46.8 us  [the longest x1 32.5 us: on_device(): mixed = lax.psum_scatter(part, 'yhi', scatter_dimension=0, tiled=True)]
    all_gather x1 -> x3, blocking collectives: 18.2 us -> 36.9 us  [the longest x1 18.4 us: on_device(): piece = lax.all_gather(hidden_in, TEN, axis=1, tiled=True)]
    dynamic_slice x16 -> x0, local copies, waits for them, and re-layouts: 9.25 us -> none  [on_device(): state, unused = lax.scan(one_part, start_state, parts)]
  transfers between devices with their start and end apart: 3 -> 3, of which waited for: 3 -> 3; matrix products, arithmetic and copies ran while one was open for 0% -> 3% of each run, Pallas kernels for 0% -> 0%
where the time goes in v1:
time: 173 us
  waiting for transfers between devices  101 us (58%)
  blocking collectives  36.9 us (21%)
  between operations  16.6 us (10%)
  matrix products  9.05 us (5%)
  other arithmetic  7.55 us (4%)
    all_gather x1, waiting for transfers between devices, on_device(): kv = lax.all_gather(kv, 'z', axis=0, tiled=True)  54.3 us
    reduce_scatter x1, waiting for transfers between devices, on_device(): mixed = lax.psum_scatter(part, 'yhi', scatter_dimension=0, tiled=True)  32.5 us
    all_gather x1, blocking collectives, on_device(): piece = lax.all_gather(hidden_in, TEN, axis=1, tiled=True)  18.4 us
    reduce_scatter x1, waiting for transfers between devices, on_device(): part = lax.psum_scatter(part, 'core', scatter_dimension=0, tiled=True)  14.3 us
    all_gather x1, blocking collectives, on_device(): kv = lax.all_gather(kv, 'x', axis=0, tiled=True)  13.6 us
    all_gather x1, blocking collectives, on_device(): kv = lax.all_gather(kv, 'ylo', axis=0, tiled=True)  5 us
  transfers between devices with their start and end apart: 3, of which 3 were waited for; matrix products, arithmetic and copies ran while one was open for 3% of the time, Pallas kernels for 0%

profile of v1, /device:TPU:6, one launch (start us, length us, event | category | flops | bytes accessed | tf_op | source)
XLA Modules:
  0.0 172.5 jit_solution(9770259826407538624)
XLA Ops:
  7.2 18.4 %all_gather.12 = bf16[128,2560]{0,1:T(8,128)(2,1)S(1)} all-gather(bf16[128,320]{0,1:T(8,128)(2,1)} %param.9), channel_id=1, replica_groups=mesh['z'=8,'x'=4,'ylo'=2,'yhi'=4,'core'=2] {'yhi','core'}, dimensions={1}, use_global_device_ids=true | all-gather | bytes 737280 | tf_op jit(solution)/shard_map/all_gather | solution.py:52
  25.6 0.4 fusion.17
  26.0 3.1 %fusion.18 = f32[128,512]{1,0:T(8,128)S(1)} fusion(bf16[2560,128]{1,0:T(8,128)(2,1)} %param.13, bf16[2560,128]{1,0:T(8,128)(2,1)} %param.12, bf16[2560,256]{1,0:T(8,128)(2,1)} %param.11, bf16[128,2560]{0,1:T(8,128)(2,1)S(1)} %all_gather.12, f32[2560]{0:T(1024)} %param.10, f32[128]{0:T(128)S(1)} %add_rsqrt_fusion.2), kind=kOutput, calls=%fused_computation.25 | convolution fusion | flops 344457216 | bytes 3549696 | tf_op jit(solution)/shard_map/dot_general | solution.py:55
  29.1 0.1 multiply_reduce_fusion.1
  29.3 0.1 copy.34
  29.4 0.1 reduce.4
  29.5 0.1 convert_reduce_fusion
  29.6 0.1 select_reduce_fusion
  29.7 0.6 fusion.48
  30.3 0.1 multiply_bitcast_fusion
  30.4 0.3 fusion.42
  30.7 0.1 pad_maximum_fusion
  30.8 5.0 %all_gather.13 = bf16[256,256]{1,0:T(8,128)(2,1)S(1)} all-gather(bf16[128,256]{1,0:T(8,128)(2,1)S(1)} %pad_maximum_fusion), channel_id=1, replica_groups=mesh['z'=8,'x'=4,'ylo'=2,'yhi'=4,'core'=2] {'ylo'}, dimensions={0}, use_global_device_ids=true | all-gather | bytes 196608 | tf_op jit(solution)/shard_map/all_gather | solution.py:72
  35.8 13.6 %all_gather.14 = bf16[1024,256]{1,0:T(8,128)(2,1)} all-gather(bf16[256,256]{1,0:T(8,128)(2,1)S(1)} %all_gather.13), channel_id=1, replica_groups=mesh['z'=8,'x'=4,'ylo'=2,'yhi'=4,'core'=2] {'x'}, dimensions={0}, use_global_device_ids=true | all-gather | bytes 655360 | tf_op jit(solution)/shard_map/all_gather | solution.py:73
  49.4 0.0 reduce-scatter.3.cloned.1.call-start
  52.1 0.1 reshape.295
  52.2 0.2 multiply_reduce_fusion
  52.4 0.1 copy.35
  52.5 0.3 multiply_cosine_fusion
  52.8 0.1 fusion.29
  52.9 0.1 subtract_convert_fusion
  53.0 2.9 %compare_and_fusion = pred[128,6272]{0,1:T(8,128)(4,1)S(1)} fusion(s32[128]{0:T(128)S(1)} %iota_add_fusion.1, s32[128]{0:T(128)S(1)} %select_reduce_fusion, s32[6272]{0:T(1024)S(1)} %iota_add_fusion), kind=kLoop, calls=%fused_computation.12 | loop fusion | flops 2408448 | bytes 828928 | tf_op jit(solution)/shard_map/and | solution.py:90
  56.0 54.3 %all-gather.2.cloned.1.call-done = bf16[8192,256]{1,0:T(8,128)(2,1)} async-done(((bf16[1024,256]{1,0:T(8,128)(2,1)}), bf16[8192,256]{1,0:T(8,128)(2,1)}) %all-gather.2.cloned.1.call-update) | async-done | bytes 4194320 | tf_op jit(solution)/shard_map/all_gather | solution.py:74
  110.3 2.8 %fusion.49 = (f32[2,128]{1,0:T(2,128)S(1)}, f32[1,2,128,6272]{2,3,1,0:T(8,128)S(1)}) fusion(bf16[128,2,64]{2,0,1:T(8,128)(2,1)S(1)} %get-tuple-element.4, bf16[128,2,64]{2,0,1:T(8,128)(2,1)S(1)} %get-tuple-element.3, bf16[8192,256]{1,0:T(8,128)(2,1)} %all-gather.2.cloned.1.call-done, s32[]{:T(128)S(6)} %select_n.21, pred[128,6272]{0,1:T(8,128)(4,1)S(1)} %compare_and_fusion), kind=kOutput, calls=%fused_computation.73 | convolution fusion | flops 415989504 | bytes 8897540 | tf_op jit(solution)/shard_map/qhgd,khd->hgqk/dot_general | solution.py:87
  113.1 1.3 fusion.2
  114.4 2.8 %fusion.24 = bf16[2,128,128]{1,2,0:T(8,128)(2,1)S(1)} fusion(bf16[8192,256]{1,0:T(8,128)(2,1)} %all-gather.2.cloned.1.call-done, s32[]{:T(128)S(6)} %select_n.21, s32[]{:T(128)S(6)} %add.88, f32[1,2,128,6272]{2,3,1,0:T(8,128)S(1)} %get-tuple-element.14, f32[2,128]{1,0:T(2,128)S(1)} %get-tuple-element.13, pred[128,6272]{0,1:T(8,128)(4,1)S(1)} %compare_and_fusion, ...), kind=kOutput, calls=%fused_computation.27 | convolution fusion | flops 415924224 | bytes 8898568 | tf_op jit(solution)/shard_map/hgqk,khd->hgqd/dot_general | solution.py:95
  117.2 0.4 convolution_convert_fusion
  117.6 0.9 copy.39
  118.5 0.0 reduce-scatter.5.cloned.1.call-start
  118.5 14.3 %reduce-scatter.3.cloned.1.call-done = bf16[64,2560]{1,0:T(8,128)(2,1)} async-done(((bf16[128,2560]{1,0:T(8,128)(2,1)}), bf16[64,2560]{1,0:T(8,128)(2,1)}) %reduce-scatter.3.cloned.1.call-update) | async-done | bytes 327696 | tf_op jit(solution)/shard_map/reduce_scatter | solution.py:108
  132.9 0.7 pad_maximum_fusion.1
  133.6 32.5 %reduce-scatter.5.cloned.1.call-done = bf16[16,2560]{1,0:T(8,128)(2,1)} async-done(((bf16[64,2560]{1,0:T(8,128)(2,1)}), bf16[16,2560]{1,0:T(8,128)(2,1)}) %reduce-scatter.5.cloned.1.call-update) | async-done | bytes 81936 | tf_op jit(solution)/shard_map/reduce_scatter | solution.py:109
  (24 shorter events, 0.3 us)
Async XLA Ops:
  7.2 110.0 %copy-start = (bf16[256,2560]{1,0:T(8,128)(2,1)S(1)}, bf16[256,2560]{1,0:T(8,128)(2,1)}, u32[]{:S(2)}) copy-start(bf16[256,2560]{1,0:T(8,128)(2,1)} %param.14) | copy-start | bytes 3932164
  7.2 103.1 %all-gather.2.cloned.1.call-start = ((), (), s32[]{:S(2)}) async-start(), calls=%async_computation.2 | async-start | bytes 4718592 | tf_op jit(solution)/shard_map/all_gather | solution.py:74
  26.0 3.3 %copy-start.4 = (s32[16]{0:T(128)S(1)}, s32[16]{0:T(128)}, u32[]{:S(2)}) copy-start(s32[16]{0:T(128)} %param.17) | copy-start | bytes 196
  26.0 4.4 %copy-start.2 = (f32[128]{0:T(128)S(1)}, f32[128]{0:T(128)}, u32[]{:S(2)}) copy-start(f32[128]{0:T(128)} %param.16) | copy-start | bytes 1540
  29.1 23.7 %copy-start.3 = (f32[128]{0:T(128)S(1)}, f32[128]{0:T(128)}, u32[]{:S(2)}) copy-start(f32[128]{0:T(128)} %param.15) | copy-start | bytes 1540
  29.2 83.9 %copy-start.1 = (bf16[128,128]{1,0:T(8,128)(2,1)}, bf16[128,128]{1,0:T(8,128)(2,1)S(1)}, u32[]{:S(2)}) copy-start(bf16[128,128]{1,0:T(8,128)(2,1)S(1)} %slice.64) | copy-start | bytes 98308
  49.4 83.4 %reduce-scatter.3.cloned.1.call-start = ((), (), s32[]{:S(2)}) async-start(), calls=%async_computation.3 | async-start | bytes 983040 | tf_op jit(solution)/shard_map/reduce_scatter | solution.py:108
  118.5 47.5 %reduce-scatter.5.cloned.1.call-start = ((), (), s32[]{:S(2)}) async-start(), calls=%async_computation.4 | async-start | bytes 409600 | tf_op jit(solution)/shard_map/reduce_scatter | solution.py:109
Sparse Core Ops, SparseCore 0:
  49.6 60.6 all-gather.1
  118.6 14.1 reduce-scatter.2
  136.2 29.7 reduce-scatter.4

commit v2 on v1

--- a/solution.py
+++ b/solution.py
@@ -104,9 +104,11 @@
     nyhi = lax.axis_size("yhi")
     ncore = lax.axis_size("core")
     chunk = tokens // (nyhi * ncore)
-    part = part.reshape(nyhi, ncore, chunk, -1).transpose(1, 0, 2, 3).reshape(tokens, -1)
-    part = lax.psum_scatter(part, "core", scatter_dimension=0, tiled=True)
-    mixed = lax.psum_scatter(part, "yhi", scatter_dimension=0, tiled=True)
+    part = part.reshape(nyhi, ncore, chunk, -1).transpose(1, 0, 2, 3)
+    part = lax.all_to_all(part, "core", 0, 0, tiled=True)
+    part = jnp.sum(part.astype(jnp.float32), axis=0).astype(jnp.bfloat16)
+    part = lax.all_to_all(part, "yhi", 0, 0, tiled=True)
+    mixed = jnp.sum(part.astype(jnp.float32), axis=0).astype(jnp.bfloat16)
     return (mixed, key_flat, value_flat)
 
 

time: 173 us -> 149 us (0.86)
  waiting for transfers between devices: 101 us -> 65.7 us
  starting transfers between devices: 0.12 us -> 6.77 us
  blocking collectives: 36.9 us -> 41.2 us
    reduce_scatter x2 -> x0, waiting for transfers between devices: 46.8 us -> none  [the longest x1 32.5 us: on_device(): mixed = lax.psum_scatter(part, 'yhi', scatter_dimension=0, tiled=True)]
    all_to_all x0 -> x1, waiting for transfers between devices: none -> 11.3 us  [on_device(): part = lax.all_to_all(part, 'yhi', 0, 0, tiled=True)]
    all_to_all x0 -> x1, starting transfers between devices: none -> 6.74 us  [on_device(): part = lax.all_to_all(part, 'yhi', 0, 0, tiled=True)]
    all_to_all x0 -> x1, blocking collectives: none -> 4.26 us  [on_device(): part = lax.all_to_all(part, 'core', 0, 0, tiled=True)]
  transfers between devices with their start and end apart: 3 -> 2, of which waited for: 3 -> 2; matrix products, arithmetic and copies ran while one was open for 3% -> 3% of each run, Pallas kernels for 0% -> 0%
where the time goes in v2:
time: 149 us
  waiting for transfers between devices  65.7 us (44%)
  blocking collectives  41.2 us (28%)
  between operations  16.9 us (11%)
  other arithmetic  9.12 us (6%)
  matrix products  9.05 us (6%)
  starting transfers between devices  6.77 us (5%)
    all_gather x1, waiting for transfers between devices, on_device(): kv = lax.all_gather(kv, 'z', axis=0, tiled=True)  54.4 us
    all_gather x1, blocking collectives, on_device(): piece = lax.all_gather(hidden_in, TEN, axis=1, tiled=True)  18.4 us
    all_gather x1, blocking collectives, on_device(): kv = lax.all_gather(kv, 'x', axis=0, tiled=True)  13.6 us
    all_to_all x1, waiting for transfers between devices, on_device(): part = lax.all_to_all(part, 'yhi', 0, 0, tiled=True)  11.3 us
    all_to_all x1, starting transfers between devices, on_device(): part = lax.all_to_all(part, 'yhi', 0, 0, tiled=True)  6.74 us
    all_gather x1, blocking collectives, on_device(): kv = lax.all_gather(kv, 'ylo', axis=0, tiled=True)  5 us
    all_to_all x1, blocking collectives, on_device(): part = lax.all_to_all(part, 'core', 0, 0, tiled=True)  4.26 us
    dot_general x1, matrix products, on_device(): acc = jnp.dot(scaled, combined, preferred_element_type=jnp.float32)  3.08 us
  transfers between devices with their start and end apart: 2, of which 2 were waited for; matrix products, arithmetic and copies ran while one was open for 3% of the time, Pallas kernels for 0%

profile of v2, /device:TPU:6, one launch (start us, length us, event | category | flops | bytes accessed | tf_op | source)
XLA Modules:
  0.0 149.1 jit_solution(11111703942229193401)
XLA Ops:
  7.2 18.4 %all_gather.12 = bf16[128,2560]{0,1:T(8,128)(2,1)S(1)} all-gather(bf16[128,320]{0,1:T(8,128)(2,1)} %param.9), channel_id=1, replica_groups=mesh['z'=8,'x'=4,'ylo'=2,'yhi'=4,'core'=2] {'yhi','core'}, dimensions={1}, use_global_device_ids=true | all-gather | bytes 737280 | tf_op jit(solution)/shard_map/all_gather | solution.py:52
  25.6 0.4 fusion.17
  26.0 3.1 %fusion.18 = f32[128,512]{1,0:T(8,128)S(1)} fusion(bf16[2560,128]{1,0:T(8,128)(2,1)} %param.13, bf16[2560,128]{1,0:T(8,128)(2,1)} %param.12, bf16[2560,256]{1,0:T(8,128)(2,1)} %param.11, bf16[128,2560]{0,1:T(8,128)(2,1)S(1)} %all_gather.12, f32[2560]{0:T(1024)} %param.10, f32[128]{0:T(128)S(1)} %add_rsqrt_fusion.2), kind=kOutput, calls=%fused_computation.25 | convolution fusion | flops 344457216 | bytes 3549696 | tf_op jit(solution)/shard_map/dot_general | solution.py:55
  29.1 0.1 multiply_reduce_fusion.1
  29.3 0.1 copy.32
  29.4 0.1 reduce.6
  29.5 0.1 convert_reduce_fusion
  29.6 0.1 select_reduce_fusion
  29.7 0.6 fusion.48
  30.3 0.1 multiply_bitcast_fusion
  30.4 0.3 fusion.42
  30.7 0.1 pad_maximum_fusion
  30.8 5.0 %all_gather.13 = bf16[256,256]{1,0:T(8,128)(2,1)S(1)} all-gather(bf16[128,256]{1,0:T(8,128)(2,1)S(1)} %pad_maximum_fusion), channel_id=1, replica_groups=mesh['z'=8,'x'=4,'ylo'=2,'yhi'=4,'core'=2] {'ylo'}, dimensions={0}, use_global_device_ids=true | all-gather | bytes 196608 | tf_op jit(solution)/shard_map/all_gather | solution.py:72
  35.8 13.6 %all_gather.14 = bf16[1024,256]{1,0:T(8,128)(2,1)} all-gather(bf16[256,256]{1,0:T(8,128)(2,1)S(1)} %all_gather.13), channel_id=1, replica_groups=mesh['z'=8,'x'=4,'ylo'=2,'yhi'=4,'core'=2] {'x'}, dimensions={0}, use_global_device_ids=true | all-gather | bytes 655360 | tf_op jit(solution)/shard_map/all_gather | solution.py:73
  52.1 0.1 reshape.292
  52.1 0.2 multiply_reduce_fusion
  52.4 0.1 copy.33
  52.5 0.3 multiply_cosine_fusion
  52.8 0.1 fusion.29
  52.9 0.1 subtract_convert_fusion
  53.0 2.9 %compare_and_fusion = pred[128,6272]{0,1:T(8,128)(4,1)S(1)} fusion(s32[128]{0:T(128)S(1)} %iota_add_fusion.1, s32[128]{0:T(128)S(1)} %select_reduce_fusion, s32[6272]{0:T(1024)S(1)} %iota_add_fusion), kind=kLoop, calls=%fused_computation.12 | loop fusion | flops 2408448 | bytes 828928 | tf_op jit(solution)/shard_map/and | solution.py:90
  55.9 54.4 %all-gather.2.cloned.1.call-done = bf16[8192,256]{1,0:T(8,128)(2,1)} async-done(((bf16[1024,256]{1,0:T(8,128)(2,1)}), bf16[8192,256]{1,0:T(8,128)(2,1)}) %all-gather.2.cloned.1.call-update) | async-done | bytes 4194320 | tf_op jit(solution)/shard_map/all_gather | solution.py:74
  110.3 2.8 %fusion.49 = (f32[2,128]{1,0:T(2,128)S(1)}, f32[1,2,128,6272]{2,3,1,0:T(8,128)S(1)}) fusion(bf16[128,2,64]{2,0,1:T(8,128)(2,1)S(1)} %get-tuple-element.4, bf16[128,2,64]{2,0,1:T(8,128)(2,1)S(1)} %get-tuple-element.3, bf16[8192,256]{1,0:T(8,128)(2,1)} %all-gather.2.cloned.1.call-done, s32[]{:T(128)S(6)} %select_n.21, pred[128,6272]{0,1:T(8,128)(4,1)S(1)} %compare_and_fusion), kind=kOutput, calls=%fused_computation.74 | convolution fusion | flops 415989504 | bytes 8897540 | tf_op jit(solution)/shard_map/qhgd,khd->hgqk/dot_general | solution.py:87
  113.1 1.3 fusion.2
  114.4 2.8 %fusion.24 = bf16[2,128,128]{1,2,0:T(8,128)(2,1)S(1)} fusion(bf16[8192,256]{1,0:T(8,128)(2,1)} %all-gather.2.cloned.1.call-done, s32[]{:T(128)S(6)} %select_n.21, s32[]{:T(128)S(6)} %add.84, f32[1,2,128,6272]{2,3,1,0:T(8,128)S(1)} %get-tuple-element.14, f32[2,128]{1,0:T(2,128)S(1)} %get-tuple-element.13, pred[128,6272]{0,1:T(8,128)(4,1)S(1)} %compare_and_fusion, ...), kind=kOutput, calls=%fused_computation.27 | convolution fusion | flops 415924224 | bytes 8898568 | tf_op jit(solution)/shard_map/hgqk,khd->hgqd/dot_general | solution.py:95
  117.2 0.4 convolution_convert_fusion
  117.6 4.3 %all_to_all.10 = bf16[2,4,16,2560]{3,2,1,0:T(8,128)(2,1)S(1)} all-to-all(bf16[2,4,16,2560]{3,2,1,0:T(8,128)(2,1)S(1)} %bitcast.50), channel_id=1, replica_groups=mesh['z'=8,'x'=4,'ylo'=2,'yhi'=4,'core'=2] {'core'}, dimensions={0} | all-to-all | bytes 1310720 | tf_op jit(solution)/shard_map/all_to_all | solution.py:108
  121.9 0.9 reduce_sum.84
  122.8 6.7 %all-to-all-start.1 = ((bf16[4,16,2560]{2,1,0:T(8,128)(2,1)}), bf16[4,16,2560]{2,1,0:T(8,128)(2,1)S(1)}, u32[]{:S(2)}, u32[]{:S(2)}) async-start(bf16[4,16,2560]{2,1,0:T(8,128)(2,1)} %reduce_sum.84), calls=%async_computation.1 | async-start | bytes 655360 | tf_op jit(solution)/shard_map/all_to_all | solution.py:110
  129.5 0.7 pad_maximum_fusion.1
  130.2 11.3 %all-to-all-done.1 = bf16[4,16,2560]{2,1,0:T(8,128)(2,1)S(1)} async-done(((bf16[4,16,2560]{2,1,0:T(8,128)(2,1)}), bf16[4,16,2560]{2,1,0:T(8,128)(2,1)S(1)}, u32[]{:S(2)}, u32[]{:S(2)}) %all-to-all-start.1) | async-done | bytes 327712 | tf_op jit(solution)/shard_map/all_to_all | solution.py:110
  141.5 0.7 reduce_sum.85
  (23 shorter events, 0.3 us)
Async XLA Ops:
  7.2 110.0 %copy-start = (bf16[256,2560]{1,0:T(8,128)(2,1)S(1)}, bf16[256,2560]{1,0:T(8,128)(2,1)}, u32[]{:S(2)}) copy-start(bf16[256,2560]{1,0:T(8,128)(2,1)} %param.14) | copy-start | bytes 3932164
  7.2 103.1 %all-gather.2.cloned.1.call-start = ((), (), s32[]{:S(2)}) async-start(), calls=%async_computation.2 | async-start | bytes 4718592 | tf_op jit(solution)/shard_map/all_gather | solution.py:74
  26.0 3.3 %copy-start.4 = (s32[16]{0:T(128)S(1)}, s32[16]{0:T(128)}, u32[]{:S(2)}) copy-start(s32[16]{0:T(128)} %param.17) | copy-start | bytes 196
  26.0 4.4 %copy-start.2 = (f32[128]{0:T(128)S(1)}, f32[128]{0:T(128)}, u32[]{:S(2)}) copy-start(f32[128]{0:T(128)} %param.16) | copy-start | bytes 1540
  29.1 23.7 %copy-start.3 = (f32[128]{0:T(128)S(1)}, f32[128]{0:T(128)}, u32[]{:S(2)}) copy-start(f32[128]{0:T(128)} %param.15) | copy-start | bytes 1540
  29.2 83.9 %copy-start.1 = (bf16[128,128]{1,0:T(8,128)(2,1)}, bf16[128,128]{1,0:T(8,128)(2,1)S(1)}, u32[]{:S(2)}) copy-start(bf16[128,128]{1,0:T(8,128)(2,1)S(1)} %slice.64) | copy-start | bytes 98308
  122.8 18.8 %all-to-all-start.1 = ((bf16[4,16,2560]{2,1,0:T(8,128)(2,1)}), bf16[4,16,2560]{2,1,0:T(8,128)(2,1)S(1)}, u32[]{:S(2)}, u32[]{:S(2)}) async-start(bf16[4,16,2560]{2,1,0:T(8,128)(2,1)} %reduce_sum.84), calls=%async_computation.1 | async-start | bytes 655360 | tf_op jit(solution)/shard_map/all_to_all | solution.py:110
Sparse Core Ops, SparseCore 0:
  49.6 60.6 all-gather.1

commit v3 on v2

--- a/solution.py
+++ b/solution.py
@@ -68,10 +68,16 @@
     key_flat = keys.reshape(tokens, kv_cols)
     value_flat = proj[:, q_cols + kv_cols :].astype(jnp.bfloat16)
 
-    kv = jnp.concatenate([key_flat, value_flat], axis=1)
-    kv = lax.all_gather(kv, "ylo", axis=0, tiled=True)
-    kv = lax.all_gather(kv, "x", axis=0, tiled=True)
-    kv = lax.all_gather(kv, "z", axis=0, tiled=True)
+    nz, nx, nlo = lax.axis_size("z"), lax.axis_size("x"), lax.axis_size("ylo")
+    kg = lax.all_gather(key_flat, "ylo", axis=0, tiled=True)
+    kg = lax.all_gather(kg, "x", axis=0, tiled=True)
+    kg = lax.all_gather(kg, "z", axis=0, tiled=True)
+    vg = lax.all_gather(value_flat, "z", axis=0, tiled=False)
+    vg = lax.all_gather(vg, "ylo", axis=1, tiled=False)
+    vg = jnp.broadcast_to(vg[None], (nx,) + vg.shape)
+    vg = lax.all_to_all(vg, "x", 0, 1, tiled=False)
+    vg = vg.reshape(nz * nx * nlo * tokens, kv_cols)
+    kv = jnp.concatenate([kg, vg], axis=1)
     rows = kv.shape[0]
     blocks = rows // tokens
     window = min(blocks, -(-(max_len - 1) // tokens) + 1)

time: 149 us -> 150 us (level); the launches traced: 149 us -> 148 us
  waiting for transfers between devices: 65.7 us -> 1.71 us
  blocking collectives: 41.2 us -> 95.6 us
  local copies, waits for them, and re-layouts: 0.33 us -> 8.9 us
  other arithmetic: 9.12 us -> 14.3 us
  matrix products: 9.05 us -> 6.27 us
  starting transfers between devices: 6.77 us -> 4.54 us
    all_gather x1, waiting for transfers between devices: 54.4 us -> 0.01 us  [on_device(): kg = lax.all_gather(kg, 'z', axis=0, tiled=True)]
    all_gather x2 -> x4, blocking collectives: 18.6 us -> 56.3 us  [the longest x1 31.7 us: on_device(): vg = lax.all_gather(value_flat, 'z', axis=0, tiled=False)]
    all_to_all x0 -> x1, blocking collectives: none -> 16.9 us  [on_device(): part = lax.all_to_all(part, 'yhi', 0, 0, tiled=True)]
    all_to_all x1, waiting for transfers between devices: 11.3 us -> 1.69 us  [on_device(): vg = lax.all_to_all(vg, 'x', 0, 1, tiled=False)]
    another operation x1 -> x2, local copies, waits for them, and re-layouts: 0.08 us -> 2.68 us  [the longest x1 1.87 us: on_device(): vg = lax.all_to_all(vg, 'x', 0, 1, tiled=False)]
    concatenate x1, other arithmetic: 0.09 us -> 2.33 us  [on_device(): kv = jnp.concatenate([kg, vg], axis=1)]
    all_to_all x1, starting transfers between devices: 6.74 us -> 4.5 us  [on_device(): vg = lax.all_to_all(vg, 'x', 0, 1, tiled=False)]
    slice x1, local copies, waits for them, and re-layouts: 0.02 us -> 1.57 us  [on_device(): proj[:, :q_cols].reshape(tokens, kv_local * group, head_dim)]
  transfers between devices with their start and end apart: 2 -> 2, of which waited for: 2 -> 1; matrix products, arithmetic and copies ran while one was open for 3% -> 10% of each run, Pallas kernels for 0% -> 0%
where the time goes in v3:
time: 150 us; the launch traced here: 148 us
  blocking collectives  95.6 us (64%)
  between operations  16.9 us (11%)
  other arithmetic  14.3 us (10%)
  local copies, waits for them, and re-layouts  8.9 us (6%)
  matrix products  6.27 us (4%)
  starting transfers between devices  4.54 us (3%)
  waiting for transfers between devices  1.71 us (1%)
    all_gather x1, blocking collectives, on_device(): vg = lax.all_gather(value_flat, 'z', axis=0, tiled=False)  31.7 us
    all_gather x1, blocking collectives, on_device(): piece = lax.all_gather(hidden_in, TEN, axis=1, tiled=True)  18.2 us
    all_to_all x1, blocking collectives, on_device(): part = lax.all_to_all(part, 'yhi', 0, 0, tiled=True)  16.9 us
    all_gather x1, blocking collectives, on_device(): kg = lax.all_gather(kg, 'x', axis=0, tiled=True)  13 us
    all_gather x1, blocking collectives, on_device(): vg = lax.all_gather(vg, 'ylo', axis=1, tiled=False)  7.03 us
    all_gather x1, blocking collectives, on_device(): kg = lax.all_gather(key_flat, 'ylo', axis=0, tiled=True)  4.57 us
    all_to_all x1, starting transfers between devices, on_device(): vg = lax.all_to_all(vg, 'x', 0, 1, tiled=False)  4.5 us
    and x1, other arithmetic, on_device(): (key_pos[None, :] >= seg_start[:, None]) & (key_pos[None, :] <= token_pos...  4.35 us
  transfers between devices with their start and end apart: 2, of which 1 were waited for; matrix products, arithmetic and copies ran while one was open for 10% of the time, Pallas kernels for 0%

profile of v3, /device:TPU:6, one launch (start us, length us, event | category | flops | bytes accessed | tf_op | source)
XLA Modules:
  0.0 148.2 jit_solution(15727035299212685136)
XLA Ops:
  7.3 0.8 copy.34
  8.2 0.7 sub.28
  9.1 0.6 subtract_convert_fusion.1
  9.7 18.2 %all_gather.24 = bf16[128,2560]{0,1:T(8,128)(2,1)S(1)} all-gather(bf16[128,320]{0,1:T(8,128)(2,1)} %param.9), channel_id=1, replica_groups=mesh['z'=8,'x'=4,'ylo'=2,'yhi'=4,'core'=2] {'yhi','core'}, dimensions={1}, use_global_device_ids=true | all-gather | bytes 737280 | tf_op jit(solution)/shard_map/all_gather | solution.py:52
  27.9 0.4 fusion.18
  28.3 3.1 %fusion.19 = f32[128,512]{1,0:T(8,128)S(1)} fusion(bf16[2560,128]{1,0:T(8,128)(2,1)} %param.13, bf16[2560,128]{1,0:T(8,128)(2,1)} %param.12, bf16[2560,256]{1,0:T(8,128)(2,1)} %param.11, bf16[128,2560]{0,1:T(8,128)(2,1)S(1)} %all_gather.24, f32[2560]{0:T(1024)} %param.10, f32[128]{0:T(128)S(1)} %add_rsqrt_fusion.2), kind=kOutput, calls=%fused_computation.28 | convolution fusion | flops 344457216 | bytes 3549696 | tf_op jit(solution)/shard_map/dot_general | solution.py:55
  31.6 0.3 fusion.43
  32.1 0.6 copy-done.3
  32.7 4.6 %all_gather.25 = bf16[256,128]{1,0:T(8,128)(2,1)S(1)} all-gather(bf16[128,128]{1,0:T(8,128)(2,1)S(1)} %pad_maximum_fusion), channel_id=1, replica_groups=mesh['z'=8,'x'=4,'ylo'=2,'yhi'=4,'core'=2] {'ylo'}, dimensions={0}, use_global_device_ids=true | all-gather | bytes 98304 | tf_op jit(solution)/shard_map/all_gather | solution.py:72
  37.2 13.0 %all_gather.26 = bf16[1024,128]{1,0:T(8,128)(2,1)} all-gather(bf16[256,128]{1,0:T(8,128)(2,1)S(1)} %all_gather.25), channel_id=1, replica_groups=mesh['z'=8,'x'=4,'ylo'=2,'yhi'=4,'core'=2] {'x'}, dimensions={0}, use_global_device_ids=true | all-gather | bytes 327680 | tf_op jit(solution)/shard_map/all_gather | solution.py:73
  50.3 31.7 %all-gather = bf16[1024,128]{1,0:T(8,128)(2,1)S(1)} all-gather(bf16[128,128]{1,0:T(8,128)(2,1)S(1)} %slice.74), channel_id=2, replica_groups=mesh['z'=8,'x'=4,'ylo'=2,'yhi'=4,'core'=2] {'z'}, dimensions={0}, use_global_device_ids=true | all-gather | bytes 294912 | tf_op jit(solution)/shard_map/all_gather | solution.py:75
  82.0 7.0 %all-gather.1 = bf16[8,256,128]{2,1,0:T(8,128)(2,1)S(1)} all-gather(bf16[8,128,128]{2,1,0:T(8,128)(2,1)S(1)} %bitcast.60), channel_id=3, replica_groups=mesh['z'=8,'x'=4,'ylo'=2,'yhi'=4,'core'=2] {'ylo'}, dimensions={1}, use_global_device_ids=true | all-gather | bytes 786432 | tf_op jit(solution)/shard_map/all_gather | solution.py:76
  89.0 1.9 %broadcast_in_dim_broadcast_in_dim.2 = bf16[4,8,1,2,128,128]{5,4,3,1,2,0:T(8,128)(2,1)} broadcast(bf16[8,2,128,128]{3,2,1,0:T(8,128)(2,1)S(1)} %bitcast.59), dimensions={1,3,4,5} | broadcast | bytes 2621440 | tf_op jit(solution)/shard_map/broadcast_in_dim;broadcast_in_dim | solution.py:78
  90.9 4.5 %all-to-all-start = ((bf16[4,8,1,2,128,128]{5,4,3,1,2,0:T(8,128)(2,1)}), bf16[4,8,1,2,128,128]{5,4,3,1,2,0:T(8,128)(2,1)S(1)}, u32[]{:S(2)}, u32[]{:S(2)}) async-start(bf16[4,8,1,2,128,128]{5,4,3,1,2,0:T(8,128)(2,1)} %broadcast_in_dim_broadcast_in_dim.2), calls=%async_computation | async-start | bytes 4194304 | tf_op jit(solution)/shard_map/all_to_all | solution.py:78
  98.0 1.6 %fusion.47 = (f32[128,256]{1,0:T(8,128)}, f32[16,2,8,128]{3,2,1,0:T(8,128)S(1)}) fusion(f32[128,512]{1,0:T(8,128)} %copy-done.2), kind=kLoop, calls=%fused_computation.73 | loop fusion | bytes 393216 | tf_op jit(solution)/shard_map/slice | solution.py:63
  99.6 1.6 %reshape.293 = f32[128,2,128]{2,1,0:T(2,128)} reshape(f32[128,256]{1,0:T(8,128)} %get-tuple-element.5) | data formatting | bytes 262144 | tf_op jit(solution)/shard_map/reshape | solution.py:63
  101.2 1.7 %multiply_reduce_fusion = f32[128,2]{1,0:T(8,128)} fusion(f32[128,2,128]{2,1,0:T(2,128)} %reshape.293), kind=kLoop, calls=%fused_computation.37 | loop fusion | flops 65280 | bytes 132096 | tf_op jit(solution)/shard_map/reduce_sum | solution.py:30
  102.9 0.9 copy.36
  103.9 0.3 multiply_cosine_fusion
  104.2 0.8 fusion.30
  105.0 4.4 %compare_and_fusion = pred[128,6272]{0,1:T(8,128)(4,1)} fusion(s32[128]{0:T(128)} %copy-done.6, s32[128]{0:T(128)S(1)} %select_reduce_fusion, s32[6272]{0:T(1024)S(1)} %iota_add_fusion), kind=kLoop, calls=%fused_computation.15 | loop fusion | flops 2408448 | bytes 828928 | tf_op jit(solution)/shard_map/and | solution.py:96
  109.4 1.7 %all-to-all-done = bf16[4,8,1,2,128,128]{5,4,3,1,2,0:T(8,128)(2,1)S(1)} async-done(((bf16[4,8,1,2,128,128]{5,4,3,1,2,0:T(8,128)(2,1)}), bf16[4,8,1,2,128,128]{5,4,3,1,2,0:T(8,128)(2,1)S(1)}, u32[]{:S(2)}, u32[]{:S(2)}) %all-to-all-start) | async-done | bytes 2097184 | tf_op jit(solution)/shard_map/all_to_all | solution.py:78
  111.1 1.4 copy.35
  112.5 2.3 %fusion.4 = bf16[6272,256]{1,0:T(8,128)(2,1)S(1)} fusion(s32[]{:T(128)S(6)} %select_n.21, bf16[8192,128]{1,0:T(8,128)(2,1)} %all-gather.4.cloned.1.call-done, bf16[8192,128]{1,0:T(8,128)(2,1)} %bitcast.56), kind=kLoop, calls=%fused_computation.9 | loop fusion | flops 6422528 | bytes 7405572 | tf_op jit(solution)/shard_map/concatenate | solution.py:80
  114.9 1.5 fusion.48
  116.3 1.3 fusion.2
  117.6 1.4 fusion.25
  119.0 0.4 convolution_convert_fusion
  119.4 4.3 %all_to_all.25 = bf16[2,4,16,2560]{3,2,1,0:T(8,128)(2,1)S(1)} all-to-all(bf16[2,4,16,2560]{3,2,1,0:T(8,128)(2,1)S(1)} %bitcast.58), channel_id=1, replica_groups=mesh['z'=8,'x'=4,'ylo'=2,'yhi'=4,'core'=2] {'core'}, dimensions={0} | all-to-all | bytes 1310720 | tf_op jit(solution)/shard_map/all_to_all | solution.py:114
  123.6 0.2 reduce_sum.84
  123.8 16.9 %all_to_all.26 = bf16[4,16,2560]{2,1,0:T(8,128)(2,1)S(1)} all-to-all(bf16[4,16,2560]{2,1,0:T(8,128)(2,1)S(1)} %reduce_sum.84), channel_id=1, replica_groups=mesh['z'=8,'x'=4,'ylo'=2,'yhi'=4,'core'=2] {'yhi'}, dimensions={0} | all-to-all | bytes 655360 | tf_op jit(solution)/shard_map/all_to_all | solution.py:116
  140.7 0.7 reduce_sum.85
  (32 shorter events, 0.9 us)
Async XLA Ops:
  7.2 111.8 %copy-start = (bf16[256,2560]{1,0:T(8,128)(2,1)S(1)}, bf16[256,2560]{1,0:T(8,128)(2,1)}, u32[]{:S(2)}) copy-start(bf16[256,2560]{1,0:T(8,128)(2,1)} %param.14) | copy-start | bytes 3932164
  7.2 105.3 %all-gather.4.cloned.1.call-start = ((), (), s32[]{:S(2)}) async-start(), calls=%async_computation.3 | async-start | bytes 2359296 | tf_op jit(solution)/shard_map/all_gather | solution.py:74
  7.3 21.0 %copy-start.6 = (s32[128]{0:T(128)}, s32[128]{0:T(128)S(1)}, u32[]{:S(2)}) copy-start(s32[128]{0:T(128)S(1)} %iota_add_fusion.1) | copy-start | bytes 1540
  28.3 3.2 %copy-start.5 = (f32[128]{0:T(128)S(1)}, f32[128]{0:T(128)}, u32[]{:S(2)}) copy-start(f32[128]{0:T(128)} %param.16) | copy-start | bytes 1540
  31.4 59.5 %copy-start.2 = (f32[128,512]{1,0:T(8,128)}, f32[128,512]{1,0:T(8,128)S(1)}, u32[]{:S(2)}) copy-start(f32[128,512]{1,0:T(8,128)S(1)} %fusion.19) | copy-start | bytes 786436
  32.0 0.6 copy-start.3
  50.3 38.7 %copy-start.4 = (bf16[128,128]{1,0:T(8,128)(2,1)}, bf16[128,128]{1,0:T(8,128)(2,1)S(1)}, u32[]{:S(2)}) copy-start(bf16[128,128]{1,0:T(8,128)(2,1)S(1)} %slice.74) | copy-start | bytes 98308
  90.9 20.2 %all-to-all-start = ((bf16[4,8,1,2,128,128]{5,4,3,1,2,0:T(8,128)(2,1)}), bf16[4,8,1,2,128,128]{5,4,3,1,2,0:T(8,128)(2,1)S(1)}, u32[]{:S(2)}, u32[]{:S(2)}) async-start(bf16[4,8,1,2,128,128]{5,4,3,1,2,0:T(8,128)(2,1)} %broadcast_in_dim_broadcast_in_dim.2), calls=%async_computation | async-start | bytes 4194304 | tf_op jit(solution)/shard_map/all_to_all | solution.py:78
  112.5 2.3 %copy-start.1 = (pred[128,6272]{0,1:T(8,128)(4,1)S(1)}, pred[128,6272]{0,1:T(8,128)(4,1)}, u32[]{:S(2)}) copy-start(pred[128,6272]{0,1:T(8,128)(4,1)} %compare_and_fusion) | copy-start | bytes 2408452
Sparse Core Ops, SparseCore 0:
  50.4 46.8 all-gather.3

commit v4 on v2

--- a/solution.py
+++ b/solution.py
@@ -40,6 +40,30 @@
     )
 
 
+def ring_gather(piece, inner, name, stride):
+    n = lax.axis_size(name)
+    c = lax.axis_index(name)
+    cw = [(i, (i + 1) % n) for i in range(n)]
+    ccw = [(i, (i - 1) % n) for i in range(n)]
+    pieces, ids = [piece], [c * stride + inner]
+    a = b = piece
+    for s in range(1, (n - 1) // 2 + 1):
+        a = lax.ppermute(a, name, cw)
+        b = lax.ppermute(b, name, ccw)
+        pieces += [a, b]
+        ids += [((c - s) % n) * stride + inner, ((c + s) % n) * stride + inner]
+    if n % 2 == 0:
+        far = ((c + n // 2) % n) * stride
+        m = piece.shape[0]
+        if m % 2 == 0:
+            pieces += [lax.ppermute(a[: m // 2], name, cw), lax.ppermute(b[m // 2 :], name, ccw)]
+            ids += [far + inner[: m // 2], far + inner[m // 2 :]]
+        else:
+            pieces += [lax.ppermute(a, name, cw)]
+            ids += [far + inner]
+    return jnp.concatenate(pieces, axis=0), jnp.concatenate(ids, axis=0)
+
+
 def on_device(hidden_in, norm_gain, w_query, w_key, w_value, w_out, q_gain, k_gain, lengths):
     tokens = hidden_in.shape[0]
     width = w_query.shape[0]
@@ -68,19 +92,17 @@
     key_flat = keys.reshape(tokens, kv_cols)
     value_flat = proj[:, q_cols + kv_cols :].astype(jnp.bfloat16)
 
-    kv = jnp.concatenate([key_flat, value_flat], axis=1)
-    kv = lax.all_gather(kv, "ylo", axis=0, tiled=True)
-    kv = lax.all_gather(kv, "x", axis=0, tiled=True)
-    kv = lax.all_gather(kv, "z", axis=0, tiled=True)
-    rows = kv.shape[0]
-    blocks = rows // tokens
-    window = min(blocks, -(-(max_len - 1) // tokens) + 1)
-    first_block = jnp.minimum(jnp.min(seg_start) // tokens, blocks - window)
-    span = window * tokens
-    kv_win = lax.dynamic_slice_in_dim(kv, first_block * tokens, span, 0)
-    key_pos = first_block * tokens + jnp.arange(span, dtype=jnp.int32)
-    key_heads = kv_win[:, :kv_cols].reshape(span, kv_local, head_dim)
-    value_heads = kv_win[:, kv_cols:].reshape(span, kv_local, head_dim)
+    nx, nlo = lax.axis_size("x"), lax.axis_size("ylo")
+    piece = jnp.concatenate([key_flat, value_flat], axis=1)[None]
+    block_ids = jnp.zeros((1,), jnp.int32)
+    piece, block_ids = ring_gather(piece, block_ids, "ylo", 1)
+    piece, block_ids = ring_gather(piece, block_ids, "x", nlo)
+    piece, block_ids = ring_gather(piece, block_ids, "z", nx * nlo)
+    span = piece.shape[0] * tokens
+    kv_all = piece.reshape(span, 2 * kv_cols)
+    key_pos = (block_ids[:, None] * tokens + jnp.arange(tokens, dtype=jnp.int32)[None, :]).reshape(span)
+    key_heads = kv_all[:, :kv_cols].reshape(span, kv_local, head_dim)
+    value_heads = kv_all[:, kv_cols:].reshape(span, kv_local, head_dim)
     query_grid = queries.reshape(tokens, kv_local, group, head_dim)
     inv_root = 1.0 / math.sqrt(head_dim)
     score = (

time: 149 us -> 147 us (0.987); the launches traced: 149 us -> 145 us
  starting transfers between devices: 6.77 us -> 56.3 us
  waiting for transfers between devices: 65.7 us -> 33.2 us
  blocking collectives: 41.2 us -> 22.6 us
  between operations: 16.9 us -> 1.15 us
  local copies, waits for them, and re-layouts: 0.33 us -> 12.5 us
  other arithmetic: 9.12 us -> 10.8 us
    all_gather x1 -> x0, waiting for transfers between devices: 54.4 us -> none  [on_device(): kv = lax.all_gather(kv, 'z', axis=0, tiled=True)]
    ppermute x0 -> x13, starting transfers between devices: none -> 51.5 us  [the longest x4 24.9 us: ring_gather(): b = lax.ppermute(b, name, ccw)]
    ppermute x0 -> x13, waiting for transfers between devices: none -> 21.8 us  [the longest x4 9.5 us: ring_gather(): b = lax.ppermute(b, name, ccw)]
    all_gather x2 -> x0, blocking collectives: 18.6 us -> none  [the longest x1 13.6 us: on_device(): kv = lax.all_gather(kv, 'x', axis=0, tiled=True)]
    unnamed x10 -> x24, local copies, waits for them, and re-layouts: 0.03 us -> 10.6 us
    all_to_all x1, starting transfers between devices: 6.74 us -> 4.84 us  [on_device(): part = lax.all_to_all(part, 'yhi', 0, 0, tiled=True)]
    concatenate x0 -> x4, local copies, waits for them, and re-layouts: none -> 1.53 us  [ring_gather(): return (jnp.concatenate(pieces, axis=0), jnp.concatenate(ids, axis=0))]
  transfers between devices with their start and end apart: 2 -> 14, of which waited for: 2 -> 7; matrix products, arithmetic and copies ran while one was open for 3% -> 11% of each run, Pallas kernels for 0% -> 0%
where the time goes in v4:
time: 147 us; the launch traced here: 145 us
  starting transfers between devices  56.3 us (38%)
  waiting for transfers between devices  33.2 us (23%)
  blocking collectives  22.6 us (15%)
  local copies, waits for them, and re-layouts  12.5 us (9%)
  other arithmetic  10.8 us (7%)
  matrix products  8.59 us (6%)
    ppermute x4, starting transfers between devices, ring_gather(): b = lax.ppermute(b, name, ccw)  24.9 us
    all_gather x1, blocking collectives, on_device(): piece = lax.all_gather(hidden_in, TEN, axis=1, tiled=True)  18.4 us
    all_to_all x1, waiting for transfers between devices, on_device(): part = lax.all_to_all(part, 'yhi', 0, 0, tiled=True)  11.4 us
    unnamed x24, local copies, waits for them, and re-layouts  10.6 us
    ppermute x4, starting transfers between devices, ring_gather(): a = lax.ppermute(a, name, cw)  10.1 us
    ppermute x4, waiting for transfers between devices, ring_gather(): b = lax.ppermute(b, name, ccw)  9.5 us
    ppermute x4, waiting for transfers between devices, ring_gather(): a = lax.ppermute(a, name, cw)  7.26 us
    ppermute x2, starting transfers between devices, ring_gather(): lax.ppermute(b[m // 2:], name, ccw)  7.05 us
  transfers between devices with their start and end apart: 14, of which 7 were waited for; matrix products, arithmetic and copies ran while one was open for 11% of the time, Pallas kernels for 0%

profile of v4, /device:TPU:6, one launch (start us, length us, event | category | flops | bytes accessed | tf_op | source)
XLA Modules:
  0.0 145.2 jit_solution(3673872703349153637)
XLA Ops:
  0.7 18.4 %all_gather.3 = bf16[128,2560]{0,1:T(8,128)(2,1)S(1)} all-gather(bf16[128,320]{0,1:T(8,128)(2,1)} %param.9), channel_id=1, replica_groups=mesh['z'=8,'x'=4,'ylo'=2,'yhi'=4,'core'=2] {'yhi','core'}, dimensions={1}, use_global_device_ids=true | all-gather | bytes 737280 | tf_op jit(solution)/shard_map/all_gather | solution.py:76
  19.4 3.1 %fusion.18 = f32[128,512]{1,0:T(8,128)S(1)} fusion(bf16[2560,128]{1,0:T(8,128)(2,1)} %param.13, bf16[2560,128]{1,0:T(8,128)(2,1)} %param.12, bf16[2560,256]{1,0:T(8,128)(2,1)} %param.11, bf16[128,2560]{0,1:T(8,128)(2,1)S(1)} %all_gather.3, f32[2560]{0:T(1024)} %param.10, f32[128]{0:T(128)S(1)} %add_rsqrt_fusion.2), kind=kOutput, calls=%fused_computation.25 | convolution fusion | flops 344457216 | bytes 3549696 | tf_op jit(solution)/shard_map/dot_general | solution.py:79
  24.2 2.4 %collective-permute-start = (bf16[1,128,256]{2,1,0:T(8,128)(2,1)S(1)}, bf16[1,128,256]{2,1,0:T(8,128)(2,1)S(1)}, u32[]{:S(2)}, u32[]{:S(2)}) collective-permute-start(bf16[1,128,256]{2,1,0:T(8,128)(2,1)S(1)} %get-tuple-element.4), channel_id=1, source_target_pairs={{0,8},{8,0},{1,9},{9,1},{2,10},{10,2},{3,11},{11,3},{4,12},{12,4},... | collective-permute-start | bytes 196616 | tf_op jit(solution)/shard_map/ppermute | solution.py:62
  27.4 3.1 %collective-permute-done = bf16[1,128,256]{2,1,0:T(8,128)(2,1)S(1)} collective-permute-done((bf16[1,128,256]{2,1,0:T(8,128)(2,1)S(1)}, bf16[1,128,256]{2,1,0:T(8,128)(2,1)S(1)}, u32[]{:S(2)}, u32[]{:S(2)}) %collective-permute-start) | collective-permute-done | bytes 65568 | tf_op jit(solution)/shard_map/ppermute | solution.py:62
  30.5 2.7 %collective-permute-start.2 = (bf16[2,128,256]{2,1,0:T(8,128)(2,1)S(1)}, bf16[2,128,256]{2,1,0:T(8,128)(2,1)S(1)}, u32[]{:S(2)}, u32[]{:S(2)}) collective-permute-start(bf16[2,128,256]{2,1,0:T(8,128)(2,1)S(1)} %pad_maximum_fusion), channel_id=1, source_target_pairs={{0,48},{16,0},{32,16},{48,32},{1,49},{17,1},{33,17},{49,33},{2,50}... | collective-permute-start | bytes 393224 | tf_op jit(solution)/shard_map/ppermute | solution.py:52
  33.2 4.3 %collective-permute-start.1 = (bf16[2,128,256]{2,1,0:T(8,128)(2,1)S(1)}, bf16[2,128,256]{2,1,0:T(8,128)(2,1)S(1)}, u32[]{:S(2)}, u32[]{:S(2)}) collective-permute-start(bf16[2,128,256]{2,1,0:T(8,128)(2,1)S(1)} %pad_maximum_fusion), channel_id=1, source_target_pairs={{0,16},{16,32},{32,48},{48,0},{1,17},{17,33},{33,49},{49,1},{2,18}... | collective-permute-start | bytes 393224 | tf_op jit(solution)/shard_map/ppermute | solution.py:51
  38.8 1.9 %collective-permute-start.4 = (bf16[1,128,256]{2,1,0:T(8,128)(2,1)S(1)}, bf16[1,128,256]{2,1,0:T(8,128)(2,1)S(1)}, u32[]{:S(2)}, u32[]{:S(2)}) collective-permute-start(bf16[1,128,256]{2,1,0:T(8,128)(2,1)S(1)} %slice.62), channel_id=1, source_target_pairs={{0,48},{16,0},{32,16},{48,32},{1,49},{17,1},{33,17},{49,33},{2,50}... | collective-permute-start | bytes 196616 | tf_op jit(solution)/shard_map/ppermute | solution.py:59
  40.8 5.1 %collective-permute-start.3 = (bf16[1,128,256]{2,1,0:T(8,128)(2,1)S(1)}, bf16[1,128,256]{2,1,0:T(8,128)(2,1)S(1)}, u32[]{:S(2)}, u32[]{:S(2)}) collective-permute-start(bf16[1,128,256]{2,1,0:T(8,128)(2,1)S(1)} %slice.61), channel_id=1, source_target_pairs={{0,16},{16,32},{32,48},{48,0},{1,17},{17,33},{33,49},{49,1},{2,18}... | collective-permute-start | bytes 196616 | tf_op jit(solution)/shard_map/ppermute | solution.py:59
  49.1 11.1 %collective-permute-start.6 = (bf16[8,128,256]{2,1,0:T(8,128)(2,1)}, bf16[8,128,256]{2,1,0:T(8,128)(2,1)S(1)}, u32[]{:S(2)}, u32[]{:S(2)}) collective-permute-start(bf16[8,128,256]{2,1,0:T(8,128)(2,1)} %get-tuple-element.15), channel_id=1, source_target_pairs={{0,448},{64,0},{128,64},{192,128},{256,192},{320,256},{384,320},{4... | collective-permute-start | bytes 1572872 | tf_op jit(solution)/shard_map/ppermute | solution.py:52
  60.2 1.9 %collective-permute-start.5 = (bf16[8,128,256]{2,1,0:T(8,128)(2,1)}, bf16[8,128,256]{2,1,0:T(8,128)(2,1)}, u32[]{:S(2)}, u32[]{:S(2)}) collective-permute-start(bf16[8,128,256]{2,1,0:T(8,128)(2,1)} %get-tuple-element.15), channel_id=1, source_target_pairs={{0,64},{64,128},{128,192},{192,256},{256,320},{320,384},{384,448},... | collective-permute-start | bytes 1572872 | tf_op jit(solution)/shard_map/ppermute | solution.py:51
  62.1 3.7 %compare_and_fusion = pred[128,8192]{0,1:T(8,128)(4,1)S(1)} fusion(s32[128]{0:T(128)S(1)} %iota_add_fusion, s32[128]{0:T(128)S(1)} %select_reduce_fusion, s32[8192]{0:T(1024)S(1)} %add_bitcast_fusion), kind=kLoop, calls=%fused_computation.11 | loop fusion | flops 3145728 | bytes 1082368 | tf_op jit(solution)/shard_map/and | solution.py:112
  66.2 3.5 %collective-permute-done.6 = bf16[8,128,256]{2,1,0:T(8,128)(2,1)S(1)} collective-permute-done((bf16[8,128,256]{2,1,0:T(8,128)(2,1)}, bf16[8,128,256]{2,1,0:T(8,128)(2,1)S(1)}, u32[]{:S(2)}, u32[]{:S(2)}) %collective-permute-start.6) | collective-permute-done | bytes 524320 | tf_op jit(solution)/shard_map/ppermute | solution.py:52
  69.7 5.5 %collective-permute-start.8 = (bf16[8,128,256]{2,1,0:T(8,128)(2,1)S(1)}, bf16[8,128,256]{2,1,0:T(8,128)(2,1)S(1)}, u32[]{:S(2)}, u32[]{:S(2)}) collective-permute-start(bf16[8,128,256]{2,1,0:T(8,128)(2,1)S(1)} %collective-permute-done.6), channel_id=1, source_target_pairs={{0,448},{64,0},{128,64},{192,128},{256,192},{320,256},{384,320},{4... | collective-permute-start | bytes 1572872 | tf_op jit(solution)/shard_map/ppermute | solution.py:52
  75.2 1.9 %collective-permute-start.7 = (bf16[8,128,256]{2,1,0:T(8,128)(2,1)}, bf16[8,128,256]{2,1,0:T(8,128)(2,1)S(1)}, u32[]{:S(2)}, u32[]{:S(2)}) collective-permute-start(bf16[8,128,256]{2,1,0:T(8,128)(2,1)} %collective-permute-done.5), channel_id=1, source_target_pairs={{0,64},{64,128},{128,192},{192,256},{256,320},{320,384},{384,448},... | collective-permute-start | bytes 1572872 | tf_op jit(solution)/shard_map/ppermute | solution.py:51
  77.6 6.0 %collective-permute-done.8 = bf16[8,128,256]{2,1,0:T(8,128)(2,1)S(1)} collective-permute-done((bf16[8,128,256]{2,1,0:T(8,128)(2,1)S(1)}, bf16[8,128,256]{2,1,0:T(8,128)(2,1)S(1)}, u32[]{:S(2)}, u32[]{:S(2)}) %collective-permute-start.8) | collective-permute-done | bytes 524320 | tf_op jit(solution)/shard_map/ppermute | solution.py:52
  83.6 5.6 %collective-permute-start.10 = (bf16[8,128,256]{2,1,0:T(8,128)(2,1)S(1)}, bf16[8,128,256]{2,1,0:T(8,128)(2,1)S(1)}, u32[]{:S(2)}, u32[]{:S(2)}) collective-permute-start(bf16[8,128,256]{2,1,0:T(8,128)(2,1)S(1)} %collective-permute-done.8), channel_id=1, source_target_pairs={{0,448},{64,0},{128,64},{192,128},{256,192},{320,256},{384,320},{4... | collective-permute-start | bytes 1572872 | tf_op jit(solution)/shard_map/ppermute | solution.py:52
  89.2 1.9 %collective-permute-start.9 = (bf16[8,128,256]{2,1,0:T(8,128)(2,1)S(1)}, bf16[8,128,256]{2,1,0:T(8,128)(2,1)S(1)}, u32[]{:S(2)}, u32[]{:S(2)}) collective-permute-start(bf16[8,128,256]{2,1,0:T(8,128)(2,1)S(1)} %collective-permute-done.7), channel_id=1, source_target_pairs={{0,64},{64,128},{128,192},{192,256},{256,320},{320,384},{384,448},... | collective-permute-start | bytes 1572872 | tf_op jit(solution)/shard_map/ppermute | solution.py:51
  91.3 1.9 %constant_dynamic-update-slice_fusion.13 = bf16[64,128,256]{2,1,0:T(8,128)(2,1)} fusion(bf16[64,128,256]{2,1,0:T(8,128)(2,1)} %get-tuple-element.16, bf16[8,128,256]{2,1,0:T(8,128)(2,1)} %collective-permute-done.5), kind=kLoop, calls=%fused_computation.68 | loop fusion | bytes 1048576
  93.1 0.8 constant_dynamic-update-slice_fusion.12
  94.0 0.8 constant_dynamic-update-slice_fusion.11
  94.8 7.3 %collective-permute-done.9 = bf16[8,128,256]{2,1,0:T(8,128)(2,1)S(1)} collective-permute-done((bf16[8,128,256]{2,1,0:T(8,128)(2,1)S(1)}, bf16[8,128,256]{2,1,0:T(8,128)(2,1)S(1)}, u32[]{:S(2)}, u32[]{:S(2)}) %collective-permute-start.9) | collective-permute-done | bytes 524320 | tf_op jit(solution)/shard_map/ppermute | solution.py:51
  102.1 1.9 %collective-permute-start.11 = (bf16[4,128,256]{2,1,0:T(8,128)(2,1)S(1)}, bf16[4,128,256]{2,1,0:T(8,128)(2,1)S(1)}, u32[]{:S(2)}, u32[]{:S(2)}) collective-permute-start(bf16[4,128,256]{2,1,0:T(8,128)(2,1)S(1)} %slice.63), channel_id=1, source_target_pairs={{0,64},{64,128},{128,192},{192,256},{256,320},{320,384},{384,448},... | collective-permute-start | bytes 786440 | tf_op jit(solution)/shard_map/ppermute | solution.py:59
  104.9 5.1 %collective-permute-start.12 = (bf16[4,128,256]{2,1,0:T(8,128)(2,1)S(1)}, bf16[4,128,256]{2,1,0:T(8,128)(2,1)S(1)}, u32[]{:S(2)}, u32[]{:S(2)}) collective-permute-start(bf16[4,128,256]{2,1,0:T(8,128)(2,1)S(1)} %slice.64), channel_id=1, source_target_pairs={{0,448},{64,0},{128,64},{192,128},{256,192},{320,256},{384,320},{4... | collective-permute-start | bytes 786440 | tf_op jit(solution)/shard_map/ppermute | solution.py:59
  110.0 0.8 constant_dynamic-update-slice_fusion.9
  112.4 1.5 %collective-permute-done.12 = bf16[4,128,256]{2,1,0:T(8,128)(2,1)S(1)} collective-permute-done((bf16[4,128,256]{2,1,0:T(8,128)(2,1)S(1)}, bf16[4,128,256]{2,1,0:T(8,128)(2,1)S(1)}, u32[]{:S(2)}, u32[]{:S(2)}) %collective-permute-start.12) | collective-permute-done | bytes 262176 | tf_op jit(solution)/shard_map/ppermute | solution.py:59
  114.6 3.4 %fusion.47 = (f32[2,128]{1,0:T(2,128)S(1)}, f32[1,2,128,8192]{2,3,1,0:T(8,128)S(1)}) fusion(bf16[128,2,64]{2,0,1:T(8,128)(2,1)S(1)} %get-tuple-element.6, bf16[128,2,64]{2,0,1:T(8,128)(2,1)S(1)} %get-tuple-element.5, bf16[8192,256]{1,0:T(8,128)(2,1)} %bitcast.61, pred[128,8192]{0,1:T(8,128)(4,1)S(1)} %compare_and_fusion), kind=kOutput, calls=%fused_computation.107 | convolution fusion | flops 543293184 | bytes 11600896 | tf_op jit(solution)/shard_map/qhgd,khd->hgqk/dot_general | solution.py:109
  118.0 1.7 %fusion.2 = f32[2,128]{1,0:T(2,128)S(1)} fusion(f32[1,2,128,8192]{2,3,1,0:T(8,128)S(1)} %get-tuple-element.31, f32[2,128]{1,0:T(2,128)S(1)} %get-tuple-element.30, pred[128,8192]{0,1:T(8,128)(4,1)S(1)} %compare_and_fusion), kind=kLoop, calls=%fused_computation.4 | loop fusion | flops 6291200 | bytes 9439232 | tf_op jit(solution)/shard_map/reduce_sum | solution.py:116
  120.2 1.8 %fusion.24 = bf16[2,128,128]{1,2,0:T(8,128)(2,1)S(1)} fusion(bf16[8192,256]{1,0:T(8,128)(2,1)S(1)} %bitcast.62, f32[1,2,128,8192]{2,3,1,0:T(8,128)S(1)} %get-tuple-element.31, f32[2,128]{1,0:T(2,128)S(1)} %get-tuple-element.30, pred[128,8192]{0,1:T(8,128)(4,1)S(1)} %compare_and_fusion, f32[2,128]{1,0:T(2,128)S(1)} %fusion.2), kind=kOutput, calls=%fused_computation.27 | convolution fusion | flops 543227904 | bytes 11601920 | tf_op jit(solution)/shard_map/hgqk,khd->hgqd/dot_general | solution.py:117
  122.4 4.3 %all_to_all.10 = bf16[2,4,16,2560]{3,2,1,0:T(8,128)(2,1)S(1)} all-to-all(bf16[2,4,16,2560]{3,2,1,0:T(8,128)(2,1)S(1)} %bitcast.59), channel_id=1, replica_groups=mesh['z'=8,'x'=4,'ylo'=2,'yhi'=4,'core'=2] {'core'}, dimensions={0} | all-to-all | bytes 1310720 | tf_op jit(solution)/shard_map/all_to_all | solution.py:130
  126.6 0.9 reduce_sum.84
  127.5 4.8 %all-to-all-start.1 = ((bf16[4,16,2560]{2,1,0:T(8,128)(2,1)}), bf16[4,16,2560]{2,1,0:T(8,128)(2,1)S(1)}, u32[]{:S(2)}, u32[]{:S(2)}) async-start(bf16[4,16,2560]{2,1,0:T(8,128)(2,1)} %reduce_sum.84), calls=%async_computation.1 | async-start | bytes 655360 | tf_op jit(solution)/shard_map/all_to_all | solution.py:132
  133.1 11.4 %all-to-all-done.1 = bf16[4,16,2560]{2,1,0:T(8,128)(2,1)S(1)} async-done(((bf16[4,16,2560]{2,1,0:T(8,128)(2,1)}), bf16[4,16,2560]{2,1,0:T(8,128)(2,1)S(1)}, u32[]{:S(2)}, u32[]{:S(2)}) %all-to-all-start.1) | async-done | bytes 327712 | tf_op jit(solution)/shard_map/all_to_all | solution.py:132
  (73 shorter events, 13.4 us)
Async XLA Ops:
  0.6 121.3 %copy-start = (bf16[256,2560]{1,0:T(8,128)(2,1)S(1)}, bf16[256,2560]{1,0:T(8,128)(2,1)}, u32[]{:S(2)}) copy-start(bf16[256,2560]{1,0:T(8,128)(2,1)} %param.14) | copy-start | bytes 3932164
  19.0 3.6 %copy-start.5 = (s32[16]{0:T(128)S(1)}, s32[16]{0:T(128)}, u32[]{:S(2)}) copy-start(s32[16]{0:T(128)} %param.17) | copy-start | bytes 196
  19.0 4.1 %copy-start.3 = (f32[128]{0:T(128)S(1)}, f32[128]{0:T(128)}, u32[]{:S(2)}) copy-start(f32[128]{0:T(128)} %param.16) | copy-start | bytes 1540
  22.5 55.0 %copy-start.4 = (f32[128]{0:T(128)S(1)}, f32[128]{0:T(128)}, u32[]{:S(2)}) copy-start(f32[128]{0:T(128)} %param.15) | copy-start | bytes 1540
  22.6 72.2 %copy-start.1 = (bf16[128,128]{1,0:T(8,128)(2,1)}, bf16[128,128]{1,0:T(8,128)(2,1)S(1)}, u32[]{:S(2)}) copy-start(bf16[128,128]{1,0:T(8,128)(2,1)S(1)} %slice.98) | copy-start | bytes 98308
  24.2 6.2 %collective-permute-start = (bf16[1,128,256]{2,1,0:T(8,128)(2,1)S(1)}, bf16[1,128,256]{2,1,0:T(8,128)(2,1)S(1)}, u32[]{:S(2)}, u32[]{:S(2)}) collective-permute-start(bf16[1,128,256]{2,1,0:T(8,128)(2,1)S(1)} %get-tuple-element.4), channel_id=1, source_target_pairs={{0,8},{8,0},{1,9},{9,1},{2,10},{10,2},{3,11},{11,3},{4,12},{12,4},... | collective-permute-start | bytes 196616 | tf_op jit(solution)/shard_map/ppermute | solution.py:62
  30.5 8.3 %collective-permute-start.2 = (bf16[2,128,256]{2,1,0:T(8,128)(2,1)S(1)}, bf16[2,128,256]{2,1,0:T(8,128)(2,1)S(1)}, u32[]{:S(2)}, u32[]{:S(2)}) collective-permute-start(bf16[2,128,256]{2,1,0:T(8,128)(2,1)S(1)} %pad_maximum_fusion), channel_id=1, source_target_pairs={{0,48},{16,0},{32,16},{48,32},{1,49},{17,1},{33,17},{49,33},{2,50}... | collective-permute-start | bytes 393224 | tf_op jit(solution)/shard_map/ppermute | solution.py:52
  33.2 7.5 %collective-permute-start.1 = (bf16[2,128,256]{2,1,0:T(8,128)(2,1)S(1)}, bf16[2,128,256]{2,1,0:T(8,128)(2,1)S(1)}, u32[]{:S(2)}, u32[]{:S(2)}) collective-permute-start(bf16[2,128,256]{2,1,0:T(8,128)(2,1)S(1)} %pad_maximum_fusion), channel_id=1, source_target_pairs={{0,16},{16,32},{32,48},{48,0},{1,17},{17,33},{33,49},{49,1},{2,18}... | collective-permute-start | bytes 393224 | tf_op jit(solution)/shard_map/ppermute | solution.py:51
  38.8 9.6 %collective-permute-start.4 = (bf16[1,128,256]{2,1,0:T(8,128)(2,1)S(1)}, bf16[1,128,256]{2,1,0:T(8,128)(2,1)S(1)}, u32[]{:S(2)}, u32[]{:S(2)}) collective-permute-start(bf16[1,128,256]{2,1,0:T(8,128)(2,1)S(1)} %slice.62), channel_id=1, source_target_pairs={{0,48},{16,0},{32,16},{48,32},{1,49},{17,1},{33,17},{49,33},{2,50}... | collective-permute-start | bytes 196616 | tf_op jit(solution)/shard_map/ppermute | solution.py:59
  40.8 7.0 %collective-permute-start.3 = (bf16[1,128,256]{2,1,0:T(8,128)(2,1)S(1)}, bf16[1,128,256]{2,1,0:T(8,128)(2,1)S(1)}, u32[]{:S(2)}, u32[]{:S(2)}) collective-permute-start(bf16[1,128,256]{2,1,0:T(8,128)(2,1)S(1)} %slice.61), channel_id=1, source_target_pairs={{0,16},{16,32},{32,48},{48,0},{1,17},{17,33},{33,49},{49,1},{2,18}... | collective-permute-start | bytes 196616 | tf_op jit(solution)/shard_map/ppermute | solution.py:59
  49.1 20.6 %collective-permute-start.6 = (bf16[8,128,256]{2,1,0:T(8,128)(2,1)}, bf16[8,128,256]{2,1,0:T(8,128)(2,1)S(1)}, u32[]{:S(2)}, u32[]{:S(2)}) collective-permute-start(bf16[8,128,256]{2,1,0:T(8,128)(2,1)} %get-tuple-element.15), channel_id=1, source_target_pairs={{0,448},{64,0},{128,64},{192,128},{256,192},{320,256},{384,320},{4... | collective-permute-start | bytes 1572872 | tf_op jit(solution)/shard_map/ppermute | solution.py:52
  60.2 15.0 %collective-permute-start.5 = (bf16[8,128,256]{2,1,0:T(8,128)(2,1)}, bf16[8,128,256]{2,1,0:T(8,128)(2,1)}, u32[]{:S(2)}, u32[]{:S(2)}) collective-permute-start(bf16[8,128,256]{2,1,0:T(8,128)(2,1)} %get-tuple-element.15), channel_id=1, source_target_pairs={{0,64},{64,128},{128,192},{192,256},{256,320},{320,384},{384,448},... | collective-permute-start | bytes 1572872 | tf_op jit(solution)/shard_map/ppermute | solution.py:51
  69.7 13.9 %collective-permute-start.8 = (bf16[8,128,256]{2,1,0:T(8,128)(2,1)S(1)}, bf16[8,128,256]{2,1,0:T(8,128)(2,1)S(1)}, u32[]{:S(2)}, u32[]{:S(2)}) collective-permute-start(bf16[8,128,256]{2,1,0:T(8,128)(2,1)S(1)} %collective-permute-done.6), channel_id=1, source_target_pairs={{0,448},{64,0},{128,64},{192,128},{256,192},{320,256},{384,320},{4... | collective-permute-start | bytes 1572872 | tf_op jit(solution)/shard_map/ppermute | solution.py:52
  75.2 14.0 %collective-permute-start.7 = (bf16[8,128,256]{2,1,0:T(8,128)(2,1)}, bf16[8,128,256]{2,1,0:T(8,128)(2,1)S(1)}, u32[]{:S(2)}, u32[]{:S(2)}) collective-permute-start(bf16[8,128,256]{2,1,0:T(8,128)(2,1)} %collective-permute-done.5), channel_id=1, source_target_pairs={{0,64},{64,128},{128,192},{192,256},{256,320},{320,384},{384,448},... | collective-permute-start | bytes 1572872 | tf_op jit(solution)/shard_map/ppermute | solution.py:51
  83.6 21.2 %collective-permute-start.10 = (bf16[8,128,256]{2,1,0:T(8,128)(2,1)S(1)}, bf16[8,128,256]{2,1,0:T(8,128)(2,1)S(1)}, u32[]{:S(2)}, u32[]{:S(2)}) collective-permute-start(bf16[8,128,256]{2,1,0:T(8,128)(2,1)S(1)} %collective-permute-done.8), channel_id=1, source_target_pairs={{0,448},{64,0},{128,64},{192,128},{256,192},{320,256},{384,320},{4... | collective-permute-start | bytes 1572872 | tf_op jit(solution)/shard_map/ppermute | solution.py:52
  89.2 12.8 %collective-permute-start.9 = (bf16[8,128,256]{2,1,0:T(8,128)(2,1)S(1)}, bf16[8,128,256]{2,1,0:T(8,128)(2,1)S(1)}, u32[]{:S(2)}, u32[]{:S(2)}) collective-permute-start(bf16[8,128,256]{2,1,0:T(8,128)(2,1)S(1)} %collective-permute-done.7), channel_id=1, source_target_pairs={{0,64},{64,128},{128,192},{192,256},{256,320},{320,384},{384,448},... | collective-permute-start | bytes 1572872 | tf_op jit(solution)/shard_map/ppermute | solution.py:51
  102.1 9.6 %collective-permute-start.11 = (bf16[4,128,256]{2,1,0:T(8,128)(2,1)S(1)}, bf16[4,128,256]{2,1,0:T(8,128)(2,1)S(1)}, u32[]{:S(2)}, u32[]{:S(2)}) collective-permute-start(bf16[4,128,256]{2,1,0:T(8,128)(2,1)S(1)} %slice.63), channel_id=1, source_target_pairs={{0,64},{64,128},{128,192},{192,256},{256,320},{320,384},{384,448},... | collective-permute-start | bytes 786440 | tf_op jit(solution)/shard_map/ppermute | solution.py:59
  104.9 9.0 %collective-permute-start.12 = (bf16[4,128,256]{2,1,0:T(8,128)(2,1)S(1)}, bf16[4,128,256]{2,1,0:T(8,128)(2,1)S(1)}, u32[]{:S(2)}, u32[]{:S(2)}) collective-permute-start(bf16[4,128,256]{2,1,0:T(8,128)(2,1)S(1)} %slice.64), channel_id=1, source_target_pairs={{0,448},{64,0},{128,64},{192,128},{256,192},{320,256},{384,320},{4... | collective-permute-start | bytes 786440 | tf_op jit(solution)/shard_map/ppermute | solution.py:59
  118.0 2.2 %copy-start.2 = (bf16[64,128,256]{2,1,0:T(8,128)(2,1)S(1)}, bf16[64,128,256]{2,1,0:T(8,128)(2,1)}, u32[]{:S(2)}) copy-start(bf16[64,128,256]{2,1,0:T(8,128)(2,1)} %constant_dynamic-update-slice_fusion.6) | copy-start | bytes 12582916
  127.5 16.9 %all-to-all-start.1 = ((bf16[4,16,2560]{2,1,0:T(8,128)(2,1)}), bf16[4,16,2560]{2,1,0:T(8,128)(2,1)S(1)}, u32[]{:S(2)}, u32[]{:S(2)}) async-start(bf16[4,16,2560]{2,1,0:T(8,128)(2,1)} %reduce_sum.84), calls=%async_computation.1 | async-start | bytes 655360 | tf_op jit(solution)/shard_map/all_to_all | solution.py:132

commit v5 on v4

--- a/solution.py
+++ b/solution.py
@@ -95,8 +95,9 @@
     nx, nlo = lax.axis_size("x"), lax.axis_size("ylo")
     piece = jnp.concatenate([key_flat, value_flat], axis=1)[None]
     block_ids = jnp.zeros((1,), jnp.int32)
-    piece, block_ids = ring_gather(piece, block_ids, "ylo", 1)
-    piece, block_ids = ring_gather(piece, block_ids, "x", nlo)
+    plane = nx * nlo
+    piece = lax.all_to_all(jnp.broadcast_to(piece, (plane,) + piece.shape[1:]), ("x", "ylo"), 0, 0, tiled=True)
+    block_ids = jnp.arange(plane, dtype=jnp.int32)
     piece, block_ids = ring_gather(piece, block_ids, "z", nx * nlo)
     span = piece.shape[0] * tokens
     kv_all = piece.reshape(span, 2 * kv_cols)

time: 147 us -> 135 us (0.918)
  starting transfers between devices: 56.3 us -> 44.9 us
  local copies, waits for them, and re-layouts: 12.5 us -> 5.14 us
  waiting for transfers between devices: 33.2 us -> 39.6 us
  other arithmetic: 10.8 us -> 13 us
  matrix products: 8.59 us -> 7.1 us
    unnamed x24 -> x26, local copies, waits for them, and re-layouts: 10.6 us -> 2.41 us
    all_to_all x0 -> x1, waiting for transfers between devices: none -> 8.13 us  [on_device(): lax.all_to_all(jnp.broadcast_to(piece, (plane,) + piece.shape[1:]), ('x',...]
    all_to_all x0 -> x1, starting transfers between devices: none -> 6.41 us  [on_device(): lax.all_to_all(jnp.broadcast_to(piece, (plane,) + piece.shape[1:]), ('x',...]
    ppermute x2 -> x1, starting transfers between devices: 7.05 us -> 1.92 us  [ring_gather(): lax.ppermute(a[:m // 2], name, cw)]
    ppermute x4 -> x3, waiting for transfers between devices: 9.5 us -> 4.47 us  [ring_gather(): b = lax.ppermute(b, name, ccw)]
    ppermute x4 -> x3, starting transfers between devices: 24.9 us -> 20.1 us  [ring_gather(): b = lax.ppermute(b, name, ccw)]
    ppermute x4 -> x3, waiting for transfers between devices: 7.26 us -> 11.3 us  [ring_gather(): a = lax.ppermute(a, name, cw)]
    ppermute x4 -> x3, starting transfers between devices: 10.1 us -> 6.18 us  [ring_gather(): a = lax.ppermute(a, name, cw)]
  transfers between devices with their start and end apart: 14 -> 10, of which waited for: 7 -> 9; matrix products, arithmetic and copies ran while one was open for 11% -> 9% of each run, Pallas kernels for 0% -> 0%
where the time goes in v5:
time: 135 us; the launch traced here: 133 us
  starting transfers between devices  44.9 us (33%)
  waiting for transfers between devices  39.6 us (29%)
  blocking collectives  22.6 us (17%)
  other arithmetic  13 us (10%)
  matrix products  7.1 us (5%)
  local copies, waits for them, and re-layouts  5.14 us (4%)
    ppermute x3, starting transfers between devices, ring_gather(): b = lax.ppermute(b, name, ccw)  20.1 us
    all_gather x1, blocking collectives, on_device(): piece = lax.all_gather(hidden_in, TEN, axis=1, tiled=True)  18.4 us
    all_to_all x1, waiting for transfers between devices, on_device(): part = lax.all_to_all(part, 'yhi', 0, 0, tiled=True)  12 us
    ppermute x3, waiting for transfers between devices, ring_gather(): a = lax.ppermute(a, name, cw)  11.3 us
    all_to_all x1, waiting for transfers between devices, on_device(): lax.all_to_all(jnp.broadcast_to(piece, (plane,) + piece.shape[1:]), ('x',...  8.13 us
    all_to_all x1, starting transfers between devices, on_device(): lax.all_to_all(jnp.broadcast_to(piece, (plane,) + piece.shape[1:]), ('x',...  6.41 us
    ppermute x3, starting transfers between devices, ring_gather(): a = lax.ppermute(a, name, cw)  6.18 us
    ppermute x1, starting transfers between devices, ring_gather(): lax.ppermute(b[m // 2:], name, ccw)  5.6 us
  transfers between devices with their start and end apart: 10, of which 9 were waited for; matrix products, arithmetic and copies ran while one was open for 9% of the time, Pallas kernels for 0%

profile of v5, /device:TPU:6, one launch (start us, length us, event | category | flops | bytes accessed | tf_op | source)
XLA Modules:
  0.0 133.4 jit_solution(1898882483405965335)
XLA Ops:
  0.7 18.4 %all_gather.3 = bf16[128,2560]{0,1:T(8,128)(2,1)S(1)} all-gather(bf16[128,320]{0,1:T(8,128)(2,1)} %param.9), channel_id=1, replica_groups=mesh['z'=8,'x'=4,'ylo'=2,'yhi'=4,'core'=2] {'yhi','core'}, dimensions={1}, use_global_device_ids=true | all-gather | bytes 737280 | tf_op jit(solution)/shard_map/all_gather | solution.py:76
  19.4 3.1 %fusion.18 = f32[128,512]{1,0:T(8,128)S(1)} fusion(bf16[2560,128]{1,0:T(8,128)(2,1)} %param.13, bf16[2560,128]{1,0:T(8,128)(2,1)} %param.12, bf16[2560,256]{1,0:T(8,128)(2,1)} %param.11, bf16[128,2560]{0,1:T(8,128)(2,1)S(1)} %all_gather.3, f32[2560]{0:T(1024)} %param.10, f32[128]{0:T(128)S(1)} %add_rsqrt_fusion.2), kind=kOutput, calls=%fused_computation.25 | convolution fusion | flops 344457216 | bytes 3549696 | tf_op jit(solution)/shard_map/dot_general | solution.py:79
  24.5 6.4 %all-to-all-start = ((bf16[8,128,256]{2,1,0:T(8,128)(2,1)}), bf16[8,128,256]{2,1,0:T(8,128)(2,1)S(1)}, u32[]{:S(2)}, u32[]{:S(2)}) async-start(bf16[8,128,256]{2,1,0:T(8,128)(2,1)} %broadcast_in_dim.31), calls=%async_computation | async-start | bytes 1048576 | tf_op jit(solution)/shard_map/all_to_all | solution.py:99
  31.2 8.1 %all-to-all-done = bf16[8,128,256]{2,1,0:T(8,128)(2,1)S(1)} async-done(((bf16[8,128,256]{2,1,0:T(8,128)(2,1)}), bf16[8,128,256]{2,1,0:T(8,128)(2,1)S(1)}, u32[]{:S(2)}, u32[]{:S(2)}) %all-to-all-start) | async-done | bytes 524320 | tf_op jit(solution)/shard_map/all_to_all | solution.py:99
  39.4 2.4 %collective-permute-start = (bf16[8,128,256]{2,1,0:T(8,128)(2,1)S(1)}, bf16[8,128,256]{2,1,0:T(8,128)(2,1)}, u32[]{:S(2)}, u32[]{:S(2)}) collective-permute-start(bf16[8,128,256]{2,1,0:T(8,128)(2,1)S(1)} %all-to-all-done), channel_id=1, source_target_pairs={{0,64},{64,128},{128,192},{192,256},{256,320},{320,384},{384,448},... | collective-permute-start | bytes 1572872 | tf_op jit(solution)/shard_map/ppermute | solution.py:51
  41.8 3.7 %compare_and_fusion = pred[128,8192]{0,1:T(8,128)(4,1)S(1)} fusion(s32[128]{0:T(128)S(1)} %iota_add_fusion, s32[128]{0:T(128)S(1)} %select_reduce_fusion, s32[8192]{0:T(1024)S(1)} %add_bitcast_fusion), kind=kLoop, calls=%fused_computation.11 | loop fusion | flops 3145728 | bytes 1082368 | tf_op jit(solution)/shard_map/and | solution.py:113
  45.5 8.9 %collective-permute-start.1 = (bf16[8,128,256]{2,1,0:T(8,128)(2,1)S(1)}, bf16[8,128,256]{2,1,0:T(8,128)(2,1)}, u32[]{:S(2)}, u32[]{:S(2)}) collective-permute-start(bf16[8,128,256]{2,1,0:T(8,128)(2,1)S(1)} %all-to-all-done), channel_id=1, source_target_pairs={{0,448},{64,0},{128,64},{192,128},{256,192},{320,256},{384,320},{4... | collective-permute-start | bytes 1572872 | tf_op jit(solution)/shard_map/ppermute | solution.py:52
  55.2 1.0 multiply_cosine_fusion
  56.1 4.0 %collective-permute-done = bf16[8,128,256]{2,1,0:T(8,128)(2,1)} collective-permute-done((bf16[8,128,256]{2,1,0:T(8,128)(2,1)S(1)}, bf16[8,128,256]{2,1,0:T(8,128)(2,1)}, u32[]{:S(2)}, u32[]{:S(2)}) %collective-permute-start) | collective-permute-done | bytes 524320 | tf_op jit(solution)/shard_map/ppermute | solution.py:51
  60.1 1.9 %collective-permute-start.2 = (bf16[8,128,256]{2,1,0:T(8,128)(2,1)}, bf16[8,128,256]{2,1,0:T(8,128)(2,1)S(1)}, u32[]{:S(2)}, u32[]{:S(2)}) collective-permute-start(bf16[8,128,256]{2,1,0:T(8,128)(2,1)} %collective-permute-done), channel_id=1, source_target_pairs={{0,64},{64,128},{128,192},{192,256},{256,320},{320,384},{384,448},... | collective-permute-start | bytes 1572872 | tf_op jit(solution)/shard_map/ppermute | solution.py:51
  62.1 1.7 %multiply_reduce_fusion = f32[128,2]{1,0:T(8,128)} fusion(f32[128,2,128]{2,1,0:T(2,128)} %reshape.365), kind=kLoop, calls=%fused_computation.34 | loop fusion | flops 65280 | bytes 132096 | tf_op jit(solution)/shard_map/reduce_sum | solution.py:30
  63.8 0.9 copy.33
  65.0 5.7 %collective-permute-start.3 = (bf16[8,128,256]{2,1,0:T(8,128)(2,1)}, bf16[8,128,256]{2,1,0:T(8,128)(2,1)S(1)}, u32[]{:S(2)}, u32[]{:S(2)}) collective-permute-start(bf16[8,128,256]{2,1,0:T(8,128)(2,1)} %collective-permute-done.1), channel_id=1, source_target_pairs={{0,448},{64,0},{128,64},{192,128},{256,192},{320,256},{384,320},{4... | collective-permute-start | bytes 1572872 | tf_op jit(solution)/shard_map/ppermute | solution.py:52
  70.8 5.1 %collective-permute-done.2 = bf16[8,128,256]{2,1,0:T(8,128)(2,1)S(1)} collective-permute-done((bf16[8,128,256]{2,1,0:T(8,128)(2,1)}, bf16[8,128,256]{2,1,0:T(8,128)(2,1)S(1)}, u32[]{:S(2)}, u32[]{:S(2)}) %collective-permute-start.2) | collective-permute-done | bytes 524320 | tf_op jit(solution)/shard_map/ppermute | solution.py:51
  75.9 1.9 %collective-permute-start.4 = (bf16[8,128,256]{2,1,0:T(8,128)(2,1)S(1)}, bf16[8,128,256]{2,1,0:T(8,128)(2,1)S(1)}, u32[]{:S(2)}, u32[]{:S(2)}) collective-permute-start(bf16[8,128,256]{2,1,0:T(8,128)(2,1)S(1)} %collective-permute-done.2), channel_id=1, source_target_pairs={{0,64},{64,128},{128,192},{192,256},{256,320},{320,384},{384,448},... | collective-permute-start | bytes 1572872 | tf_op jit(solution)/shard_map/ppermute | solution.py:51
  77.8 1.0 subtract_convert_fusion
  78.8 1.8 %collective-permute-done.3 = bf16[8,128,256]{2,1,0:T(8,128)(2,1)S(1)} collective-permute-done((bf16[8,128,256]{2,1,0:T(8,128)(2,1)}, bf16[8,128,256]{2,1,0:T(8,128)(2,1)S(1)}, u32[]{:S(2)}, u32[]{:S(2)}) %collective-permute-start.3) | collective-permute-done | bytes 524320 | tf_op jit(solution)/shard_map/ppermute | solution.py:52
  80.7 5.5 %collective-permute-start.5 = (bf16[8,128,256]{2,1,0:T(8,128)(2,1)S(1)}, bf16[8,128,256]{2,1,0:T(8,128)(2,1)S(1)}, u32[]{:S(2)}, u32[]{:S(2)}) collective-permute-start(bf16[8,128,256]{2,1,0:T(8,128)(2,1)S(1)} %collective-permute-done.3), channel_id=1, source_target_pairs={{0,448},{64,0},{128,64},{192,128},{256,192},{320,256},{384,320},{4... | collective-permute-start | bytes 1572872 | tf_op jit(solution)/shard_map/ppermute | solution.py:52
  86.2 1.1 constant_dynamic-update-slice_fusion.7
  87.3 1.1 constant_dynamic-update-slice_fusion.6
  88.4 2.2 %collective-permute-done.4 = bf16[8,128,256]{2,1,0:T(8,128)(2,1)S(1)} collective-permute-done((bf16[8,128,256]{2,1,0:T(8,128)(2,1)S(1)}, bf16[8,128,256]{2,1,0:T(8,128)(2,1)S(1)}, u32[]{:S(2)}, u32[]{:S(2)}) %collective-permute-start.4) | collective-permute-done | bytes 524320 | tf_op jit(solution)/shard_map/ppermute | solution.py:51
  90.6 1.9 %collective-permute-start.6 = (bf16[4,128,256]{2,1,0:T(8,128)(2,1)S(1)}, bf16[4,128,256]{2,1,0:T(8,128)(2,1)S(1)}, u32[]{:S(2)}, u32[]{:S(2)}) collective-permute-start(bf16[4,128,256]{2,1,0:T(8,128)(2,1)S(1)} %slice.57), channel_id=1, source_target_pairs={{0,64},{64,128},{128,192},{192,256},{256,320},{320,384},{384,448},... | collective-permute-start | bytes 786440 | tf_op jit(solution)/shard_map/ppermute | solution.py:59
  92.6 2.4 %collective-permute-done.5 = bf16[8,128,256]{2,1,0:T(8,128)(2,1)S(1)} collective-permute-done((bf16[8,128,256]{2,1,0:T(8,128)(2,1)S(1)}, bf16[8,128,256]{2,1,0:T(8,128)(2,1)S(1)}, u32[]{:S(2)}, u32[]{:S(2)}) %collective-permute-start.5) | collective-permute-done | bytes 524320 | tf_op jit(solution)/shard_map/ppermute | solution.py:52
  95.0 5.6 %collective-permute-start.7 = (bf16[4,128,256]{2,1,0:T(8,128)(2,1)S(1)}, bf16[4,128,256]{2,1,0:T(8,128)(2,1)S(1)}, u32[]{:S(2)}, u32[]{:S(2)}) collective-permute-start(bf16[4,128,256]{2,1,0:T(8,128)(2,1)S(1)} %slice.58), channel_id=1, source_target_pairs={{0,448},{64,0},{128,64},{192,128},{256,192},{320,256},{384,320},{4... | collective-permute-start | bytes 786440 | tf_op jit(solution)/shard_map/ppermute | solution.py:59
  100.7 3.7 %collective-permute-done.7 = bf16[4,128,256]{2,1,0:T(8,128)(2,1)S(1)} collective-permute-done((bf16[4,128,256]{2,1,0:T(8,128)(2,1)S(1)}, bf16[4,128,256]{2,1,0:T(8,128)(2,1)S(1)}, u32[]{:S(2)}, u32[]{:S(2)}) %collective-permute-start.7) | collective-permute-done | bytes 262176 | tf_op jit(solution)/shard_map/ppermute | solution.py:59
  104.5 1.9 %fusion.47 = (f32[2,128]{1,0:T(2,128)S(1)}, f32[1,2,128,8192]{2,3,1,0:T(8,128)S(1)}) fusion(bf16[128,2,64]{2,0,1:T(8,128)(2,1)S(1)} %get-tuple-element.4, bf16[128,2,64]{2,0,1:T(8,128)(2,1)S(1)} %get-tuple-element.3, bf16[8192,256]{1,0:T(8,128)(2,1)S(1)} %bitcast.55, pred[128,8192]{0,1:T(8,128)(4,1)S(1)} %compare_and_fusion), kind=kOutput, calls=%fused_computation.91 | convolution fusion | flops 543293184 | bytes 11666432 | tf_op jit(solution)/shard_map/qhgd,khd->hgqk/dot_general | solution.py:110
  106.4 1.7 %fusion.2 = f32[2,128]{1,0:T(2,128)S(1)} fusion(f32[1,2,128,8192]{2,3,1,0:T(8,128)S(1)} %get-tuple-element.12, f32[2,128]{1,0:T(2,128)S(1)} %get-tuple-element.11, pred[128,8192]{0,1:T(8,128)(4,1)S(1)} %compare_and_fusion), kind=kLoop, calls=%fused_computation.4 | loop fusion | flops 6291200 | bytes 9439232 | tf_op jit(solution)/shard_map/reduce_sum | solution.py:117
  108.1 1.8 %fusion.24 = bf16[2,128,128]{1,2,0:T(8,128)(2,1)S(1)} fusion(bf16[8192,256]{1,0:T(8,128)(2,1)S(1)} %bitcast.56, f32[1,2,128,8192]{2,3,1,0:T(8,128)S(1)} %get-tuple-element.12, f32[2,128]{1,0:T(2,128)S(1)} %get-tuple-element.11, pred[128,8192]{0,1:T(8,128)(4,1)S(1)} %compare_and_fusion, f32[2,128]{1,0:T(2,128)S(1)} %fusion.2), kind=kOutput, calls=%fused_computation.27 | convolution fusion | flops 543227904 | bytes 11601920 | tf_op jit(solution)/shard_map/hgqk,khd->hgqd/dot_general | solution.py:118
  110.3 4.3 %all_to_all.15 = bf16[2,4,16,2560]{3,2,1,0:T(8,128)(2,1)S(1)} all-to-all(bf16[2,4,16,2560]{3,2,1,0:T(8,128)(2,1)S(1)} %bitcast.53), channel_id=1, replica_groups=mesh['z'=8,'x'=4,'ylo'=2,'yhi'=4,'core'=2] {'core'}, dimensions={0} | all-to-all | bytes 1310720 | tf_op jit(solution)/shard_map/all_to_all | solution.py:131
  114.6 0.9 reduce_sum.84
  115.4 4.7 %all-to-all-start.2 = ((bf16[4,16,2560]{2,1,0:T(8,128)(2,1)}), bf16[4,16,2560]{2,1,0:T(8,128)(2,1)S(1)}, u32[]{:S(2)}, u32[]{:S(2)}) async-start(bf16[4,16,2560]{2,1,0:T(8,128)(2,1)} %reduce_sum.84), calls=%async_computation.2 | async-start | bytes 655360 | tf_op jit(solution)/shard_map/all_to_all | solution.py:133
  120.8 12.0 %all-to-all-done.2 = bf16[4,16,2560]{2,1,0:T(8,128)(2,1)S(1)} async-done(((bf16[4,16,2560]{2,1,0:T(8,128)(2,1)}), bf16[4,16,2560]{2,1,0:T(8,128)(2,1)S(1)}, u32[]{:S(2)}, u32[]{:S(2)}) %all-to-all-start.2) | async-done | bytes 327712 | tf_op jit(solution)/shard_map/all_to_all | solution.py:133
  (65 shorter events, 5.7 us)
Async XLA Ops:
  0.6 109.2 %copy-start = (bf16[256,2560]{1,0:T(8,128)(2,1)S(1)}, bf16[256,2560]{1,0:T(8,128)(2,1)}, u32[]{:S(2)}) copy-start(bf16[256,2560]{1,0:T(8,128)(2,1)} %param.14) | copy-start | bytes 3932164
  19.0 3.6 %copy-start.8 = (s32[16]{0:T(128)S(1)}, s32[16]{0:T(128)}, u32[]{:S(2)}) copy-start(s32[16]{0:T(128)} %param.17) | copy-start | bytes 196
  19.0 4.1 %copy-start.6 = (f32[128]{0:T(128)S(1)}, f32[128]{0:T(128)}, u32[]{:S(2)}) copy-start(f32[128]{0:T(128)} %param.16) | copy-start | bytes 1540
  22.5 48.2 %copy-start.7 = (f32[128]{0:T(128)S(1)}, f32[128]{0:T(128)}, u32[]{:S(2)}) copy-start(f32[128]{0:T(128)} %param.15) | copy-start | bytes 1540
  22.6 1.9 %copy-start.5 = (bf16[128,128]{1,0:T(8,128)(2,1)}, bf16[128,128]{1,0:T(8,128)(2,1)S(1)}, u32[]{:S(2)}) copy-start(bf16[128,128]{1,0:T(8,128)(2,1)S(1)} %slice.94) | copy-start | bytes 98308
  23.5 0.9 copy-start.1
  23.5 0.9 copy-start.3
  24.5 14.9 %all-to-all-start = ((bf16[8,128,256]{2,1,0:T(8,128)(2,1)}), bf16[8,128,256]{2,1,0:T(8,128)(2,1)S(1)}, u32[]{:S(2)}, u32[]{:S(2)}) async-start(bf16[8,128,256]{2,1,0:T(8,128)(2,1)} %broadcast_in_dim.31), calls=%async_computation | async-start | bytes 1048576 | tf_op jit(solution)/shard_map/all_to_all | solution.py:99
  39.4 20.8 %collective-permute-start = (bf16[8,128,256]{2,1,0:T(8,128)(2,1)S(1)}, bf16[8,128,256]{2,1,0:T(8,128)(2,1)}, u32[]{:S(2)}, u32[]{:S(2)}) collective-permute-start(bf16[8,128,256]{2,1,0:T(8,128)(2,1)S(1)} %all-to-all-done), channel_id=1, source_target_pairs={{0,64},{64,128},{128,192},{192,256},{256,320},{320,384},{384,448},... | collective-permute-start | bytes 1572872 | tf_op jit(solution)/shard_map/ppermute | solution.py:51
  45.5 19.5 %collective-permute-start.1 = (bf16[8,128,256]{2,1,0:T(8,128)(2,1)S(1)}, bf16[8,128,256]{2,1,0:T(8,128)(2,1)}, u32[]{:S(2)}, u32[]{:S(2)}) collective-permute-start(bf16[8,128,256]{2,1,0:T(8,128)(2,1)S(1)} %all-to-all-done), channel_id=1, source_target_pairs={{0,448},{64,0},{128,64},{192,128},{256,192},{320,256},{384,320},{4... | collective-permute-start | bytes 1572872 | tf_op jit(solution)/shard_map/ppermute | solution.py:52
  60.1 15.8 %collective-permute-start.2 = (bf16[8,128,256]{2,1,0:T(8,128)(2,1)}, bf16[8,128,256]{2,1,0:T(8,128)(2,1)S(1)}, u32[]{:S(2)}, u32[]{:S(2)}) collective-permute-start(bf16[8,128,256]{2,1,0:T(8,128)(2,1)} %collective-permute-done), channel_id=1, source_target_pairs={{0,64},{64,128},{128,192},{192,256},{256,320},{320,384},{384,448},... | collective-permute-start | bytes 1572872 | tf_op jit(solution)/shard_map/ppermute | solution.py:51
  65.0 15.7 %collective-permute-start.3 = (bf16[8,128,256]{2,1,0:T(8,128)(2,1)}, bf16[8,128,256]{2,1,0:T(8,128)(2,1)S(1)}, u32[]{:S(2)}, u32[]{:S(2)}) collective-permute-start(bf16[8,128,256]{2,1,0:T(8,128)(2,1)} %collective-permute-done.1), channel_id=1, source_target_pairs={{0,448},{64,0},{128,64},{192,128},{256,192},{320,256},{384,320},{4... | collective-permute-start | bytes 1572872 | tf_op jit(solution)/shard_map/ppermute | solution.py:52
  75.9 14.7 %collective-permute-start.4 = (bf16[8,128,256]{2,1,0:T(8,128)(2,1)S(1)}, bf16[8,128,256]{2,1,0:T(8,128)(2,1)S(1)}, u32[]{:S(2)}, u32[]{:S(2)}) collective-permute-start(bf16[8,128,256]{2,1,0:T(8,128)(2,1)S(1)} %collective-permute-done.2), channel_id=1, source_target_pairs={{0,64},{64,128},{128,192},{192,256},{256,320},{320,384},{384,448},... | collective-permute-start | bytes 1572872 | tf_op jit(solution)/shard_map/ppermute | solution.py:51
  80.7 14.3 %collective-permute-start.5 = (bf16[8,128,256]{2,1,0:T(8,128)(2,1)S(1)}, bf16[8,128,256]{2,1,0:T(8,128)(2,1)S(1)}, u32[]{:S(2)}, u32[]{:S(2)}) collective-permute-start(bf16[8,128,256]{2,1,0:T(8,128)(2,1)S(1)} %collective-permute-done.3), channel_id=1, source_target_pairs={{0,448},{64,0},{128,64},{192,128},{256,192},{320,256},{384,320},{4... | collective-permute-start | bytes 1572872 | tf_op jit(solution)/shard_map/ppermute | solution.py:52
  90.6 10.1 %collective-permute-start.6 = (bf16[4,128,256]{2,1,0:T(8,128)(2,1)S(1)}, bf16[4,128,256]{2,1,0:T(8,128)(2,1)S(1)}, u32[]{:S(2)}, u32[]{:S(2)}) collective-permute-start(bf16[4,128,256]{2,1,0:T(8,128)(2,1)S(1)} %slice.57), channel_id=1, source_target_pairs={{0,64},{64,128},{128,192},{192,256},{256,320},{320,384},{384,448},... | collective-permute-start | bytes 786440 | tf_op jit(solution)/shard_map/ppermute | solution.py:59
  95.0 9.5 %collective-permute-start.7 = (bf16[4,128,256]{2,1,0:T(8,128)(2,1)S(1)}, bf16[4,128,256]{2,1,0:T(8,128)(2,1)S(1)}, u32[]{:S(2)}, u32[]{:S(2)}) collective-permute-start(bf16[4,128,256]{2,1,0:T(8,128)(2,1)S(1)} %slice.58), channel_id=1, source_target_pairs={{0,448},{64,0},{128,64},{192,128},{256,192},{320,256},{384,320},{4... | collective-permute-start | bytes 786440 | tf_op jit(solution)/shard_map/ppermute | solution.py:59
  109.8 10.3 %copy-start.2 = (bf16[128,64]{1,0:T(8,128)(2,1)S(1)}, bf16[128,64]{1,0:T(8,128)(2,1)}, u32[]{:S(2)}) copy-start(bf16[128,64]{1,0:T(8,128)(2,1)} %copy-done.1) | copy-start | bytes 49156
  109.9 10.3 %copy-start.4 = (bf16[128,64]{1,0:T(8,128)(2,1)S(1)}, bf16[128,64]{1,0:T(8,128)(2,1)}, u32[]{:S(2)}) copy-start(bf16[128,64]{1,0:T(8,128)(2,1)} %copy-done.3) | copy-start | bytes 49156
  115.4 17.3 %all-to-all-start.2 = ((bf16[4,16,2560]{2,1,0:T(8,128)(2,1)}), bf16[4,16,2560]{2,1,0:T(8,128)(2,1)S(1)}, u32[]{:S(2)}, u32[]{:S(2)}) async-start(bf16[4,16,2560]{2,1,0:T(8,128)(2,1)} %reduce_sum.84), calls=%async_computation.2 | async-start | bytes 655360 | tf_op jit(solution)/shard_map/all_to_all | solution.py:133

commit v6 on v5

--- a/solution.py
+++ b/solution.py
@@ -93,17 +93,16 @@
     value_flat = proj[:, q_cols + kv_cols :].astype(jnp.bfloat16)
 
     nx, nlo = lax.axis_size("x"), lax.axis_size("ylo")
-    piece = jnp.concatenate([key_flat, value_flat], axis=1)[None]
-    block_ids = jnp.zeros((1,), jnp.int32)
     plane = nx * nlo
-    piece = lax.all_to_all(jnp.broadcast_to(piece, (plane,) + piece.shape[1:]), ("x", "ylo"), 0, 0, tiled=True)
-    block_ids = jnp.arange(plane, dtype=jnp.int32)
-    piece, block_ids = ring_gather(piece, block_ids, "z", nx * nlo)
-    span = piece.shape[0] * tokens
-    kv_all = piece.reshape(span, 2 * kv_cols)
+    kp = lax.all_to_all(jnp.broadcast_to(key_flat[None], (plane, tokens, kv_cols)), ("x", "ylo"), 0, 0, tiled=True)
+    kp, block_ids = ring_gather(kp, jnp.arange(plane, dtype=jnp.int32), "z", plane)
+    vz, unused = ring_gather(value_flat[None], jnp.zeros((1,), jnp.int32), "z", plane)
+    vp = lax.all_to_all(jnp.broadcast_to(vz[None], (plane,) + vz.shape), ("x", "ylo"), 0, 0, tiled=False)
+    vp = jnp.swapaxes(vp, 0, 1)
+    span = kp.shape[0] * tokens
     key_pos = (block_ids[:, None] * tokens + jnp.arange(tokens, dtype=jnp.int32)[None, :]).reshape(span)
-    key_heads = kv_all[:, :kv_cols].reshape(span, kv_local, head_dim)
-    value_heads = kv_all[:, kv_cols:].reshape(span, kv_local, head_dim)
+    key_heads = kp.reshape(span, kv_local, head_dim)
+    value_heads = vp.reshape(span, kv_local, head_dim)
     query_grid = queries.reshape(tokens, kv_local, group, head_dim)
     inv_root = 1.0 / math.sqrt(head_dim)
     score = (

time: 135 us -> 166 us (1.23)
  waiting for transfers between devices: 39.6 us -> 14.1 us
  starting transfers between devices: 44.9 us -> 68.3 us
  blocking collectives: 22.6 us -> 40.4 us
  local copies, waits for them, and re-layouts: 5.14 us -> 19.5 us
  matrix products: 7.1 us -> 10.8 us
  other arithmetic: 13 us -> 10.8 us
    all_to_all x2, waiting for transfers between devices: 20.1 us -> 0.01 us  [the longest x1 0.01 us: on_device(): lax.all_to_all(jnp.broadcast_to(vz[None], (plane,) + vz.shape), ('x', 'yl...]
    all_to_all x0 -> x1, blocking collectives: none -> 17.8 us  [on_device(): part = lax.all_to_all(part, 'yhi', 0, 0, tiled=True)]
    ppermute x3 -> x6, starting transfers between devices: 20.1 us -> 34.4 us  [ring_gather(): b = lax.ppermute(b, name, ccw)]
    ppermute x3 -> x6, starting transfers between devices: 6.18 us -> 13.9 us  [ring_gather(): a = lax.ppermute(a, name, cw)]
    ppermute x0 -> x1, waiting for transfers between devices: none -> 5.05 us  [ring_gather(): pieces += [lax.ppermute(a, name, cw)]]
    ppermute x3 -> x6, waiting for transfers between devices: 11.3 us -> 6.79 us  [ring_gather(): a = lax.ppermute(a, name, cw)]
    ppermute x3 -> x6, waiting for transfers between devices: 4.47 us -> 0.02 us  [ring_gather(): b = lax.ppermute(b, name, ccw)]
    another operation x1 -> x2, local copies, waits for them, and re-layouts: 0.08 us -> 4.35 us
  transfers between devices with their start and end apart: 10 -> 17, of which waited for: 9 -> 6; matrix products, arithmetic and copies ran while one was open for 9% -> 11% of each run, Pallas kernels for 0% -> 0%
where the time goes in v6:
time: 166 us; the launch traced here: 165 us
  starting transfers between devices  68.3 us (41%)
  blocking collectives  40.4 us (24%)
  local copies, waits for them, and re-layouts  19.5 us (12%)
  waiting for transfers between devices  14.1 us (8%)
  other arithmetic  10.8 us (7%)
  matrix products  10.8 us (7%)
    ppermute x6, starting transfers between devices, ring_gather(): b = lax.ppermute(b, name, ccw)  34.4 us
    all_gather x1, blocking collectives, on_device(): piece = lax.all_gather(hidden_in, TEN, axis=1, tiled=True)  18.4 us
    all_to_all x1, blocking collectives, on_device(): part = lax.all_to_all(part, 'yhi', 0, 0, tiled=True)  17.8 us
    ppermute x6, starting transfers between devices, ring_gather(): a = lax.ppermute(a, name, cw)  13.9 us
    ppermute x6, waiting for transfers between devices, ring_gather(): a = lax.ppermute(a, name, cw)  6.79 us
    all_to_all x1, starting transfers between devices, on_device(): lax.all_to_all(jnp.broadcast_to(vz[None], (plane,) + vz.shape), ('x', 'yl...  5.7 us
    ppermute x1, starting transfers between devices, ring_gather(): lax.ppermute(b[m // 2:], name, ccw)  5.56 us
    dot_general x1, matrix products, on_device(): jnp.einsum('hgqk,khd->hgqd', weights.astype(jnp.bfloat16), value_heads, p...  5.55 us
  transfers between devices with their start and end apart: 17, of which 6 were waited for; matrix products, arithmetic and copies ran while one was open for 11% of the time, Pallas kernels for 0%

profile of v6, /device:TPU:6, one launch (start us, length us, event | category | flops | bytes accessed | tf_op | source)
XLA Modules:
  0.0 165.1 jit_solution(8914091443264214410)
XLA Ops:
  0.6 18.4 %all_gather.3 = bf16[128,2560]{0,1:T(8,128)(2,1)S(1)} all-gather(bf16[128,320]{0,1:T(8,128)(2,1)} %param.9), channel_id=1, replica_groups=mesh['z'=8,'x'=4,'ylo'=2,'yhi'=4,'core'=2] {'yhi','core'}, dimensions={1}, use_global_device_ids=true | all-gather | bytes 737280 | tf_op jit(solution)/shard_map/all_gather | solution.py:76
  19.4 3.1 %fusion.18 = f32[128,512]{1,0:T(8,128)S(1)} fusion(bf16[2560,128]{1,0:T(8,128)(2,1)} %param.13, bf16[2560,128]{1,0:T(8,128)(2,1)} %param.12, bf16[2560,256]{1,0:T(8,128)(2,1)} %param.11, bf16[128,2560]{0,1:T(8,128)(2,1)S(1)} %all_gather.3, f32[2560]{0:T(1024)} %param.10, f32[128]{0:T(128)S(1)} %add_rsqrt_fusion.2), kind=kOutput, calls=%fused_computation.23 | convolution fusion | flops 344457216 | bytes 3549696 | tf_op jit(solution)/shard_map/dot_general | solution.py:79
  22.5 4.3 %collective-permute-start.8 = (bf16[1,128,128]{2,1,0:T(8,128)(2,1)S(1)}, bf16[1,128,128]{2,1,0:T(8,128)(2,1)S(1)}, u32[]{:S(2)}, u32[]{:S(2)}) collective-permute-start(bf16[1,128,128]{2,1,0:T(8,128)(2,1)S(1)} %bitcast.53), channel_id=1, source_target_pairs={{0,64},{64,128},{128,192},{192,256},{256,320},{320,384},{384,448},... | collective-permute-start | bytes 98312 | tf_op jit(solution)/shard_map/ppermute | solution.py:51
  26.8 8.7 %collective-permute-start.9 = (bf16[1,128,128]{2,1,0:T(8,128)(2,1)S(1)}, bf16[1,128,128]{2,1,0:T(8,128)(2,1)S(1)}, u32[]{:S(2)}, u32[]{:S(2)}) collective-permute-start(bf16[1,128,128]{2,1,0:T(8,128)(2,1)S(1)} %bitcast.54), channel_id=1, source_target_pairs={{0,448},{64,0},{128,64},{192,128},{256,192},{320,256},{384,320},{4... | collective-permute-start | bytes 98312 | tf_op jit(solution)/shard_map/ppermute | solution.py:52
  37.4 5.0 %all-to-all-start = ((bf16[8,128,128]{2,1,0:T(8,128)(2,1)}), bf16[8,128,128]{2,1,0:T(8,128)(2,1)S(1)}, u32[]{:S(2)}, u32[]{:S(2)}) async-start(bf16[8,128,128]{2,1,0:T(8,128)(2,1)} %broadcast_in_dim.35), calls=%async_computation | async-start | bytes 524288 | tf_op jit(solution)/shard_map/all_to_all | solution.py:97
  42.7 1.9 %collective-permute-start.10 = (bf16[1,128,128]{2,1,0:T(8,128)(2,1)S(1)}, bf16[1,128,128]{2,1,0:T(8,128)(2,1)S(1)}, u32[]{:S(2)}, u32[]{:S(2)}) collective-permute-start(bf16[1,128,128]{2,1,0:T(8,128)(2,1)S(1)} %collective-permute-done.8), channel_id=1, source_target_pairs={{0,64},{64,128},{128,192},{192,256},{256,320},{320,384},{384,448},... | collective-permute-start | bytes 98312 | tf_op jit(solution)/shard_map/ppermute | solution.py:51
  44.7 5.1 %collective-permute-start.11 = (bf16[1,128,128]{2,1,0:T(8,128)(2,1)S(1)}, bf16[1,128,128]{2,1,0:T(8,128)(2,1)S(1)}, u32[]{:S(2)}, u32[]{:S(2)}) collective-permute-start(bf16[1,128,128]{2,1,0:T(8,128)(2,1)S(1)} %collective-permute-done.9), channel_id=1, source_target_pairs={{0,448},{64,0},{128,64},{192,128},{256,192},{320,256},{384,320},{4... | collective-permute-start | bytes 98312 | tf_op jit(solution)/shard_map/ppermute | solution.py:52
  49.8 1.9 %collective-permute-start.12 = (bf16[1,128,128]{2,1,0:T(8,128)(2,1)S(1)}, bf16[1,128,128]{2,1,0:T(8,128)(2,1)S(1)}, u32[]{:S(2)}, u32[]{:S(2)}) collective-permute-start(bf16[1,128,128]{2,1,0:T(8,128)(2,1)S(1)} %collective-permute-done.10), channel_id=1, source_target_pairs={{0,64},{64,128},{128,192},{192,256},{256,320},{320,384},{384,448},... | collective-permute-start | bytes 98312 | tf_op jit(solution)/shard_map/ppermute | solution.py:51
  51.8 5.1 %collective-permute-start.13 = (bf16[1,128,128]{2,1,0:T(8,128)(2,1)S(1)}, bf16[1,128,128]{2,1,0:T(8,128)(2,1)S(1)}, u32[]{:S(2)}, u32[]{:S(2)}) collective-permute-start(bf16[1,128,128]{2,1,0:T(8,128)(2,1)S(1)} %collective-permute-done.11), channel_id=1, source_target_pairs={{0,448},{64,0},{128,64},{192,128},{256,192},{320,256},{384,320},{4... | collective-permute-start | bytes 98312 | tf_op jit(solution)/shard_map/ppermute | solution.py:52
  56.9 1.9 %collective-permute-start.14 = (bf16[1,128,128]{2,1,0:T(8,128)(2,1)S(1)}, bf16[1,128,128]{2,1,0:T(8,128)(2,1)S(1)}, u32[]{:S(2)}, u32[]{:S(2)}) collective-permute-start(bf16[1,128,128]{2,1,0:T(8,128)(2,1)S(1)} %collective-permute-done.12), channel_id=1, source_target_pairs={{0,64},{64,128},{128,192},{192,256},{256,320},{320,384},{384,448},... | collective-permute-start | bytes 98312 | tf_op jit(solution)/shard_map/ppermute | solution.py:62
  58.9 5.0 %collective-permute-done.14 = bf16[1,128,128]{2,1,0:T(8,128)(2,1)S(1)} collective-permute-done((bf16[1,128,128]{2,1,0:T(8,128)(2,1)S(1)}, bf16[1,128,128]{2,1,0:T(8,128)(2,1)S(1)}, u32[]{:S(2)}, u32[]{:S(2)}) %collective-permute-start.14) | collective-permute-done | bytes 32800 | tf_op jit(solution)/shard_map/ppermute | solution.py:62
  65.8 5.7 %all-to-all-start.1 = ((bf16[8,8,128,128]{2,1,3,0:T(8,128)(2,1)}), bf16[8,8,128,128]{2,1,3,0:T(8,128)(2,1)S(1)}, u32[]{:S(2)}, u32[]{:S(2)}) async-start(bf16[8,8,128,128]{2,1,3,0:T(8,128)(2,1)} %broadcast_in_dim.39), calls=%async_computation.1 | async-start | bytes 4194304 | tf_op jit(solution)/shard_map/all_to_all | solution.py:100
  71.5 4.5 %compare_and_fusion = pred[128,8192]{0,1:T(8,128)(4,1)} fusion(s32[128]{0:T(128)S(1)} %iota_add_fusion, s32[128]{0:T(128)S(1)} %select_reduce_fusion, s32[8192]{0:T(1024)S(1)} %add_bitcast_fusion), kind=kLoop, calls=%fused_computation.11 | loop fusion | flops 3145728 | bytes 1082368 | tf_op jit(solution)/shard_map/and | solution.py:112
  79.2 1.7 %multiply_reduce_fusion = f32[128,2]{1,0:T(8,128)} fusion(f32[128,2,128]{2,1,0:T(2,128)} %reshape.381), kind=kLoop, calls=%fused_computation.31 | loop fusion | flops 65280 | bytes 132096 | tf_op jit(solution)/shard_map/reduce_sum | solution.py:30
  82.2 1.9 %collective-permute-start = (bf16[8,128,128]{2,1,0:T(8,128)(2,1)}, bf16[8,128,128]{2,1,0:T(8,128)(2,1)S(1)}, u32[]{:S(2)}, u32[]{:S(2)}) collective-permute-start(bf16[8,128,128]{2,1,0:T(8,128)(2,1)} %copy-done.4), channel_id=1, source_target_pairs={{0,64},{64,128},{128,192},{192,256},{256,320},{320,384},{384,448},... | collective-permute-start | bytes 786440 | tf_op jit(solution)/shard_map/ppermute | solution.py:51
  84.1 5.1 %collective-permute-start.1 = (bf16[8,128,128]{2,1,0:T(8,128)(2,1)}, bf16[8,128,128]{2,1,0:T(8,128)(2,1)S(1)}, u32[]{:S(2)}, u32[]{:S(2)}) collective-permute-start(bf16[8,128,128]{2,1,0:T(8,128)(2,1)} %copy-done.4), channel_id=1, source_target_pairs={{0,448},{64,0},{128,64},{192,128},{256,192},{320,256},{384,320},{4... | collective-permute-start | bytes 786440 | tf_op jit(solution)/shard_map/ppermute | solution.py:52
  89.4 2.5 %collective-permute-done = bf16[8,128,128]{2,1,0:T(8,128)(2,1)S(1)} collective-permute-done((bf16[8,128,128]{2,1,0:T(8,128)(2,1)}, bf16[8,128,128]{2,1,0:T(8,128)(2,1)S(1)}, u32[]{:S(2)}, u32[]{:S(2)}) %collective-permute-start) | collective-permute-done | bytes 262176 | tf_op jit(solution)/shard_map/ppermute | solution.py:51
  91.8 1.9 %collective-permute-start.2 = (bf16[8,128,128]{2,1,0:T(8,128)(2,1)S(1)}, bf16[8,128,128]{2,1,0:T(8,128)(2,1)S(1)}, u32[]{:S(2)}, u32[]{:S(2)}) collective-permute-start(bf16[8,128,128]{2,1,0:T(8,128)(2,1)S(1)} %collective-permute-done), channel_id=1, source_target_pairs={{0,64},{64,128},{128,192},{192,256},{256,320},{320,384},{384,448},... | collective-permute-start | bytes 786440 | tf_op jit(solution)/shard_map/ppermute | solution.py:51
  93.8 5.1 %collective-permute-start.3 = (bf16[8,128,128]{2,1,0:T(8,128)(2,1)S(1)}, bf16[8,128,128]{2,1,0:T(8,128)(2,1)S(1)}, u32[]{:S(2)}, u32[]{:S(2)}) collective-permute-start(bf16[8,128,128]{2,1,0:T(8,128)(2,1)S(1)} %collective-permute-done.1), channel_id=1, source_target_pairs={{0,448},{64,0},{128,64},{192,128},{256,192},{320,256},{384,320},{4... | collective-permute-start | bytes 786440 | tf_op jit(solution)/shard_map/ppermute | solution.py:52
  101.3 1.9 %collective-permute-start.4 = (bf16[8,128,128]{2,1,0:T(8,128)(2,1)S(1)}, bf16[8,128,128]{2,1,0:T(8,128)(2,1)S(1)}, u32[]{:S(2)}, u32[]{:S(2)}) collective-permute-start(bf16[8,128,128]{2,1,0:T(8,128)(2,1)S(1)} %collective-permute-done.2), channel_id=1, source_target_pairs={{0,64},{64,128},{128,192},{192,256},{256,320},{320,384},{384,448},... | collective-permute-start | bytes 786440 | tf_op jit(solution)/shard_map/ppermute | solution.py:51
  103.2 5.1 %collective-permute-start.5 = (bf16[8,128,128]{2,1,0:T(8,128)(2,1)S(1)}, bf16[8,128,128]{2,1,0:T(8,128)(2,1)S(1)}, u32[]{:S(2)}, u32[]{:S(2)}) collective-permute-start(bf16[8,128,128]{2,1,0:T(8,128)(2,1)S(1)} %collective-permute-done.3), channel_id=1, source_target_pairs={{0,448},{64,0},{128,64},{192,128},{256,192},{320,256},{384,320},{4... | collective-permute-start | bytes 786440 | tf_op jit(solution)/shard_map/ppermute | solution.py:52
  108.5 3.0 %collective-permute-done.4 = bf16[8,128,128]{2,1,0:T(8,128)(2,1)S(1)} collective-permute-done((bf16[8,128,128]{2,1,0:T(8,128)(2,1)S(1)}, bf16[8,128,128]{2,1,0:T(8,128)(2,1)S(1)}, u32[]{:S(2)}, u32[]{:S(2)}) %collective-permute-start.4) | collective-permute-done | bytes 262176 | tf_op jit(solution)/shard_map/ppermute | solution.py:51
  111.6 1.9 %collective-permute-start.6 = (bf16[4,128,128]{2,1,0:T(8,128)(2,1)S(1)}, bf16[4,128,128]{2,1,0:T(8,128)(2,1)S(1)}, u32[]{:S(2)}, u32[]{:S(2)}) collective-permute-start(bf16[4,128,128]{2,1,0:T(8,128)(2,1)S(1)} %slice.49), channel_id=1, source_target_pairs={{0,64},{64,128},{128,192},{192,256},{256,320},{320,384},{384,448},... | collective-permute-start | bytes 393224 | tf_op jit(solution)/shard_map/ppermute | solution.py:59
  113.5 5.6 %collective-permute-start.7 = (bf16[4,128,128]{2,1,0:T(8,128)(2,1)S(1)}, bf16[4,128,128]{2,1,0:T(8,128)(2,1)S(1)}, u32[]{:S(2)}, u32[]{:S(2)}) collective-permute-start(bf16[4,128,128]{2,1,0:T(8,128)(2,1)S(1)} %slice.50), channel_id=1, source_target_pairs={{0,448},{64,0},{128,64},{192,128},{256,192},{320,256},{384,320},{4... | collective-permute-start | bytes 393224 | tf_op jit(solution)/shard_map/ppermute | solution.py:59
  119.7 1.7 %collective-permute-done.7 = bf16[4,128,128]{2,1,0:T(8,128)(2,1)S(1)} collective-permute-done((bf16[4,128,128]{2,1,0:T(8,128)(2,1)S(1)}, bf16[4,128,128]{2,1,0:T(8,128)(2,1)S(1)}, u32[]{:S(2)}, u32[]{:S(2)}) %collective-permute-start.7) | collective-permute-done | bytes 131104 | tf_op jit(solution)/shard_map/ppermute | solution.py:59
  121.4 1.8 %fusion.43 = (f32[2,128]{1,0:T(2,128)S(1)}, f32[1,2,128,8192]{2,3,1,0:T(8,128)S(1)}) fusion(bf16[8192,128,1]{1,0,2:T(8,128)(2,1)S(1)} %bitcast.55, bf16[128,2,64]{2,0,1:T(8,128)(2,1)S(1)} %get-tuple-element.6, bf16[128,2,64]{2,0,1:T(8,128)(2,1)S(1)} %get-tuple-element.5, pred[128,8192]{0,1:T(8,128)(4,1)S(1)} %copy-done.2), kind=kOutput, calls=%fused_computation.95 | convolution fusion | flops 543293184 | bytes 11600896 | tf_op jit(solution)/shard_map/qhgd,khd->hgqk/dot_general | solution.py:109
  123.3 3.2 %copy-done.1 = f32[1,2,128,8192]{2,3,1,0:T(8,128)} copy-done((f32[1,2,128,8192]{2,3,1,0:T(8,128)}, f32[1,2,128,8192]{2,3,1,0:T(8,128)S(1)}, u32[]{:S(2)}) %copy-start.1) | copy-done | bytes 8388632
  128.2 3.8 %copy.38 = bf16[8,8,128,128]{2,1,0,3:T(8,128)(2,1)} copy(bf16[8,8,128,128]{2,0,3,1:T(8,128)(2,1)S(1)} %bitcast.49) | data formatting | bytes 4194304 | tf_op jit(solution)/shard_map/transpose | solution.py:101
  131.9 4.3 %reshape.386 = bf16[8192,128,1]{0,1,2:T(8,128)(2,1)} reshape(bf16[8,8,128,128]{2,1,0,3:T(8,128)(2,1)} %copy.38) | data formatting | bytes 4194304 | tf_op jit(solution)/shard_map/reshape.23
  136.2 5.5 %divide_convert_fusion = bf16[2,128,128]{1,2,0:T(8,128)(2,1)S(1)} fusion(f32[2,128]{1,0:T(2,128)S(1)} %fusion.2, bf16[8192,128,1]{0,1,2:T(8,128)(2,1)} %reshape.386, f32[1,2,128,8192]{2,3,1,0:T(8,128)} %copy-done.1, f32[2,128]{1,0:T(2,128)S(1)} %get-tuple-element.13, pred[128,8192]{0,1:T(8,128)(4,1)S(1)} %copy-done.3), kind=kOutput, calls=%fused_computation.28 | convolution fusion | flops 543227904 | bytes 11601920 | tf_op jit(solution)/shard_map/hgqk,khd->hgqd/dot_general | solution.py:117
  142.2 4.3 %all_to_all.20 = bf16[2,4,16,2560]{3,2,1,0:T(8,128)(2,1)S(1)} all-to-all(bf16[2,4,16,2560]{3,2,1,0:T(8,128)(2,1)S(1)} %bitcast.51), channel_id=1, replica_groups=mesh['z'=8,'x'=4,'ylo'=2,'yhi'=4,'core'=2] {'core'}, dimensions={0} | all-to-all | bytes 1310720 | tf_op jit(solution)/shard_map/all_to_all | solution.py:130
  146.6 17.8 %all_to_all.21 = bf16[4,16,2560]{2,1,0:T(8,128)(2,1)S(1)} all-to-all(bf16[4,16,2560]{2,1,0:T(8,128)(2,1)S(1)} %reduce_sum.84), channel_id=1, replica_groups=mesh['z'=8,'x'=4,'ylo'=2,'yhi'=4,'core'=2] {'yhi'}, dimensions={0} | all-to-all | bytes 655360 | tf_op jit(solution)/shard_map/all_to_all | solution.py:132
  (94 shorter events, 14.9 us)
Async XLA Ops:
  0.6 141.1 %copy-start = (bf16[256,2560]{1,0:T(8,128)(2,1)S(1)}, bf16[256,2560]{1,0:T(8,128)(2,1)}, u32[]{:S(2)}) copy-start(bf16[256,2560]{1,0:T(8,128)(2,1)} %param.14) | copy-start | bytes 3932164
  19.4 16.3 %copy-start.10 = (s32[16]{0:T(128)S(1)}, s32[16]{0:T(128)}, u32[]{:S(2)}) copy-start(s32[16]{0:T(128)} %param.17) | copy-start | bytes 196
  19.4 16.8 %copy-start.8 = (f32[128]{0:T(128)S(1)}, f32[128]{0:T(128)}, u32[]{:S(2)}) copy-start(f32[128]{0:T(128)} %param.16) | copy-start | bytes 1540
  22.5 41.5 %copy-start.5 = (f32[128,512]{1,0:T(8,128)}, f32[128,512]{1,0:T(8,128)S(1)}, u32[]{:S(2)}) copy-start(f32[128,512]{1,0:T(8,128)S(1)} %fusion.18) | copy-start | bytes 786436
  22.5 43.3 %copy-start.7 = (bf16[128,128]{1,0:T(8,128)(2,1)}, bf16[128,128]{1,0:T(8,128)(2,1)S(1)}, u32[]{:S(2)}) copy-start(bf16[128,128]{1,0:T(8,128)(2,1)S(1)} %get-tuple-element.4) | copy-start | bytes 98308
  22.5 20.2 %collective-permute-start.8 = (bf16[1,128,128]{2,1,0:T(8,128)(2,1)S(1)}, bf16[1,128,128]{2,1,0:T(8,128)(2,1)S(1)}, u32[]{:S(2)}, u32[]{:S(2)}) collective-permute-start(bf16[1,128,128]{2,1,0:T(8,128)(2,1)S(1)} %bitcast.53), channel_id=1, source_target_pairs={{0,64},{64,128},{128,192},{192,256},{256,320},{320,384},{384,448},... | collective-permute-start | bytes 98312 | tf_op jit(solution)/shard_map/ppermute | solution.py:51
  26.8 17.8 %collective-permute-start.9 = (bf16[1,128,128]{2,1,0:T(8,128)(2,1)S(1)}, bf16[1,128,128]{2,1,0:T(8,128)(2,1)S(1)}, u32[]{:S(2)}, u32[]{:S(2)}) collective-permute-start(bf16[1,128,128]{2,1,0:T(8,128)(2,1)S(1)} %bitcast.54), channel_id=1, source_target_pairs={{0,448},{64,0},{128,64},{192,128},{256,192},{320,256},{384,320},{4... | collective-permute-start | bytes 98312 | tf_op jit(solution)/shard_map/ppermute | solution.py:52
  36.7 0.7 copy-start.6
  37.4 26.8 %all-to-all-start = ((bf16[8,128,128]{2,1,0:T(8,128)(2,1)}), bf16[8,128,128]{2,1,0:T(8,128)(2,1)S(1)}, u32[]{:S(2)}, u32[]{:S(2)}) async-start(bf16[8,128,128]{2,1,0:T(8,128)(2,1)} %broadcast_in_dim.35), calls=%async_computation | async-start | bytes 524288 | tf_op jit(solution)/shard_map/all_to_all | solution.py:97
  42.7 7.1 %collective-permute-start.10 = (bf16[1,128,128]{2,1,0:T(8,128)(2,1)S(1)}, bf16[1,128,128]{2,1,0:T(8,128)(2,1)S(1)}, u32[]{:S(2)}, u32[]{:S(2)}) collective-permute-start(bf16[1,128,128]{2,1,0:T(8,128)(2,1)S(1)} %collective-permute-done.8), channel_id=1, source_target_pairs={{0,64},{64,128},{128,192},{192,256},{256,320},{320,384},{384,448},... | collective-permute-start | bytes 98312 | tf_op jit(solution)/shard_map/ppermute | solution.py:51
  44.7 7.1 %collective-permute-start.11 = (bf16[1,128,128]{2,1,0:T(8,128)(2,1)S(1)}, bf16[1,128,128]{2,1,0:T(8,128)(2,1)S(1)}, u32[]{:S(2)}, u32[]{:S(2)}) collective-permute-start(bf16[1,128,128]{2,1,0:T(8,128)(2,1)S(1)} %collective-permute-done.9), channel_id=1, source_target_pairs={{0,448},{64,0},{128,64},{192,128},{256,192},{320,256},{384,320},{4... | collective-permute-start | bytes 98312 | tf_op jit(solution)/shard_map/ppermute | solution.py:52
  49.8 7.1 %collective-permute-start.12 = (bf16[1,128,128]{2,1,0:T(8,128)(2,1)S(1)}, bf16[1,128,128]{2,1,0:T(8,128)(2,1)S(1)}, u32[]{:S(2)}, u32[]{:S(2)}) collective-permute-start(bf16[1,128,128]{2,1,0:T(8,128)(2,1)S(1)} %collective-permute-done.10), channel_id=1, source_target_pairs={{0,64},{64,128},{128,192},{192,256},{256,320},{320,384},{384,448},... | collective-permute-start | bytes 98312 | tf_op jit(solution)/shard_map/ppermute | solution.py:51
  51.8 7.1 %collective-permute-start.13 = (bf16[1,128,128]{2,1,0:T(8,128)(2,1)S(1)}, bf16[1,128,128]{2,1,0:T(8,128)(2,1)S(1)}, u32[]{:S(2)}, u32[]{:S(2)}) collective-permute-start(bf16[1,128,128]{2,1,0:T(8,128)(2,1)S(1)} %collective-permute-done.11), channel_id=1, source_target_pairs={{0,448},{64,0},{128,64},{192,128},{256,192},{320,256},{384,320},{4... | collective-permute-start | bytes 98312 | tf_op jit(solution)/shard_map/ppermute | solution.py:52
  56.9 7.0 %collective-permute-start.14 = (bf16[1,128,128]{2,1,0:T(8,128)(2,1)S(1)}, bf16[1,128,128]{2,1,0:T(8,128)(2,1)S(1)}, u32[]{:S(2)}, u32[]{:S(2)}) collective-permute-start(bf16[1,128,128]{2,1,0:T(8,128)(2,1)S(1)} %collective-permute-done.12), channel_id=1, source_target_pairs={{0,64},{64,128},{128,192},{192,256},{256,320},{320,384},{384,448},... | collective-permute-start | bytes 98312 | tf_op jit(solution)/shard_map/ppermute | solution.py:62
  64.2 1.6 copy-start.4
  65.8 62.3 %all-to-all-start.1 = ((bf16[8,8,128,128]{2,1,3,0:T(8,128)(2,1)}), bf16[8,8,128,128]{2,1,3,0:T(8,128)(2,1)S(1)}, u32[]{:S(2)}, u32[]{:S(2)}) async-start(bf16[8,8,128,128]{2,1,3,0:T(8,128)(2,1)} %broadcast_in_dim.39), calls=%async_computation.1 | async-start | bytes 4194304 | tf_op jit(solution)/shard_map/all_to_all | solution.py:100
  71.5 17.7 %copy-start.9 = (f32[128]{0:T(128)S(1)}, f32[128]{0:T(128)}, u32[]{:S(2)}) copy-start(f32[128]{0:T(128)} %param.15) | copy-start | bytes 1540
  82.2 9.7 %collective-permute-start = (bf16[8,128,128]{2,1,0:T(8,128)(2,1)}, bf16[8,128,128]{2,1,0:T(8,128)(2,1)S(1)}, u32[]{:S(2)}, u32[]{:S(2)}) collective-permute-start(bf16[8,128,128]{2,1,0:T(8,128)(2,1)} %copy-done.4), channel_id=1, source_target_pairs={{0,64},{64,128},{128,192},{192,256},{256,320},{320,384},{384,448},... | collective-permute-start | bytes 786440 | tf_op jit(solution)/shard_map/ppermute | solution.py:51
  84.1 9.7 %collective-permute-start.1 = (bf16[8,128,128]{2,1,0:T(8,128)(2,1)}, bf16[8,128,128]{2,1,0:T(8,128)(2,1)S(1)}, u32[]{:S(2)}, u32[]{:S(2)}) collective-permute-start(bf16[8,128,128]{2,1,0:T(8,128)(2,1)} %copy-done.4), channel_id=1, source_target_pairs={{0,448},{64,0},{128,64},{192,128},{256,192},{320,256},{384,320},{4... | collective-permute-start | bytes 786440 | tf_op jit(solution)/shard_map/ppermute | solution.py:52
  91.8 9.5 %collective-permute-start.2 = (bf16[8,128,128]{2,1,0:T(8,128)(2,1)S(1)}, bf16[8,128,128]{2,1,0:T(8,128)(2,1)S(1)}, u32[]{:S(2)}, u32[]{:S(2)}) collective-permute-start(bf16[8,128,128]{2,1,0:T(8,128)(2,1)S(1)} %collective-permute-done), channel_id=1, source_target_pairs={{0,64},{64,128},{128,192},{192,256},{256,320},{320,384},{384,448},... | collective-permute-start | bytes 786440 | tf_op jit(solution)/shard_map/ppermute | solution.py:51
  93.8 9.5 %collective-permute-start.3 = (bf16[8,128,128]{2,1,0:T(8,128)(2,1)S(1)}, bf16[8,128,128]{2,1,0:T(8,128)(2,1)S(1)}, u32[]{:S(2)}, u32[]{:S(2)}) collective-permute-start(bf16[8,128,128]{2,1,0:T(8,128)(2,1)S(1)} %collective-permute-done.1), channel_id=1, source_target_pairs={{0,448},{64,0},{128,64},{192,128},{256,192},{320,256},{384,320},{4... | collective-permute-start | bytes 786440 | tf_op jit(solution)/shard_map/ppermute | solution.py:52
  100.0 21.4 %copy-start.2 = (pred[128,8192]{0,1:T(8,128)(4,1)S(1)}, pred[128,8192]{0,1:T(8,128)(4,1)}, u32[]{:S(2)}) copy-start(pred[128,8192]{0,1:T(8,128)(4,1)} %compare_and_fusion) | copy-start | bytes 3145732
  101.3 10.2 %collective-permute-start.4 = (bf16[8,128,128]{2,1,0:T(8,128)(2,1)S(1)}, bf16[8,128,128]{2,1,0:T(8,128)(2,1)S(1)}, u32[]{:S(2)}, u32[]{:S(2)}) collective-permute-start(bf16[8,128,128]{2,1,0:T(8,128)(2,1)S(1)} %collective-permute-done.2), channel_id=1, source_target_pairs={{0,64},{64,128},{128,192},{192,256},{256,320},{320,384},{384,448},... | collective-permute-start | bytes 786440 | tf_op jit(solution)/shard_map/ppermute | solution.py:51
  103.2 10.3 %collective-permute-start.5 = (bf16[8,128,128]{2,1,0:T(8,128)(2,1)S(1)}, bf16[8,128,128]{2,1,0:T(8,128)(2,1)S(1)}, u32[]{:S(2)}, u32[]{:S(2)}) collective-permute-start(bf16[8,128,128]{2,1,0:T(8,128)(2,1)S(1)} %collective-permute-done.3), channel_id=1, source_target_pairs={{0,448},{64,0},{128,64},{192,128},{256,192},{320,256},{384,320},{4... | collective-permute-start | bytes 786440 | tf_op jit(solution)/shard_map/ppermute | solution.py:52
  111.6 8.1 %collective-permute-start.6 = (bf16[4,128,128]{2,1,0:T(8,128)(2,1)S(1)}, bf16[4,128,128]{2,1,0:T(8,128)(2,1)S(1)}, u32[]{:S(2)}, u32[]{:S(2)}) collective-permute-start(bf16[4,128,128]{2,1,0:T(8,128)(2,1)S(1)} %slice.49), channel_id=1, source_target_pairs={{0,64},{64,128},{128,192},{192,256},{256,320},{320,384},{384,448},... | collective-permute-start | bytes 393224 | tf_op jit(solution)/shard_map/ppermute | solution.py:59
  113.5 7.9 %collective-permute-start.7 = (bf16[4,128,128]{2,1,0:T(8,128)(2,1)S(1)}, bf16[4,128,128]{2,1,0:T(8,128)(2,1)S(1)}, u32[]{:S(2)}, u32[]{:S(2)}) collective-permute-start(bf16[4,128,128]{2,1,0:T(8,128)(2,1)S(1)} %slice.50), channel_id=1, source_target_pairs={{0,448},{64,0},{128,64},{192,128},{256,192},{320,256},{384,320},{4... | collective-permute-start | bytes 393224 | tf_op jit(solution)/shard_map/ppermute | solution.py:59
  123.2 3.2 %copy-start.1 = (f32[1,2,128,8192]{2,3,1,0:T(8,128)}, f32[1,2,128,8192]{2,3,1,0:T(8,128)S(1)}, u32[]{:S(2)}) copy-start(f32[1,2,128,8192]{2,3,1,0:T(8,128)S(1)} %get-tuple-element.14) | copy-start | bytes 25165828
  131.9 4.3 %copy-start.3 = (pred[128,8192]{0,1:T(8,128)(4,1)S(1)}, pred[128,8192]{0,1:T(8,128)(4,1)}, u32[]{:S(2)}) copy-start(pred[128,8192]{0,1:T(8,128)(4,1)} %compare_and_fusion) | copy-start | bytes 3145732

commit v7 on v5

--- a/solution.py
+++ b/solution.py
@@ -73,11 +73,15 @@
     kv_local = kv_cols // head_dim
     group = q_cols // kv_cols
     combined = jnp.concatenate([w_query, w_key, w_value], axis=1)
-    piece = lax.all_gather(hidden_in, TEN, axis=1, tiled=True)
+    cols = lax.axis_size(TEN)
+    piece = lax.all_to_all(jnp.broadcast_to(hidden_in[None], (cols,) + hidden_in.shape), TEN, 0, 0, tiled=True)
     wide = piece.astype(jnp.float32)
-    scaled = (wide * norm_gain[None, :]).astype(jnp.bfloat16)
-    acc = jnp.dot(scaled, combined, preferred_element_type=jnp.float32)
-    sumsq = jnp.sum(wide * wide, axis=1)
+    scaled = (wide * norm_gain.reshape(cols, 1, -1)).astype(jnp.bfloat16)
+    acc = jnp.einsum(
+        "jtc,jcn->tn", scaled, combined.reshape(cols, -1, combined.shape[1]),
+        preferred_element_type=jnp.float32,
+    )
+    sumsq = jnp.sum(wide * wide, axis=(0, 2))
     proj = acc * lax.rsqrt(sumsq / width + norm_eps)[:, None]
     block_index = lax.axis_index(SEQ)
     token_pos = block_index * tokens + jnp.arange(tokens, dtype=jnp.int32)

time: 135 us -> 140 us (1.037)
  blocking collectives: 22.6 us -> 4.26 us
  starting transfers between devices: 44.9 us -> 54.4 us
  waiting for transfers between devices: 39.6 us -> 47.5 us
  local copies, waits for them, and re-layouts: 5.14 us -> 8.19 us
  other arithmetic: 13 us -> 15.5 us
    all_gather x1 -> x0, blocking collectives: 18.4 us -> none  [on_device(): piece = lax.all_gather(hidden_in, TEN, axis=1, tiled=True)]
    all_to_all x0 -> x1, waiting for transfers between devices: none -> 14.4 us  [on_device(): lax.all_to_all(jnp.broadcast_to(hidden_in[None], (cols,) + hidden_in.shap...]
    all_to_all x0 -> x1, starting transfers between devices: none -> 7.1 us  [on_device(): lax.all_to_all(jnp.broadcast_to(hidden_in[None], (cols,) + hidden_in.shap...]
    ppermute x3, waiting for transfers between devices: 11.3 us -> 5.18 us  [ring_gather(): a = lax.ppermute(a, name, cw)]
    concatenate x0 -> x1, other arithmetic: none -> 3.47 us  [on_device(): combined = jnp.concatenate([w_query, w_key, w_value], axis=1)]
    all_to_all x1, starting transfers between devices: 4.66 us -> 7.84 us  [on_device(): part = lax.all_to_all(part, 'yhi', 0, 0, tiled=True)]
    broadcast_in_dim x0 -> x1, local copies, waits for them, and re-layouts: none -> 1.92 us  [on_device(): jnp.broadcast_to(hidden_in[None], (cols,) + hidden_in.shape)]
    all_to_all x1, starting transfers between devices: 6.41 us -> 4.77 us  [on_device(): lax.all_to_all(jnp.broadcast_to(piece, (plane,) + piece.shape[1:]), ('x',...]
  transfers between devices with their start and end apart: 10 -> 11, of which waited for: 9 -> 10; matrix products, arithmetic and copies ran while one was open for 9% -> 12% of each run, Pallas kernels for 0% -> 0%
where the time goes in v7:
time: 140 us; the launch traced here: 138 us
  starting transfers between devices  54.4 us (39%)
  waiting for transfers between devices  47.5 us (34%)
  other arithmetic  15.5 us (11%)
  local copies, waits for them, and re-layouts  8.19 us (6%)
  matrix products  6.9 us (5%)
  blocking collectives  4.26 us (3%)
    ppermute x3, starting transfers between devices, ring_gather(): b = lax.ppermute(b, name, ccw)  19.8 us
    all_to_all x1, waiting for transfers between devices, on_device(): lax.all_to_all(jnp.broadcast_to(hidden_in[None], (cols,) + hidden_in.shap...  14.4 us
    all_to_all x1, waiting for transfers between devices, on_device(): part = lax.all_to_all(part, 'yhi', 0, 0, tiled=True)  11.3 us
    all_to_all x1, starting transfers between devices, on_device(): part = lax.all_to_all(part, 'yhi', 0, 0, tiled=True)  7.84 us
    ppermute x3, starting transfers between devices, ring_gather(): a = lax.ppermute(a, name, cw)  7.37 us
    all_to_all x1, starting transfers between devices, on_device(): lax.all_to_all(jnp.broadcast_to(hidden_in[None], (cols,) + hidden_in.shap...  7.1 us
    all_to_all x1, waiting for transfers between devices, on_device(): lax.all_to_all(jnp.broadcast_to(piece, (plane,) + piece.shape[1:]), ('x',...  6.74 us
    ppermute x3, waiting for transfers between devices, ring_gather(): b = lax.ppermute(b, name, ccw)  6.06 us
  transfers between devices with their start and end apart: 11, of which 10 were waited for; matrix products, arithmetic and copies ran while one was open for 12% of the time, Pallas kernels for 0%

profile of v7, /device:TPU:6, one launch (start us, length us, event | category | flops | bytes accessed | tf_op | source)
XLA Modules:
  0.0 137.7 jit_solution(1446440659913407938)
XLA Ops:
  0.6 1.9 %broadcast_in_dim.33 = bf16[8,128,320]{1,2,0:T(8,128)(2,1)} broadcast(bf16[128,320]{0,1:T(8,128)(2,1)} %param.9), dimensions={1,2} | broadcast | bytes 737280 | tf_op jit(solution)/shard_map/broadcast_in_dim | solution.py:77
  2.6 7.1 %all-to-all-start = ((bf16[8,128,320]{1,2,0:T(8,128)(2,1)}), bf16[8,128,320]{1,2,0:T(8,128)(2,1)S(1)}, u32[]{:S(2)}, u32[]{:S(2)}) async-start(bf16[8,128,320]{1,2,0:T(8,128)(2,1)} %broadcast_in_dim.33), calls=%async_computation | async-start | bytes 1310720 | tf_op jit(solution)/shard_map/all_to_all | solution.py:77
  12.2 3.5 %pad_maximum_fusion = bf16[2560,512]{1,0:T(8,128)(2,1)} fusion(bf16[2560,128]{1,0:T(8,128)(2,1)} %param.13, bf16[2560,128]{1,0:T(8,128)(2,1)} %param.12, bf16[2560,256]{1,0:T(8,128)(2,1)} %param.11), kind=kLoop, calls=%fused_computation.13 | loop fusion | flops 7864320 | bytes 5242880 | tf_op jit(solution)/shard_map/concatenate | solution.py:75
  15.7 14.4 %all-to-all-done = bf16[8,128,320]{1,2,0:T(8,128)(2,1)S(1)} async-done(((bf16[8,128,320]{1,2,0:T(8,128)(2,1)}), bf16[8,128,320]{1,2,0:T(8,128)(2,1)S(1)}, u32[]{:S(2)}, u32[]{:S(2)}) %all-to-all-start) | async-done | bytes 655392 | tf_op jit(solution)/shard_map/all_to_all | solution.py:77
  30.5 2.9 %fusion.12 = f32[128,512]{1,0:T(8,128)S(1)} fusion(bf16[8,320,512]{2,1,0:T(8,128)(2,1)} %bitcast.58, bf16[8,128,320]{1,2,0:T(8,128)(2,1)S(1)} %all-to-all-done, f32[8,320]{1,0:T(8,128)S(1)} %mul.212, f32[128]{0:T(128)S(1)} %add_rsqrt_fusion.2), kind=kOutput, calls=%fused_computation.21 | convolution fusion | flops 336592896 | bytes 3549696 | tf_op jit(solution)/shard_map/jtc,jcn->tn/dot_general | solution.py:80
  35.1 4.8 %all-to-all-start.1 = ((bf16[8,128,256]{2,1,0:T(8,128)(2,1)}), bf16[8,128,256]{2,1,0:T(8,128)(2,1)S(1)}, u32[]{:S(2)}, u32[]{:S(2)}) async-start(bf16[8,128,256]{2,1,0:T(8,128)(2,1)} %broadcast_in_dim.34), calls=%async_computation.1 | async-start | bytes 1048576 | tf_op jit(solution)/shard_map/all_to_all | solution.py:103
  40.1 6.7 %all-to-all-done.1 = bf16[8,128,256]{2,1,0:T(8,128)(2,1)S(1)} async-done(((bf16[8,128,256]{2,1,0:T(8,128)(2,1)}), bf16[8,128,256]{2,1,0:T(8,128)(2,1)S(1)}, u32[]{:S(2)}, u32[]{:S(2)}) %all-to-all-start.1) | async-done | bytes 524320 | tf_op jit(solution)/shard_map/all_to_all | solution.py:103
  46.9 3.6 %collective-permute-start = (bf16[8,128,256]{2,1,0:T(8,128)(2,1)S(1)}, bf16[8,128,256]{2,1,0:T(8,128)(2,1)}, u32[]{:S(2)}, u32[]{:S(2)}) collective-permute-start(bf16[8,128,256]{2,1,0:T(8,128)(2,1)S(1)} %all-to-all-done.1), channel_id=1, source_target_pairs={{0,64},{64,128},{128,192},{192,256},{256,320},{320,384},{384,448},... | collective-permute-start | bytes 1572872 | tf_op jit(solution)/shard_map/ppermute | solution.py:51
  50.4 3.7 %compare_and_fusion = pred[128,8192]{0,1:T(8,128)(4,1)S(1)} fusion(s32[128]{0:T(128)S(1)} %iota_add_fusion, s32[128]{0:T(128)S(1)} %select_reduce_fusion, s32[8192]{0:T(1024)S(1)} %add_bitcast_fusion), kind=kLoop, calls=%fused_computation.11 | loop fusion | flops 3145728 | bytes 1082368 | tf_op jit(solution)/shard_map/and | solution.py:117
  54.2 8.6 %collective-permute-start.1 = (bf16[8,128,256]{2,1,0:T(8,128)(2,1)S(1)}, bf16[8,128,256]{2,1,0:T(8,128)(2,1)}, u32[]{:S(2)}, u32[]{:S(2)}) collective-permute-start(bf16[8,128,256]{2,1,0:T(8,128)(2,1)S(1)} %all-to-all-done.1), channel_id=1, source_target_pairs={{0,448},{64,0},{128,64},{192,128},{256,192},{320,256},{384,320},{4... | collective-permute-start | bytes 1572872 | tf_op jit(solution)/shard_map/ppermute | solution.py:52
  63.8 2.3 %collective-permute-done = bf16[8,128,256]{2,1,0:T(8,128)(2,1)} collective-permute-done((bf16[8,128,256]{2,1,0:T(8,128)(2,1)S(1)}, bf16[8,128,256]{2,1,0:T(8,128)(2,1)}, u32[]{:S(2)}, u32[]{:S(2)}) %collective-permute-start) | collective-permute-done | bytes 524320 | tf_op jit(solution)/shard_map/ppermute | solution.py:51
  66.1 1.9 %collective-permute-start.2 = (bf16[8,128,256]{2,1,0:T(8,128)(2,1)}, bf16[8,128,256]{2,1,0:T(8,128)(2,1)}, u32[]{:S(2)}, u32[]{:S(2)}) collective-permute-start(bf16[8,128,256]{2,1,0:T(8,128)(2,1)} %collective-permute-done), channel_id=1, source_target_pairs={{0,64},{64,128},{128,192},{192,256},{256,320},{320,384},{384,448},... | collective-permute-start | bytes 1572872 | tf_op jit(solution)/shard_map/ppermute | solution.py:51
  68.3 2.6 %collective-permute-done.1 = bf16[8,128,256]{2,1,0:T(8,128)(2,1)} collective-permute-done((bf16[8,128,256]{2,1,0:T(8,128)(2,1)S(1)}, bf16[8,128,256]{2,1,0:T(8,128)(2,1)}, u32[]{:S(2)}, u32[]{:S(2)}) %collective-permute-start.1) | collective-permute-done | bytes 524320 | tf_op jit(solution)/shard_map/ppermute | solution.py:52
  70.9 5.7 %collective-permute-start.3 = (bf16[8,128,256]{2,1,0:T(8,128)(2,1)}, bf16[8,128,256]{2,1,0:T(8,128)(2,1)S(1)}, u32[]{:S(2)}, u32[]{:S(2)}) collective-permute-start(bf16[8,128,256]{2,1,0:T(8,128)(2,1)} %collective-permute-done.1), channel_id=1, source_target_pairs={{0,448},{64,0},{128,64},{192,128},{256,192},{320,256},{384,320},{4... | collective-permute-start | bytes 1572872 | tf_op jit(solution)/shard_map/ppermute | solution.py:52
  76.8 2.9 %collective-permute-done.2 = bf16[8,128,256]{2,1,0:T(8,128)(2,1)} collective-permute-done((bf16[8,128,256]{2,1,0:T(8,128)(2,1)}, bf16[8,128,256]{2,1,0:T(8,128)(2,1)}, u32[]{:S(2)}, u32[]{:S(2)}) %collective-permute-start.2) | collective-permute-done | bytes 524320 | tf_op jit(solution)/shard_map/ppermute | solution.py:51
  79.6 1.9 %collective-permute-start.4 = (bf16[8,128,256]{2,1,0:T(8,128)(2,1)}, bf16[8,128,256]{2,1,0:T(8,128)(2,1)S(1)}, u32[]{:S(2)}, u32[]{:S(2)}) collective-permute-start(bf16[8,128,256]{2,1,0:T(8,128)(2,1)} %collective-permute-done.2), channel_id=1, source_target_pairs={{0,64},{64,128},{128,192},{192,256},{256,320},{320,384},{384,448},... | collective-permute-start | bytes 1572872 | tf_op jit(solution)/shard_map/ppermute | solution.py:51
  81.5 0.9 subtract_convert_fusion
  82.5 1.8 %collective-permute-done.3 = bf16[8,128,256]{2,1,0:T(8,128)(2,1)S(1)} collective-permute-done((bf16[8,128,256]{2,1,0:T(8,128)(2,1)}, bf16[8,128,256]{2,1,0:T(8,128)(2,1)S(1)}, u32[]{:S(2)}, u32[]{:S(2)}) %collective-permute-start.3) | collective-permute-done | bytes 524320 | tf_op jit(solution)/shard_map/ppermute | solution.py:52
  84.3 5.5 %collective-permute-start.5 = (bf16[8,128,256]{2,1,0:T(8,128)(2,1)S(1)}, bf16[8,128,256]{2,1,0:T(8,128)(2,1)S(1)}, u32[]{:S(2)}, u32[]{:S(2)}) collective-permute-start(bf16[8,128,256]{2,1,0:T(8,128)(2,1)S(1)} %collective-permute-done.3), channel_id=1, source_target_pairs={{0,448},{64,0},{128,64},{192,128},{256,192},{320,256},{384,320},{4... | collective-permute-start | bytes 1572872 | tf_op jit(solution)/shard_map/ppermute | solution.py:52
  89.8 1.1 constant_dynamic-update-slice_fusion.7
  90.9 1.1 constant_dynamic-update-slice_fusion.6
  92.0 1.1 constant_dynamic-update-slice_fusion.5
  93.1 1.9 %collective-permute-start.6 = (bf16[4,128,256]{2,1,0:T(8,128)(2,1)S(1)}, bf16[4,128,256]{2,1,0:T(8,128)(2,1)S(1)}, u32[]{:S(2)}, u32[]{:S(2)}) collective-permute-start(bf16[4,128,256]{2,1,0:T(8,128)(2,1)S(1)} %slice.57), channel_id=1, source_target_pairs={{0,64},{64,128},{128,192},{192,256},{256,320},{320,384},{384,448},... | collective-permute-start | bytes 786440 | tf_op jit(solution)/shard_map/ppermute | solution.py:59
  95.1 1.7 %collective-permute-done.5 = bf16[8,128,256]{2,1,0:T(8,128)(2,1)S(1)} collective-permute-done((bf16[8,128,256]{2,1,0:T(8,128)(2,1)S(1)}, bf16[8,128,256]{2,1,0:T(8,128)(2,1)S(1)}, u32[]{:S(2)}, u32[]{:S(2)}) %collective-permute-start.5) | collective-permute-done | bytes 524320 | tf_op jit(solution)/shard_map/ppermute | solution.py:52
  96.8 5.6 %collective-permute-start.7 = (bf16[4,128,256]{2,1,0:T(8,128)(2,1)S(1)}, bf16[4,128,256]{2,1,0:T(8,128)(2,1)S(1)}, u32[]{:S(2)}, u32[]{:S(2)}) collective-permute-start(bf16[4,128,256]{2,1,0:T(8,128)(2,1)S(1)} %slice.58), channel_id=1, source_target_pairs={{0,448},{64,0},{128,64},{192,128},{256,192},{320,256},{384,320},{4... | collective-permute-start | bytes 786440 | tf_op jit(solution)/shard_map/ppermute | solution.py:59
  102.6 3.6 %collective-permute-done.7 = bf16[4,128,256]{2,1,0:T(8,128)(2,1)S(1)} collective-permute-done((bf16[4,128,256]{2,1,0:T(8,128)(2,1)S(1)}, bf16[4,128,256]{2,1,0:T(8,128)(2,1)S(1)}, u32[]{:S(2)}, u32[]{:S(2)}) %collective-permute-start.7) | collective-permute-done | bytes 262176 | tf_op jit(solution)/shard_map/ppermute | solution.py:59
  106.3 1.9 %fusion.38 = (f32[2,128]{1,0:T(2,128)S(1)}, f32[1,2,128,8192]{2,3,1,0:T(8,128)S(1)}) fusion(bf16[128,2,64]{2,0,1:T(8,128)(2,1)S(1)} %get-tuple-element.4, bf16[128,2,64]{2,0,1:T(8,128)(2,1)S(1)} %get-tuple-element.3, bf16[8192,256]{1,0:T(8,128)(2,1)S(1)} %bitcast.62, pred[128,8192]{0,1:T(8,128)(4,1)S(1)} %compare_and_fusion), kind=kOutput, calls=%fused_computation.86 | convolution fusion | flops 543293184 | bytes 11666432 | tf_op jit(solution)/shard_map/qhgd,khd->hgqk/dot_general | solution.py:114
  108.1 1.7 %fusion.2 = f32[2,128]{1,0:T(2,128)S(1)} fusion(f32[1,2,128,8192]{2,3,1,0:T(8,128)S(1)} %get-tuple-element.12, f32[2,128]{1,0:T(2,128)S(1)} %get-tuple-element.11, pred[128,8192]{0,1:T(8,128)(4,1)S(1)} %compare_and_fusion), kind=kLoop, calls=%fused_computation.4 | loop fusion | flops 6291200 | bytes 9439232 | tf_op jit(solution)/shard_map/reduce_sum | solution.py:121
  109.8 1.8 %fusion.16 = bf16[2,128,128]{1,2,0:T(8,128)(2,1)S(1)} fusion(bf16[8192,256]{1,0:T(8,128)(2,1)S(1)} %bitcast.63, f32[1,2,128,8192]{2,3,1,0:T(8,128)S(1)} %get-tuple-element.12, f32[2,128]{1,0:T(2,128)S(1)} %get-tuple-element.11, pred[128,8192]{0,1:T(8,128)(4,1)S(1)} %compare_and_fusion, f32[2,128]{1,0:T(2,128)S(1)} %fusion.2), kind=kOutput, calls=%fused_computation.23 | convolution fusion | flops 543227904 | bytes 11601920 | tf_op jit(solution)/shard_map/hgqk,khd->hgqd/dot_general | solution.py:122
  112.0 4.3 %all_to_all.20 = bf16[2,4,16,2560]{3,2,1,0:T(8,128)(2,1)S(1)} all-to-all(bf16[2,4,16,2560]{3,2,1,0:T(8,128)(2,1)S(1)} %bitcast.60), channel_id=1, replica_groups=mesh['z'=8,'x'=4,'ylo'=2,'yhi'=4,'core'=2] {'core'}, dimensions={0} | all-to-all | bytes 1310720 | tf_op jit(solution)/shard_map/all_to_all | solution.py:135
  117.2 7.8 %all-to-all-start.3 = ((bf16[4,16,2560]{2,1,0:T(8,128)(2,1)}), bf16[4,16,2560]{2,1,0:T(8,128)(2,1)S(1)}, u32[]{:S(2)}, u32[]{:S(2)}) async-start(bf16[4,16,2560]{2,1,0:T(8,128)(2,1)} %reduce_sum.84), calls=%async_computation.3 | async-start | bytes 655360 | tf_op jit(solution)/shard_map/all_to_all | solution.py:137
  125.7 11.3 %all-to-all-done.3 = bf16[4,16,2560]{2,1,0:T(8,128)(2,1)S(1)} async-done(((bf16[4,16,2560]{2,1,0:T(8,128)(2,1)}), bf16[4,16,2560]{2,1,0:T(8,128)(2,1)S(1)}, u32[]{:S(2)}, u32[]{:S(2)}) %all-to-all-start.3) | async-done | bytes 327712 | tf_op jit(solution)/shard_map/all_to_all | solution.py:137
  (59 shorter events, 9.2 us)
Async XLA Ops:
  0.6 111.0 %copy-start = (bf16[256,2560]{1,0:T(8,128)(2,1)S(1)}, bf16[256,2560]{1,0:T(8,128)(2,1)}, u32[]{:S(2)}) copy-start(bf16[256,2560]{1,0:T(8,128)(2,1)} %param.14) | copy-start | bytes 3932164
  2.6 27.6 %all-to-all-start = ((bf16[8,128,320]{1,2,0:T(8,128)(2,1)}), bf16[8,128,320]{1,2,0:T(8,128)(2,1)S(1)}, u32[]{:S(2)}, u32[]{:S(2)}) async-start(bf16[8,128,320]{1,2,0:T(8,128)(2,1)} %broadcast_in_dim.33), calls=%async_computation | async-start | bytes 1310720 | tf_op jit(solution)/shard_map/all_to_all | solution.py:77
  12.2 21.3 %copy-start.2 = (f32[128]{0:T(128)S(1)}, f32[128]{0:T(128)}, u32[]{:S(2)}) copy-start(f32[128]{0:T(128)} %param.16) | copy-start | bytes 1540
  30.5 46.2 %copy-start.3 = (f32[128]{0:T(128)S(1)}, f32[128]{0:T(128)}, u32[]{:S(2)}) copy-start(f32[128]{0:T(128)} %param.15) | copy-start | bytes 1540
  33.5 0.6 copy-start.1
  35.1 11.8 %all-to-all-start.1 = ((bf16[8,128,256]{2,1,0:T(8,128)(2,1)}), bf16[8,128,256]{2,1,0:T(8,128)(2,1)S(1)}, u32[]{:S(2)}, u32[]{:S(2)}) async-start(bf16[8,128,256]{2,1,0:T(8,128)(2,1)} %broadcast_in_dim.34), calls=%async_computation.1 | async-start | bytes 1048576 | tf_op jit(solution)/shard_map/all_to_all | solution.py:103
  46.9 19.3 %collective-permute-start = (bf16[8,128,256]{2,1,0:T(8,128)(2,1)S(1)}, bf16[8,128,256]{2,1,0:T(8,128)(2,1)}, u32[]{:S(2)}, u32[]{:S(2)}) collective-permute-start(bf16[8,128,256]{2,1,0:T(8,128)(2,1)S(1)} %all-to-all-done.1), channel_id=1, source_target_pairs={{0,64},{64,128},{128,192},{192,256},{256,320},{320,384},{384,448},... | collective-permute-start | bytes 1572872 | tf_op jit(solution)/shard_map/ppermute | solution.py:51
  54.2 16.8 %collective-permute-start.1 = (bf16[8,128,256]{2,1,0:T(8,128)(2,1)S(1)}, bf16[8,128,256]{2,1,0:T(8,128)(2,1)}, u32[]{:S(2)}, u32[]{:S(2)}) collective-permute-start(bf16[8,128,256]{2,1,0:T(8,128)(2,1)S(1)} %all-to-all-done.1), channel_id=1, source_target_pairs={{0,448},{64,0},{128,64},{192,128},{256,192},{320,256},{384,320},{4... | collective-permute-start | bytes 1572872 | tf_op jit(solution)/shard_map/ppermute | solution.py:52
  66.1 13.5 %collective-permute-start.2 = (bf16[8,128,256]{2,1,0:T(8,128)(2,1)}, bf16[8,128,256]{2,1,0:T(8,128)(2,1)}, u32[]{:S(2)}, u32[]{:S(2)}) collective-permute-start(bf16[8,128,256]{2,1,0:T(8,128)(2,1)} %collective-permute-done), channel_id=1, source_target_pairs={{0,64},{64,128},{128,192},{192,256},{256,320},{320,384},{384,448},... | collective-permute-start | bytes 1572872 | tf_op jit(solution)/shard_map/ppermute | solution.py:51
  70.9 13.3 %collective-permute-start.3 = (bf16[8,128,256]{2,1,0:T(8,128)(2,1)}, bf16[8,128,256]{2,1,0:T(8,128)(2,1)S(1)}, u32[]{:S(2)}, u32[]{:S(2)}) collective-permute-start(bf16[8,128,256]{2,1,0:T(8,128)(2,1)} %collective-permute-done.1), channel_id=1, source_target_pairs={{0,448},{64,0},{128,64},{192,128},{256,192},{320,256},{384,320},{4... | collective-permute-start | bytes 1572872 | tf_op jit(solution)/shard_map/ppermute | solution.py:52
  79.6 13.4 %collective-permute-start.4 = (bf16[8,128,256]{2,1,0:T(8,128)(2,1)}, bf16[8,128,256]{2,1,0:T(8,128)(2,1)S(1)}, u32[]{:S(2)}, u32[]{:S(2)}) collective-permute-start(bf16[8,128,256]{2,1,0:T(8,128)(2,1)} %collective-permute-done.2), channel_id=1, source_target_pairs={{0,64},{64,128},{128,192},{192,256},{256,320},{320,384},{384,448},... | collective-permute-start | bytes 1572872 | tf_op jit(solution)/shard_map/ppermute | solution.py:51
  84.3 12.5 %collective-permute-start.5 = (bf16[8,128,256]{2,1,0:T(8,128)(2,1)S(1)}, bf16[8,128,256]{2,1,0:T(8,128)(2,1)S(1)}, u32[]{:S(2)}, u32[]{:S(2)}) collective-permute-start(bf16[8,128,256]{2,1,0:T(8,128)(2,1)S(1)} %collective-permute-done.3), channel_id=1, source_target_pairs={{0,448},{64,0},{128,64},{192,128},{256,192},{320,256},{384,320},{4... | collective-permute-start | bytes 1572872 | tf_op jit(solution)/shard_map/ppermute | solution.py:52
  93.1 9.5 %collective-permute-start.6 = (bf16[4,128,256]{2,1,0:T(8,128)(2,1)S(1)}, bf16[4,128,256]{2,1,0:T(8,128)(2,1)S(1)}, u32[]{:S(2)}, u32[]{:S(2)}) collective-permute-start(bf16[4,128,256]{2,1,0:T(8,128)(2,1)S(1)} %slice.57), channel_id=1, source_target_pairs={{0,64},{64,128},{128,192},{192,256},{256,320},{320,384},{384,448},... | collective-permute-start | bytes 786440 | tf_op jit(solution)/shard_map/ppermute | solution.py:59
  96.8 9.5 %collective-permute-start.7 = (bf16[4,128,256]{2,1,0:T(8,128)(2,1)S(1)}, bf16[4,128,256]{2,1,0:T(8,128)(2,1)S(1)}, u32[]{:S(2)}, u32[]{:S(2)}) collective-permute-start(bf16[4,128,256]{2,1,0:T(8,128)(2,1)S(1)} %slice.58), channel_id=1, source_target_pairs={{0,448},{64,0},{128,64},{192,128},{256,192},{320,256},{384,320},{4... | collective-permute-start | bytes 786440 | tf_op jit(solution)/shard_map/ppermute | solution.py:59
  117.2 19.9 %all-to-all-start.3 = ((bf16[4,16,2560]{2,1,0:T(8,128)(2,1)}), bf16[4,16,2560]{2,1,0:T(8,128)(2,1)S(1)}, u32[]{:S(2)}, u32[]{:S(2)}) async-start(bf16[4,16,2560]{2,1,0:T(8,128)(2,1)} %reduce_sum.84), calls=%async_computation.3 | async-start | bytes 655360 | tf_op jit(solution)/shard_map/all_to_all | solution.py:137

commit v8 on v5

--- a/solution.py
+++ b/solution.py
@@ -124,13 +124,9 @@
     attn = summed / denom[..., None]
     attn = jnp.transpose(attn, (2, 0, 1, 3)).reshape(tokens, q_cols).astype(jnp.bfloat16)
     part = jnp.dot(attn, w_out, preferred_element_type=jnp.float32).astype(jnp.bfloat16)
-    nyhi = lax.axis_size("yhi")
-    ncore = lax.axis_size("core")
-    chunk = tokens // (nyhi * ncore)
-    part = part.reshape(nyhi, ncore, chunk, -1).transpose(1, 0, 2, 3)
-    part = lax.all_to_all(part, "core", 0, 0, tiled=True)
-    part = jnp.sum(part.astype(jnp.float32), axis=0).astype(jnp.bfloat16)
-    part = lax.all_to_all(part, "yhi", 0, 0, tiled=True)
+    nten = lax.axis_size(TEN)
+    part = part.reshape(nten, tokens // nten, -1)
+    part = lax.all_to_all(part, TEN, 0, 0, tiled=True)
     mixed = jnp.sum(part.astype(jnp.float32), axis=0).astype(jnp.bfloat16)
     return (mixed, key_flat, value_flat)
 

time: 135 us -> 138 us (1.022)
  waiting for transfers between devices: 39.6 us -> 48.1 us
  blocking collectives: 22.6 us -> 18.4 us
    all_to_all x1, waiting for transfers between devices: 12 us -> 20.4 us  [on_device(): part = lax.all_to_all(part, TEN, 0, 0, tiled=True)]
    all_to_all x1 -> x0, blocking collectives: 4.26 us -> none  [on_device(): part = lax.all_to_all(part, 'core', 0, 0, tiled=True)]
where the time goes in v8:
time: 138 us
  waiting for transfers between devices  48.1 us (35%)
  starting transfers between devices  44.9 us (33%)
  blocking collectives  18.4 us (13%)
  other arithmetic  12.1 us (9%)
  matrix products  7.95 us (6%)
  local copies, waits for them, and re-layouts  5.1 us (4%)
    all_to_all x1, waiting for transfers between devices, on_device(): part = lax.all_to_all(part, TEN, 0, 0, tiled=True)  20.4 us
    ppermute x3, starting transfers between devices, ring_gather(): b = lax.ppermute(b, name, ccw)  20.1 us
    all_gather x1, blocking collectives, on_device(): piece = lax.all_gather(hidden_in, TEN, axis=1, tiled=True)  18.4 us
    ppermute x3, waiting for transfers between devices, ring_gather(): a = lax.ppermute(a, name, cw)  11.3 us
    all_to_all x1, waiting for transfers between devices, on_device(): lax.all_to_all(jnp.broadcast_to(piece, (plane,) + piece.shape[1:]), ('x',...  8.13 us
    all_to_all x1, starting transfers between devices, on_device(): lax.all_to_all(jnp.broadcast_to(piece, (plane,) + piece.shape[1:]), ('x',...  6.41 us
    ppermute x3, starting transfers between devices, ring_gather(): a = lax.ppermute(a, name, cw)  6.18 us
    ppermute x1, starting transfers between devices, ring_gather(): lax.ppermute(b[m // 2:], name, ccw)  5.6 us
  transfers between devices with their start and end apart: 10, of which 9 were waited for; matrix products, arithmetic and copies ran while one was open for 9% of the time, Pallas kernels for 0%

profile of v8, /device:TPU:6, one launch (start us, length us, event | category | flops | bytes accessed | tf_op | source)
XLA Modules:
  0.0 137.6 jit_solution(3737718809739192556)
XLA Ops:
  0.7 18.4 %all_gather.3 = bf16[128,2560]{0,1:T(8,128)(2,1)S(1)} all-gather(bf16[128,320]{0,1:T(8,128)(2,1)} %param.9), channel_id=1, replica_groups=mesh['z'=8,'x'=4,'ylo'=2,'yhi'=4,'core'=2] {'yhi','core'}, dimensions={1}, use_global_device_ids=true | all-gather | bytes 737280 | tf_op jit(solution)/shard_map/all_gather | solution.py:76
  19.4 3.1 %fusion.18 = f32[128,512]{1,0:T(8,128)S(1)} fusion(bf16[2560,128]{1,0:T(8,128)(2,1)} %param.13, bf16[2560,128]{1,0:T(8,128)(2,1)} %param.12, bf16[2560,256]{1,0:T(8,128)(2,1)} %param.11, bf16[128,2560]{0,1:T(8,128)(2,1)S(1)} %all_gather.3, f32[2560]{0:T(1024)} %param.10, f32[128]{0:T(128)S(1)} %add_rsqrt_fusion.2), kind=kOutput, calls=%fused_computation.25 | convolution fusion | flops 344457216 | bytes 3549696 | tf_op jit(solution)/shard_map/dot_general | solution.py:79
  23.6 0.8 broadcast_in_dim.31
  24.5 6.4 %all-to-all-start = ((bf16[8,128,256]{2,1,0:T(8,128)(2,1)}), bf16[8,128,256]{2,1,0:T(8,128)(2,1)S(1)}, u32[]{:S(2)}, u32[]{:S(2)}) async-start(bf16[8,128,256]{2,1,0:T(8,128)(2,1)} %broadcast_in_dim.31), calls=%async_computation | async-start | bytes 1048576 | tf_op jit(solution)/shard_map/all_to_all | solution.py:99
  31.2 8.1 %all-to-all-done = bf16[8,128,256]{2,1,0:T(8,128)(2,1)S(1)} async-done(((bf16[8,128,256]{2,1,0:T(8,128)(2,1)}), bf16[8,128,256]{2,1,0:T(8,128)(2,1)S(1)}, u32[]{:S(2)}, u32[]{:S(2)}) %all-to-all-start) | async-done | bytes 524320 | tf_op jit(solution)/shard_map/all_to_all | solution.py:99
  39.4 2.4 %collective-permute-start = (bf16[8,128,256]{2,1,0:T(8,128)(2,1)S(1)}, bf16[8,128,256]{2,1,0:T(8,128)(2,1)}, u32[]{:S(2)}, u32[]{:S(2)}) collective-permute-start(bf16[8,128,256]{2,1,0:T(8,128)(2,1)S(1)} %all-to-all-done), channel_id=1, source_target_pairs={{0,64},{64,128},{128,192},{192,256},{256,320},{320,384},{384,448},... | collective-permute-start | bytes 1572872 | tf_op jit(solution)/shard_map/ppermute | solution.py:51
  41.7 3.7 %compare_and_fusion = pred[128,8192]{0,1:T(8,128)(4,1)S(1)} fusion(s32[128]{0:T(128)S(1)} %iota_add_fusion, s32[128]{0:T(128)S(1)} %select_reduce_fusion, s32[8192]{0:T(1024)S(1)} %add_bitcast_fusion), kind=kLoop, calls=%fused_computation.11 | loop fusion | flops 3145728 | bytes 1082368 | tf_op jit(solution)/shard_map/and | solution.py:113
  45.5 8.9 %collective-permute-start.1 = (bf16[8,128,256]{2,1,0:T(8,128)(2,1)S(1)}, bf16[8,128,256]{2,1,0:T(8,128)(2,1)}, u32[]{:S(2)}, u32[]{:S(2)}) collective-permute-start(bf16[8,128,256]{2,1,0:T(8,128)(2,1)S(1)} %all-to-all-done), channel_id=1, source_target_pairs={{0,448},{64,0},{128,64},{192,128},{256,192},{320,256},{384,320},{4... | collective-permute-start | bytes 1572872 | tf_op jit(solution)/shard_map/ppermute | solution.py:52
  55.2 1.0 multiply_cosine_fusion
  56.1 4.0 %collective-permute-done = bf16[8,128,256]{2,1,0:T(8,128)(2,1)} collective-permute-done((bf16[8,128,256]{2,1,0:T(8,128)(2,1)S(1)}, bf16[8,128,256]{2,1,0:T(8,128)(2,1)}, u32[]{:S(2)}, u32[]{:S(2)}) %collective-permute-start) | collective-permute-done | bytes 524320 | tf_op jit(solution)/shard_map/ppermute | solution.py:51
  60.1 1.9 %collective-permute-start.2 = (bf16[8,128,256]{2,1,0:T(8,128)(2,1)}, bf16[8,128,256]{2,1,0:T(8,128)(2,1)S(1)}, u32[]{:S(2)}, u32[]{:S(2)}) collective-permute-start(bf16[8,128,256]{2,1,0:T(8,128)(2,1)} %collective-permute-done), channel_id=1, source_target_pairs={{0,64},{64,128},{128,192},{192,256},{256,320},{320,384},{384,448},... | collective-permute-start | bytes 1572872 | tf_op jit(solution)/shard_map/ppermute | solution.py:51
  62.1 1.7 %multiply_reduce_fusion = f32[128,2]{1,0:T(8,128)} fusion(f32[128,2,128]{2,1,0:T(2,128)} %reshape.365), kind=kLoop, calls=%fused_computation.33 | loop fusion | flops 65280 | bytes 132096 | tf_op jit(solution)/shard_map/reduce_sum | solution.py:30
  63.8 0.9 copy.31
  65.0 5.7 %collective-permute-start.3 = (bf16[8,128,256]{2,1,0:T(8,128)(2,1)}, bf16[8,128,256]{2,1,0:T(8,128)(2,1)S(1)}, u32[]{:S(2)}, u32[]{:S(2)}) collective-permute-start(bf16[8,128,256]{2,1,0:T(8,128)(2,1)} %collective-permute-done.1), channel_id=1, source_target_pairs={{0,448},{64,0},{128,64},{192,128},{256,192},{320,256},{384,320},{4... | collective-permute-start | bytes 1572872 | tf_op jit(solution)/shard_map/ppermute | solution.py:52
  70.8 5.1 %collective-permute-done.2 = bf16[8,128,256]{2,1,0:T(8,128)(2,1)S(1)} collective-permute-done((bf16[8,128,256]{2,1,0:T(8,128)(2,1)}, bf16[8,128,256]{2,1,0:T(8,128)(2,1)S(1)}, u32[]{:S(2)}, u32[]{:S(2)}) %collective-permute-start.2) | collective-permute-done | bytes 524320 | tf_op jit(solution)/shard_map/ppermute | solution.py:51
  75.9 1.9 %collective-permute-start.4 = (bf16[8,128,256]{2,1,0:T(8,128)(2,1)S(1)}, bf16[8,128,256]{2,1,0:T(8,128)(2,1)S(1)}, u32[]{:S(2)}, u32[]{:S(2)}) collective-permute-start(bf16[8,128,256]{2,1,0:T(8,128)(2,1)S(1)} %collective-permute-done.2), channel_id=1, source_target_pairs={{0,64},{64,128},{128,192},{192,256},{256,320},{320,384},{384,448},... | collective-permute-start | bytes 1572872 | tf_op jit(solution)/shard_map/ppermute | solution.py:51
  77.8 1.0 subtract_convert_fusion
  78.8 1.8 %collective-permute-done.3 = bf16[8,128,256]{2,1,0:T(8,128)(2,1)S(1)} collective-permute-done((bf16[8,128,256]{2,1,0:T(8,128)(2,1)}, bf16[8,128,256]{2,1,0:T(8,128)(2,1)S(1)}, u32[]{:S(2)}, u32[]{:S(2)}) %collective-permute-start.3) | collective-permute-done | bytes 524320 | tf_op jit(solution)/shard_map/ppermute | solution.py:52
  80.6 5.5 %collective-permute-start.5 = (bf16[8,128,256]{2,1,0:T(8,128)(2,1)S(1)}, bf16[8,128,256]{2,1,0:T(8,128)(2,1)S(1)}, u32[]{:S(2)}, u32[]{:S(2)}) collective-permute-start(bf16[8,128,256]{2,1,0:T(8,128)(2,1)S(1)} %collective-permute-done.3), channel_id=1, source_target_pairs={{0,448},{64,0},{128,64},{192,128},{256,192},{320,256},{384,320},{4... | collective-permute-start | bytes 1572872 | tf_op jit(solution)/shard_map/ppermute | solution.py:52
  86.2 1.1 constant_dynamic-update-slice_fusion.7
  87.3 1.1 constant_dynamic-update-slice_fusion.6
  88.4 2.2 %collective-permute-done.4 = bf16[8,128,256]{2,1,0:T(8,128)(2,1)S(1)} collective-permute-done((bf16[8,128,256]{2,1,0:T(8,128)(2,1)S(1)}, bf16[8,128,256]{2,1,0:T(8,128)(2,1)S(1)}, u32[]{:S(2)}, u32[]{:S(2)}) %collective-permute-start.4) | collective-permute-done | bytes 524320 | tf_op jit(solution)/shard_map/ppermute | solution.py:51
  90.6 1.9 %collective-permute-start.6 = (bf16[4,128,256]{2,1,0:T(8,128)(2,1)S(1)}, bf16[4,128,256]{2,1,0:T(8,128)(2,1)S(1)}, u32[]{:S(2)}, u32[]{:S(2)}) collective-permute-start(bf16[4,128,256]{2,1,0:T(8,128)(2,1)S(1)} %slice.57), channel_id=1, source_target_pairs={{0,64},{64,128},{128,192},{192,256},{256,320},{320,384},{384,448},... | collective-permute-start | bytes 786440 | tf_op jit(solution)/shard_map/ppermute | solution.py:59
  92.6 2.4 %collective-permute-done.5 = bf16[8,128,256]{2,1,0:T(8,128)(2,1)S(1)} collective-permute-done((bf16[8,128,256]{2,1,0:T(8,128)(2,1)S(1)}, bf16[8,128,256]{2,1,0:T(8,128)(2,1)S(1)}, u32[]{:S(2)}, u32[]{:S(2)}) %collective-permute-start.5) | collective-permute-done | bytes 524320 | tf_op jit(solution)/shard_map/ppermute | solution.py:52
  95.0 5.6 %collective-permute-start.7 = (bf16[4,128,256]{2,1,0:T(8,128)(2,1)S(1)}, bf16[4,128,256]{2,1,0:T(8,128)(2,1)S(1)}, u32[]{:S(2)}, u32[]{:S(2)}) collective-permute-start(bf16[4,128,256]{2,1,0:T(8,128)(2,1)S(1)} %slice.58), channel_id=1, source_target_pairs={{0,448},{64,0},{128,64},{192,128},{256,192},{320,256},{384,320},{4... | collective-permute-start | bytes 786440 | tf_op jit(solution)/shard_map/ppermute | solution.py:59
  100.7 3.7 %collective-permute-done.7 = bf16[4,128,256]{2,1,0:T(8,128)(2,1)S(1)} collective-permute-done((bf16[4,128,256]{2,1,0:T(8,128)(2,1)S(1)}, bf16[4,128,256]{2,1,0:T(8,128)(2,1)S(1)}, u32[]{:S(2)}, u32[]{:S(2)}) %collective-permute-start.7) | collective-permute-done | bytes 262176 | tf_op jit(solution)/shard_map/ppermute | solution.py:59
  104.5 1.9 %fusion.47 = (f32[2,128]{1,0:T(2,128)S(1)}, f32[1,2,128,8192]{2,3,1,0:T(8,128)S(1)}) fusion(bf16[128,2,64]{2,0,1:T(8,128)(2,1)S(1)} %get-tuple-element.4, bf16[128,2,64]{2,0,1:T(8,128)(2,1)S(1)} %get-tuple-element.3, bf16[8192,256]{1,0:T(8,128)(2,1)S(1)} %bitcast.50, pred[128,8192]{0,1:T(8,128)(4,1)S(1)} %compare_and_fusion), kind=kOutput, calls=%fused_computation.90 | convolution fusion | flops 543293184 | bytes 11666432 | tf_op jit(solution)/shard_map/qhgd,khd->hgqk/dot_general | solution.py:110
  106.4 1.7 %fusion.2 = f32[2,128]{1,0:T(2,128)S(1)} fusion(f32[1,2,128,8192]{2,3,1,0:T(8,128)S(1)} %get-tuple-element.12, f32[2,128]{1,0:T(2,128)S(1)} %get-tuple-element.11, pred[128,8192]{0,1:T(8,128)(4,1)S(1)} %compare_and_fusion), kind=kLoop, calls=%fused_computation.4 | loop fusion | flops 6291200 | bytes 9439232 | tf_op jit(solution)/shard_map/reduce_sum | solution.py:117
  108.1 1.8 %fusion.24 = bf16[2,128,128]{1,2,0:T(8,128)(2,1)S(1)} fusion(bf16[8192,256]{1,0:T(8,128)(2,1)S(1)} %bitcast.51, f32[1,2,128,8192]{2,3,1,0:T(8,128)S(1)} %get-tuple-element.12, f32[2,128]{1,0:T(2,128)S(1)} %get-tuple-element.11, pred[128,8192]{0,1:T(8,128)(4,1)S(1)} %compare_and_fusion, f32[2,128]{1,0:T(2,128)S(1)} %fusion.2), kind=kOutput, calls=%fused_computation.27 | convolution fusion | flops 543227904 | bytes 11601920 | tf_op jit(solution)/shard_map/hgqk,khd->hgqd/dot_general | solution.py:118
  109.9 1.2 convolution_convert_fusion
  111.1 4.7 %all-to-all-start.1 = ((bf16[8,16,2560]{2,1,0:T(8,128)(2,1)}), bf16[8,16,2560]{2,1,0:T(8,128)(2,1)S(1)}, u32[]{:S(2)}, u32[]{:S(2)}) async-start(bf16[8,16,2560]{2,1,0:T(8,128)(2,1)} %bitcast.14), calls=%async_computation.1 | async-start | bytes 1310720 | tf_op jit(solution)/shard_map/all_to_all | solution.py:129
  116.5 20.4 %all-to-all-done.1 = bf16[8,16,2560]{2,1,0:T(8,128)(2,1)S(1)} async-done(((bf16[8,16,2560]{2,1,0:T(8,128)(2,1)}), bf16[8,16,2560]{2,1,0:T(8,128)(2,1)S(1)}, u32[]{:S(2)}, u32[]{:S(2)}) %all-to-all-start.1) | async-done | bytes 655392 | tf_op jit(solution)/shard_map/all_to_all | solution.py:129
  (62 shorter events, 4.5 us)
Async XLA Ops:
  0.6 109.2 %copy-start = (bf16[256,2560]{1,0:T(8,128)(2,1)S(1)}, bf16[256,2560]{1,0:T(8,128)(2,1)}, u32[]{:S(2)}) copy-start(bf16[256,2560]{1,0:T(8,128)(2,1)} %param.14) | copy-start | bytes 3932164
  19.0 3.6 %copy-start.8 = (s32[16]{0:T(128)S(1)}, s32[16]{0:T(128)}, u32[]{:S(2)}) copy-start(s32[16]{0:T(128)} %param.17) | copy-start | bytes 196
  19.0 4.1 %copy-start.6 = (f32[128]{0:T(128)S(1)}, f32[128]{0:T(128)}, u32[]{:S(2)}) copy-start(f32[128]{0:T(128)} %param.16) | copy-start | bytes 1540
  22.5 48.2 %copy-start.7 = (f32[128]{0:T(128)S(1)}, f32[128]{0:T(128)}, u32[]{:S(2)}) copy-start(f32[128]{0:T(128)} %param.15) | copy-start | bytes 1540
  22.6 1.8 %copy-start.5 = (bf16[128,128]{1,0:T(8,128)(2,1)}, bf16[128,128]{1,0:T(8,128)(2,1)S(1)}, u32[]{:S(2)}) copy-start(bf16[128,128]{1,0:T(8,128)(2,1)S(1)} %slice.94) | copy-start | bytes 98308
  23.5 0.9 copy-start.1
  23.5 0.9 copy-start.3
  24.5 14.9 %all-to-all-start = ((bf16[8,128,256]{2,1,0:T(8,128)(2,1)}), bf16[8,128,256]{2,1,0:T(8,128)(2,1)S(1)}, u32[]{:S(2)}, u32[]{:S(2)}) async-start(bf16[8,128,256]{2,1,0:T(8,128)(2,1)} %broadcast_in_dim.31), calls=%async_computation | async-start | bytes 1048576 | tf_op jit(solution)/shard_map/all_to_all | solution.py:99
  39.4 20.8 %collective-permute-start = (bf16[8,128,256]{2,1,0:T(8,128)(2,1)S(1)}, bf16[8,128,256]{2,1,0:T(8,128)(2,1)}, u32[]{:S(2)}, u32[]{:S(2)}) collective-permute-start(bf16[8,128,256]{2,1,0:T(8,128)(2,1)S(1)} %all-to-all-done), channel_id=1, source_target_pairs={{0,64},{64,128},{128,192},{192,256},{256,320},{320,384},{384,448},... | collective-permute-start | bytes 1572872 | tf_op jit(solution)/shard_map/ppermute | solution.py:51
  45.5 19.5 %collective-permute-start.1 = (bf16[8,128,256]{2,1,0:T(8,128)(2,1)S(1)}, bf16[8,128,256]{2,1,0:T(8,128)(2,1)}, u32[]{:S(2)}, u32[]{:S(2)}) collective-permute-start(bf16[8,128,256]{2,1,0:T(8,128)(2,1)S(1)} %all-to-all-done), channel_id=1, source_target_pairs={{0,448},{64,0},{128,64},{192,128},{256,192},{320,256},{384,320},{4... | collective-permute-start | bytes 1572872 | tf_op jit(solution)/shard_map/ppermute | solution.py:52
  60.1 15.8 %collective-permute-start.2 = (bf16[8,128,256]{2,1,0:T(8,128)(2,1)}, bf16[8,128,256]{2,1,0:T(8,128)(2,1)S(1)}, u32[]{:S(2)}, u32[]{:S(2)}) collective-permute-start(bf16[8,128,256]{2,1,0:T(8,128)(2,1)} %collective-permute-done), channel_id=1, source_target_pairs={{0,64},{64,128},{128,192},{192,256},{256,320},{320,384},{384,448},... | collective-permute-start | bytes 1572872 | tf_op jit(solution)/shard_map/ppermute | solution.py:51
  65.0 15.7 %collective-permute-start.3 = (bf16[8,128,256]{2,1,0:T(8,128)(2,1)}, bf16[8,128,256]{2,1,0:T(8,128)(2,1)S(1)}, u32[]{:S(2)}, u32[]{:S(2)}) collective-permute-start(bf16[8,128,256]{2,1,0:T(8,128)(2,1)} %collective-permute-done.1), channel_id=1, source_target_pairs={{0,448},{64,0},{128,64},{192,128},{256,192},{320,256},{384,320},{4... | collective-permute-start | bytes 1572872 | tf_op jit(solution)/shard_map/ppermute | solution.py:52
  75.9 14.7 %collective-permute-start.4 = (bf16[8,128,256]{2,1,0:T(8,128)(2,1)S(1)}, bf16[8,128,256]{2,1,0:T(8,128)(2,1)S(1)}, u32[]{:S(2)}, u32[]{:S(2)}) collective-permute-start(bf16[8,128,256]{2,1,0:T(8,128)(2,1)S(1)} %collective-permute-done.2), channel_id=1, source_target_pairs={{0,64},{64,128},{128,192},{192,256},{256,320},{320,384},{384,448},... | collective-permute-start | bytes 1572872 | tf_op jit(solution)/shard_map/ppermute | solution.py:51
  80.6 14.3 %collective-permute-start.5 = (bf16[8,128,256]{2,1,0:T(8,128)(2,1)S(1)}, bf16[8,128,256]{2,1,0:T(8,128)(2,1)S(1)}, u32[]{:S(2)}, u32[]{:S(2)}) collective-permute-start(bf16[8,128,256]{2,1,0:T(8,128)(2,1)S(1)} %collective-permute-done.3), channel_id=1, source_target_pairs={{0,448},{64,0},{128,64},{192,128},{256,192},{320,256},{384,320},{4... | collective-permute-start | bytes 1572872 | tf_op jit(solution)/shard_map/ppermute | solution.py:52
  90.6 10.1 %collective-permute-start.6 = (bf16[4,128,256]{2,1,0:T(8,128)(2,1)S(1)}, bf16[4,128,256]{2,1,0:T(8,128)(2,1)S(1)}, u32[]{:S(2)}, u32[]{:S(2)}) collective-permute-start(bf16[4,128,256]{2,1,0:T(8,128)(2,1)S(1)} %slice.57), channel_id=1, source_target_pairs={{0,64},{64,128},{128,192},{192,256},{256,320},{320,384},{384,448},... | collective-permute-start | bytes 786440 | tf_op jit(solution)/shard_map/ppermute | solution.py:59
  95.0 9.5 %collective-permute-start.7 = (bf16[4,128,256]{2,1,0:T(8,128)(2,1)S(1)}, bf16[4,128,256]{2,1,0:T(8,128)(2,1)S(1)}, u32[]{:S(2)}, u32[]{:S(2)}) collective-permute-start(bf16[4,128,256]{2,1,0:T(8,128)(2,1)S(1)} %slice.58), channel_id=1, source_target_pairs={{0,448},{64,0},{128,64},{192,128},{256,192},{320,256},{384,320},{4... | collective-permute-start | bytes 786440 | tf_op jit(solution)/shard_map/ppermute | solution.py:59
  108.0 7.7 %copy-start.2 = (bf16[128,64]{1,0:T(8,128)(2,1)S(1)}, bf16[128,64]{1,0:T(8,128)(2,1)}, u32[]{:S(2)}) copy-start(bf16[128,64]{1,0:T(8,128)(2,1)} %copy-done.1) | copy-start | bytes 49156
  108.1 7.7 %copy-start.4 = (bf16[128,64]{1,0:T(8,128)(2,1)S(1)}, bf16[128,64]{1,0:T(8,128)(2,1)}, u32[]{:S(2)}) copy-start(bf16[128,64]{1,0:T(8,128)(2,1)} %copy-done.3) | copy-start | bytes 49156
  111.1 25.8 %all-to-all-start.1 = ((bf16[8,16,2560]{2,1,0:T(8,128)(2,1)}), bf16[8,16,2560]{2,1,0:T(8,128)(2,1)S(1)}, u32[]{:S(2)}, u32[]{:S(2)}) async-start(bf16[8,16,2560]{2,1,0:T(8,128)(2,1)} %bitcast.14), calls=%async_computation.1 | async-start | bytes 1310720 | tf_op jit(solution)/shard_map/all_to_all | solution.py:129

commit v9 on v5

--- a/solution.py
+++ b/solution.py
@@ -73,7 +73,9 @@
     kv_local = kv_cols // head_dim
     group = q_cols // kv_cols
     combined = jnp.concatenate([w_query, w_key, w_value], axis=1)
-    piece = lax.all_gather(hidden_in, TEN, axis=1, tiled=True)
+    piece = lax.all_gather(hidden_in, "core", axis=0, tiled=False)
+    piece = lax.all_gather(piece, "yhi", axis=0, tiled=False)
+    piece = jnp.moveaxis(piece.reshape(-1, *hidden_in.shape), 0, 1).reshape(hidden_in.shape[0], -1)
     wide = piece.astype(jnp.float32)
     scaled = (wide * norm_gain[None, :]).astype(jnp.bfloat16)
     acc = jnp.dot(scaled, combined, preferred_element_type=jnp.float32)

time: 135 us -> 135 us (level)
  waiting for transfers between devices: 39.6 us -> 31.5 us
  blocking collectives: 22.6 us -> 28.5 us
    ppermute x3, waiting for transfers between devices: 11.3 us -> 2.83 us  [ring_gather(): a = lax.ppermute(a, name, cw)]
    all_gather x1 -> x2, blocking collectives: 18.4 us -> 24.2 us  [the longest x1 21.9 us: on_device(): piece = lax.all_gather(piece, 'yhi', axis=0, tiled=False)]
    ppermute x3, waiting for transfers between devices: 4.47 us -> 6.8 us  [ring_gather(): b = lax.ppermute(b, name, ccw)]
    all_to_all x1, waiting for transfers between devices: 8.13 us -> 6.45 us  [on_device(): lax.all_to_all(jnp.broadcast_to(piece, (plane,) + piece.shape[1:]), ('x',...]
    all_to_all x1, starting transfers between devices: 4.66 us -> 6.06 us  [on_device(): part = lax.all_to_all(part, 'yhi', 0, 0, tiled=True)]
where the time goes in v9:
time: 135 us; the launch traced here: 133 us
  starting transfers between devices  45.9 us (34%)
  waiting for transfers between devices  31.5 us (23%)
  blocking collectives  28.5 us (21%)
  other arithmetic  14.1 us (10%)
  matrix products  6.31 us (5%)
  local copies, waits for them, and re-layouts  5.16 us (4%)
    all_gather x1, blocking collectives, on_device(): piece = lax.all_gather(piece, 'yhi', axis=0, tiled=False)  21.9 us
    ppermute x3, starting transfers between devices, ring_gather(): b = lax.ppermute(b, name, ccw)  19.8 us
    all_to_all x1, waiting for transfers between devices, on_device(): part = lax.all_to_all(part, 'yhi', 0, 0, tiled=True)  11.7 us
    ppermute x3, starting transfers between devices, ring_gather(): a = lax.ppermute(a, name, cw)  7.01 us
    ppermute x3, waiting for transfers between devices, ring_gather(): b = lax.ppermute(b, name, ccw)  6.8 us
    all_to_all x1, waiting for transfers between devices, on_device(): lax.all_to_all(jnp.broadcast_to(piece, (plane,) + piece.shape[1:]), ('x',...  6.45 us
    all_to_all x1, starting transfers between devices, on_device(): part = lax.all_to_all(part, 'yhi', 0, 0, tiled=True)  6.06 us
    ppermute x1, starting transfers between devices, ring_gather(): lax.ppermute(b[m // 2:], name, ccw)  5.6 us
  transfers between devices with their start and end apart: 10, of which 9 were waited for; matrix products, arithmetic and copies ran while one was open for 9% of the time, Pallas kernels for 0%

profile of v9, /device:TPU:6, one launch (start us, length us, event | category | flops | bytes accessed | tf_op | source)
XLA Modules:
  0.0 132.6 jit_solution(15872743420465671932)
XLA Ops:
  0.7 2.3 %all-gather = bf16[256,320]{0,1:T(8,128)(2,1)S(1)} all-gather(bf16[128,320]{0,1:T(8,128)(2,1)} %param.9), channel_id=2, replica_groups=mesh['z'=8,'x'=4,'ylo'=2,'yhi'=4,'core'=2] {'core'}, dimensions={0}, use_global_device_ids=true | all-gather | bytes 245760 | tf_op jit(solution)/shard_map/all_gather | solution.py:76
  3.0 21.9 %all-gather.1 = bf16[8,128,320]{1,2,0:T(8,128)(2,1)S(1)} all-gather(bf16[2,128,320]{1,2,0:T(8,128)(2,1)S(1)} %copy_bitcast_fusion.1), channel_id=3, replica_groups=mesh['z'=8,'x'=4,'ylo'=2,'yhi'=4,'core'=2] {'yhi'}, dimensions={0}, use_global_device_ids=true | all-gather | bytes 819200 | tf_op jit(solution)/shard_map/all_gather | solution.py:77
  25.3 1.1 fusion.16
  26.4 2.3 %fusion.17 = f32[128,512]{1,0:T(8,128)S(1)} fusion(bf16[128,2560]{0,1:T(8,128)(2,1)S(1)} %fusion.16, bf16[2560,128]{1,0:T(8,128)(2,1)} %param.13, bf16[2560,128]{1,0:T(8,128)(2,1)} %param.12, bf16[2560,256]{1,0:T(8,128)(2,1)} %param.11, f32[128]{0:T(128)S(1)} %add_rsqrt_fusion.2), kind=kOutput, calls=%fused_computation.24 | convolution fusion | flops 343474176 | bytes 3539456 | tf_op jit(solution)/shard_map/dot_general | solution.py:81
  30.7 5.6 %all-to-all-start = ((bf16[8,128,256]{2,1,0:T(8,128)(2,1)}), bf16[8,128,256]{2,1,0:T(8,128)(2,1)S(1)}, u32[]{:S(2)}, u32[]{:S(2)}) async-start(bf16[8,128,256]{2,1,0:T(8,128)(2,1)} %broadcast_in_dim.31), calls=%async_computation | async-start | bytes 1048576 | tf_op jit(solution)/shard_map/all_to_all | solution.py:101
  36.6 6.5 %all-to-all-done = bf16[8,128,256]{2,1,0:T(8,128)(2,1)S(1)} async-done(((bf16[8,128,256]{2,1,0:T(8,128)(2,1)}), bf16[8,128,256]{2,1,0:T(8,128)(2,1)S(1)}, u32[]{:S(2)}, u32[]{:S(2)}) %all-to-all-start) | async-done | bytes 524320 | tf_op jit(solution)/shard_map/all_to_all | solution.py:101
  43.1 3.2 %collective-permute-start = (bf16[8,128,256]{2,1,0:T(8,128)(2,1)S(1)}, bf16[8,128,256]{2,1,0:T(8,128)(2,1)}, u32[]{:S(2)}, u32[]{:S(2)}) collective-permute-start(bf16[8,128,256]{2,1,0:T(8,128)(2,1)S(1)} %all-to-all-done), channel_id=1, source_target_pairs={{0,64},{64,128},{128,192},{192,256},{256,320},{320,384},{384,448},... | collective-permute-start | bytes 1572872 | tf_op jit(solution)/shard_map/ppermute | solution.py:51
  46.3 3.7 %compare_and_fusion = pred[128,8192]{0,1:T(8,128)(4,1)S(1)} fusion(s32[128]{0:T(128)S(1)} %iota_add_fusion, s32[128]{0:T(128)S(1)} %select_reduce_fusion, s32[8192]{0:T(1024)S(1)} %add_bitcast_fusion), kind=kLoop, calls=%fused_computation.11 | loop fusion | flops 3145728 | bytes 1082368 | tf_op jit(solution)/shard_map/and | solution.py:115
  50.0 8.6 %collective-permute-start.1 = (bf16[8,128,256]{2,1,0:T(8,128)(2,1)S(1)}, bf16[8,128,256]{2,1,0:T(8,128)(2,1)}, u32[]{:S(2)}, u32[]{:S(2)}) collective-permute-start(bf16[8,128,256]{2,1,0:T(8,128)(2,1)S(1)} %all-to-all-done), channel_id=1, source_target_pairs={{0,448},{64,0},{128,64},{192,128},{256,192},{320,256},{384,320},{4... | collective-permute-start | bytes 1572872 | tf_op jit(solution)/shard_map/ppermute | solution.py:52
  59.3 1.0 multiply_cosine_fusion
  60.7 1.9 %collective-permute-start.2 = (bf16[8,128,256]{2,1,0:T(8,128)(2,1)}, bf16[8,128,256]{2,1,0:T(8,128)(2,1)S(1)}, u32[]{:S(2)}, u32[]{:S(2)}) collective-permute-start(bf16[8,128,256]{2,1,0:T(8,128)(2,1)} %collective-permute-done), channel_id=1, source_target_pairs={{0,64},{64,128},{128,192},{192,256},{256,320},{320,384},{384,448},... | collective-permute-start | bytes 1572872 | tf_op jit(solution)/shard_map/ppermute | solution.py:51
  62.6 1.7 %multiply_reduce_fusion.1 = f32[128,2]{1,0:T(8,128)} fusion(f32[128,2,128]{2,1,0:T(2,128)} %reshape.373), kind=kLoop, calls=%fused_computation.33 | loop fusion | flops 65280 | bytes 132096 | tf_op jit(solution)/shard_map/reduce_sum | solution.py:30
  64.4 0.9 copy.41
  65.5 5.7 %collective-permute-start.3 = (bf16[8,128,256]{2,1,0:T(8,128)(2,1)}, bf16[8,128,256]{2,1,0:T(8,128)(2,1)S(1)}, u32[]{:S(2)}, u32[]{:S(2)}) collective-permute-start(bf16[8,128,256]{2,1,0:T(8,128)(2,1)} %collective-permute-done.1), channel_id=1, source_target_pairs={{0,448},{64,0},{128,64},{192,128},{256,192},{320,256},{384,320},{4... | collective-permute-start | bytes 1572872 | tf_op jit(solution)/shard_map/ppermute | solution.py:52
  71.3 2.3 %collective-permute-done.2 = bf16[8,128,256]{2,1,0:T(8,128)(2,1)S(1)} collective-permute-done((bf16[8,128,256]{2,1,0:T(8,128)(2,1)}, bf16[8,128,256]{2,1,0:T(8,128)(2,1)S(1)}, u32[]{:S(2)}, u32[]{:S(2)}) %collective-permute-start.2) | collective-permute-done | bytes 524320 | tf_op jit(solution)/shard_map/ppermute | solution.py:51
  73.6 1.9 %collective-permute-start.4 = (bf16[8,128,256]{2,1,0:T(8,128)(2,1)S(1)}, bf16[8,128,256]{2,1,0:T(8,128)(2,1)S(1)}, u32[]{:S(2)}, u32[]{:S(2)}) collective-permute-start(bf16[8,128,256]{2,1,0:T(8,128)(2,1)S(1)} %collective-permute-done.2), channel_id=1, source_target_pairs={{0,64},{64,128},{128,192},{192,256},{256,320},{320,384},{384,448},... | collective-permute-start | bytes 1572872 | tf_op jit(solution)/shard_map/ppermute | solution.py:51
  75.6 1.0 subtract_convert_fusion
  76.5 2.4 %collective-permute-done.3 = bf16[8,128,256]{2,1,0:T(8,128)(2,1)S(1)} collective-permute-done((bf16[8,128,256]{2,1,0:T(8,128)(2,1)}, bf16[8,128,256]{2,1,0:T(8,128)(2,1)S(1)}, u32[]{:S(2)}, u32[]{:S(2)}) %collective-permute-start.3) | collective-permute-done | bytes 524320 | tf_op jit(solution)/shard_map/ppermute | solution.py:52
  78.9 5.5 %collective-permute-start.5 = (bf16[8,128,256]{2,1,0:T(8,128)(2,1)S(1)}, bf16[8,128,256]{2,1,0:T(8,128)(2,1)S(1)}, u32[]{:S(2)}, u32[]{:S(2)}) collective-permute-start(bf16[8,128,256]{2,1,0:T(8,128)(2,1)S(1)} %collective-permute-done.3), channel_id=1, source_target_pairs={{0,448},{64,0},{128,64},{192,128},{256,192},{320,256},{384,320},{4... | collective-permute-start | bytes 1572872 | tf_op jit(solution)/shard_map/ppermute | solution.py:52
  84.5 1.1 constant_dynamic-update-slice_fusion.7
  85.6 1.1 constant_dynamic-update-slice_fusion.6
  86.9 1.9 %collective-permute-start.6 = (bf16[4,128,256]{2,1,0:T(8,128)(2,1)S(1)}, bf16[4,128,256]{2,1,0:T(8,128)(2,1)S(1)}, u32[]{:S(2)}, u32[]{:S(2)}) collective-permute-start(bf16[4,128,256]{2,1,0:T(8,128)(2,1)S(1)} %slice.57), channel_id=1, source_target_pairs={{0,64},{64,128},{128,192},{192,256},{256,320},{320,384},{384,448},... | collective-permute-start | bytes 786440 | tf_op jit(solution)/shard_map/ppermute | solution.py:59
  88.8 4.1 %collective-permute-done.5 = bf16[8,128,256]{2,1,0:T(8,128)(2,1)S(1)} collective-permute-done((bf16[8,128,256]{2,1,0:T(8,128)(2,1)S(1)}, bf16[8,128,256]{2,1,0:T(8,128)(2,1)S(1)}, u32[]{:S(2)}, u32[]{:S(2)}) %collective-permute-start.5) | collective-permute-done | bytes 524320 | tf_op jit(solution)/shard_map/ppermute | solution.py:52
  93.0 5.6 %collective-permute-start.7 = (bf16[4,128,256]{2,1,0:T(8,128)(2,1)S(1)}, bf16[4,128,256]{2,1,0:T(8,128)(2,1)S(1)}, u32[]{:S(2)}, u32[]{:S(2)}) collective-permute-start(bf16[4,128,256]{2,1,0:T(8,128)(2,1)S(1)} %slice.58), channel_id=1, source_target_pairs={{0,448},{64,0},{128,64},{192,128},{256,192},{320,256},{384,320},{4... | collective-permute-start | bytes 786440 | tf_op jit(solution)/shard_map/ppermute | solution.py:59
  98.7 3.7 %collective-permute-done.7 = bf16[4,128,256]{2,1,0:T(8,128)(2,1)S(1)} collective-permute-done((bf16[4,128,256]{2,1,0:T(8,128)(2,1)S(1)}, bf16[4,128,256]{2,1,0:T(8,128)(2,1)S(1)}, u32[]{:S(2)}, u32[]{:S(2)}) %collective-permute-start.7) | collective-permute-done | bytes 262176 | tf_op jit(solution)/shard_map/ppermute | solution.py:59
  102.5 1.9 %fusion.44 = (f32[2,128]{1,0:T(2,128)S(1)}, f32[1,2,128,8192]{2,3,1,0:T(8,128)S(1)}) fusion(bf16[128,2,64]{2,0,1:T(8,128)(2,1)S(1)} %get-tuple-element.4, bf16[128,2,64]{2,0,1:T(8,128)(2,1)S(1)} %get-tuple-element.3, bf16[8192,256]{1,0:T(8,128)(2,1)S(1)} %bitcast.67, pred[128,8192]{0,1:T(8,128)(4,1)S(1)} %compare_and_fusion), kind=kOutput, calls=%fused_computation.90 | convolution fusion | flops 543293184 | bytes 11666432 | tf_op jit(solution)/shard_map/qhgd,khd->hgqk/dot_general | solution.py:112
  104.4 1.7 %fusion.2 = f32[2,128]{1,0:T(2,128)S(1)} fusion(f32[1,2,128,8192]{2,3,1,0:T(8,128)S(1)} %get-tuple-element.12, f32[2,128]{1,0:T(2,128)S(1)} %get-tuple-element.11, pred[128,8192]{0,1:T(8,128)(4,1)S(1)} %compare_and_fusion), kind=kLoop, calls=%fused_computation.4 | loop fusion | flops 6291200 | bytes 9439232 | tf_op jit(solution)/shard_map/reduce_sum | solution.py:119
  106.1 1.8 %fusion.23 = bf16[2,128,128]{1,2,0:T(8,128)(2,1)S(1)} fusion(bf16[8192,256]{1,0:T(8,128)(2,1)S(1)} %bitcast.68, f32[1,2,128,8192]{2,3,1,0:T(8,128)S(1)} %get-tuple-element.12, f32[2,128]{1,0:T(2,128)S(1)} %get-tuple-element.11, pred[128,8192]{0,1:T(8,128)(4,1)S(1)} %compare_and_fusion, f32[2,128]{1,0:T(2,128)S(1)} %fusion.2), kind=kOutput, calls=%fused_computation.26 | convolution fusion | flops 543227904 | bytes 11601920 | tf_op jit(solution)/shard_map/hgqk,khd->hgqd/dot_general | solution.py:120
  108.3 4.3 %all_to_all.15 = bf16[2,4,16,2560]{3,2,1,0:T(8,128)(2,1)S(1)} all-to-all(bf16[2,4,16,2560]{3,2,1,0:T(8,128)(2,1)S(1)} %bitcast.65), channel_id=1, replica_groups=mesh['z'=8,'x'=4,'ylo'=2,'yhi'=4,'core'=2] {'core'}, dimensions={0} | all-to-all | bytes 1310720 | tf_op jit(solution)/shard_map/all_to_all | solution.py:133
  112.6 0.9 reduce_sum.84
  113.5 6.1 %all-to-all-start.2 = ((bf16[4,16,2560]{2,1,0:T(8,128)(2,1)}), bf16[4,16,2560]{2,1,0:T(8,128)(2,1)S(1)}, u32[]{:S(2)}, u32[]{:S(2)}) async-start(bf16[4,16,2560]{2,1,0:T(8,128)(2,1)} %reduce_sum.84), calls=%async_computation.2 | async-start | bytes 655360 | tf_op jit(solution)/shard_map/all_to_all | solution.py:135
  120.2 11.7 %all-to-all-done.2 = bf16[4,16,2560]{2,1,0:T(8,128)(2,1)S(1)} async-done(((bf16[4,16,2560]{2,1,0:T(8,128)(2,1)}), bf16[4,16,2560]{2,1,0:T(8,128)(2,1)S(1)}, u32[]{:S(2)}, u32[]{:S(2)}) %all-to-all-start.2) | async-done | bytes 327712 | tf_op jit(solution)/shard_map/all_to_all | solution.py:135
  (68 shorter events, 6.2 us)
Async XLA Ops:
  0.6 107.3 %copy-start = (bf16[256,2560]{1,0:T(8,128)(2,1)S(1)}, bf16[256,2560]{1,0:T(8,128)(2,1)}, u32[]{:S(2)}) copy-start(bf16[256,2560]{1,0:T(8,128)(2,1)} %param.14) | copy-start | bytes 3932164
  25.2 3.6 %copy-start.8 = (s32[16]{0:T(128)S(1)}, s32[16]{0:T(128)}, u32[]{:S(2)}) copy-start(s32[16]{0:T(128)} %param.17) | copy-start | bytes 196
  25.2 4.1 %copy-start.6 = (f32[128]{0:T(128)S(1)}, f32[128]{0:T(128)}, u32[]{:S(2)}) copy-start(f32[128]{0:T(128)} %param.16) | copy-start | bytes 1540
  26.4 44.8 %copy-start.7 = (f32[128]{0:T(128)S(1)}, f32[128]{0:T(128)}, u32[]{:S(2)}) copy-start(f32[128]{0:T(128)} %param.15) | copy-start | bytes 1540
  28.8 1.9 %copy-start.5 = (bf16[128,128]{1,0:T(8,128)(2,1)}, bf16[128,128]{1,0:T(8,128)(2,1)S(1)}, u32[]{:S(2)}) copy-start(bf16[128,128]{1,0:T(8,128)(2,1)S(1)} %slice.94) | copy-start | bytes 98308
  29.7 0.9 copy-start.1
  29.8 0.9 copy-start.3
  30.7 12.4 %all-to-all-start = ((bf16[8,128,256]{2,1,0:T(8,128)(2,1)}), bf16[8,128,256]{2,1,0:T(8,128)(2,1)S(1)}, u32[]{:S(2)}, u32[]{:S(2)}) async-start(bf16[8,128,256]{2,1,0:T(8,128)(2,1)} %broadcast_in_dim.31), calls=%async_computation | async-start | bytes 1048576 | tf_op jit(solution)/shard_map/all_to_all | solution.py:101
  43.1 17.6 %collective-permute-start = (bf16[8,128,256]{2,1,0:T(8,128)(2,1)S(1)}, bf16[8,128,256]{2,1,0:T(8,128)(2,1)}, u32[]{:S(2)}, u32[]{:S(2)}) collective-permute-start(bf16[8,128,256]{2,1,0:T(8,128)(2,1)S(1)} %all-to-all-done), channel_id=1, source_target_pairs={{0,64},{64,128},{128,192},{192,256},{256,320},{320,384},{384,448},... | collective-permute-start | bytes 1572872 | tf_op jit(solution)/shard_map/ppermute | solution.py:51
  50.0 15.5 %collective-permute-start.1 = (bf16[8,128,256]{2,1,0:T(8,128)(2,1)S(1)}, bf16[8,128,256]{2,1,0:T(8,128)(2,1)}, u32[]{:S(2)}, u32[]{:S(2)}) collective-permute-start(bf16[8,128,256]{2,1,0:T(8,128)(2,1)S(1)} %all-to-all-done), channel_id=1, source_target_pairs={{0,448},{64,0},{128,64},{192,128},{256,192},{320,256},{384,320},{4... | collective-permute-start | bytes 1572872 | tf_op jit(solution)/shard_map/ppermute | solution.py:52
  60.7 12.9 %collective-permute-start.2 = (bf16[8,128,256]{2,1,0:T(8,128)(2,1)}, bf16[8,128,256]{2,1,0:T(8,128)(2,1)S(1)}, u32[]{:S(2)}, u32[]{:S(2)}) collective-permute-start(bf16[8,128,256]{2,1,0:T(8,128)(2,1)} %collective-permute-done), channel_id=1, source_target_pairs={{0,64},{64,128},{128,192},{192,256},{256,320},{320,384},{384,448},... | collective-permute-start | bytes 1572872 | tf_op jit(solution)/shard_map/ppermute | solution.py:51
  65.5 13.4 %collective-permute-start.3 = (bf16[8,128,256]{2,1,0:T(8,128)(2,1)}, bf16[8,128,256]{2,1,0:T(8,128)(2,1)S(1)}, u32[]{:S(2)}, u32[]{:S(2)}) collective-permute-start(bf16[8,128,256]{2,1,0:T(8,128)(2,1)} %collective-permute-done.1), channel_id=1, source_target_pairs={{0,448},{64,0},{128,64},{192,128},{256,192},{320,256},{384,320},{4... | collective-permute-start | bytes 1572872 | tf_op jit(solution)/shard_map/ppermute | solution.py:52
  73.6 13.2 %collective-permute-start.4 = (bf16[8,128,256]{2,1,0:T(8,128)(2,1)S(1)}, bf16[8,128,256]{2,1,0:T(8,128)(2,1)S(1)}, u32[]{:S(2)}, u32[]{:S(2)}) collective-permute-start(bf16[8,128,256]{2,1,0:T(8,128)(2,1)S(1)} %collective-permute-done.2), channel_id=1, source_target_pairs={{0,64},{64,128},{128,192},{192,256},{256,320},{320,384},{384,448},... | collective-permute-start | bytes 1572872 | tf_op jit(solution)/shard_map/ppermute | solution.py:51
  78.9 14.0 %collective-permute-start.5 = (bf16[8,128,256]{2,1,0:T(8,128)(2,1)S(1)}, bf16[8,128,256]{2,1,0:T(8,128)(2,1)S(1)}, u32[]{:S(2)}, u32[]{:S(2)}) collective-permute-start(bf16[8,128,256]{2,1,0:T(8,128)(2,1)S(1)} %collective-permute-done.3), channel_id=1, source_target_pairs={{0,448},{64,0},{128,64},{192,128},{256,192},{320,256},{384,320},{4... | collective-permute-start | bytes 1572872 | tf_op jit(solution)/shard_map/ppermute | solution.py:52
  86.9 11.8 %collective-permute-start.6 = (bf16[4,128,256]{2,1,0:T(8,128)(2,1)S(1)}, bf16[4,128,256]{2,1,0:T(8,128)(2,1)S(1)}, u32[]{:S(2)}, u32[]{:S(2)}) collective-permute-start(bf16[4,128,256]{2,1,0:T(8,128)(2,1)S(1)} %slice.57), channel_id=1, source_target_pairs={{0,64},{64,128},{128,192},{192,256},{256,320},{320,384},{384,448},... | collective-permute-start | bytes 786440 | tf_op jit(solution)/shard_map/ppermute | solution.py:59
  93.0 9.5 %collective-permute-start.7 = (bf16[4,128,256]{2,1,0:T(8,128)(2,1)S(1)}, bf16[4,128,256]{2,1,0:T(8,128)(2,1)S(1)}, u32[]{:S(2)}, u32[]{:S(2)}) collective-permute-start(bf16[4,128,256]{2,1,0:T(8,128)(2,1)S(1)} %slice.58), channel_id=1, source_target_pairs={{0,448},{64,0},{128,64},{192,128},{256,192},{320,256},{384,320},{4... | collective-permute-start | bytes 786440 | tf_op jit(solution)/shard_map/ppermute | solution.py:59
  107.9 11.7 %copy-start.2 = (bf16[128,64]{1,0:T(8,128)(2,1)S(1)}, bf16[128,64]{1,0:T(8,128)(2,1)}, u32[]{:S(2)}) copy-start(bf16[128,64]{1,0:T(8,128)(2,1)} %copy-done.1) | copy-start | bytes 49156
  107.9 11.7 %copy-start.4 = (bf16[128,64]{1,0:T(8,128)(2,1)S(1)}, bf16[128,64]{1,0:T(8,128)(2,1)}, u32[]{:S(2)}) copy-start(bf16[128,64]{1,0:T(8,128)(2,1)} %copy-done.3) | copy-start | bytes 49156
  113.5 18.4 %all-to-all-start.2 = ((bf16[4,16,2560]{2,1,0:T(8,128)(2,1)}), bf16[4,16,2560]{2,1,0:T(8,128)(2,1)S(1)}, u32[]{:S(2)}, u32[]{:S(2)}) async-start(bf16[4,16,2560]{2,1,0:T(8,128)(2,1)} %reduce_sum.84), calls=%async_computation.2 | async-start | bytes 655360 | tf_op jit(solution)/shard_map/all_to_all | solution.py:135

commit v10 on v4

--- a/solution.py
+++ b/solution.py
@@ -92,12 +92,10 @@
     key_flat = keys.reshape(tokens, kv_cols)
     value_flat = proj[:, q_cols + kv_cols :].astype(jnp.bfloat16)
 
-    nx, nlo = lax.axis_size("x"), lax.axis_size("ylo")
+    nseq = lax.axis_size(SEQ)
     piece = jnp.concatenate([key_flat, value_flat], axis=1)[None]
-    block_ids = jnp.zeros((1,), jnp.int32)
-    piece, block_ids = ring_gather(piece, block_ids, "ylo", 1)
-    piece, block_ids = ring_gather(piece, block_ids, "x", nlo)
-    piece, block_ids = ring_gather(piece, block_ids, "z", nx * nlo)
+    piece = lax.all_to_all(jnp.broadcast_to(piece, (nseq,) + piece.shape[1:]), SEQ, 0, 0, tiled=True)
+    block_ids = jnp.arange(nseq, dtype=jnp.int32)
     span = piece.shape[0] * tokens
     kv_all = piece.reshape(span, 2 * kv_cols)
     key_pos = (block_ids[:, None] * tokens + jnp.arange(tokens, dtype=jnp.int32)[None, :]).reshape(span)

time: 147 us -> 175 us (1.19)
  waiting for transfers between devices: 33.2 us -> 108 us
  starting transfers between devices: 56.3 us -> 20.3 us
  local copies, waits for them, and re-layouts: 12.5 us -> 2.8 us
    all_to_all x0 -> x1, waiting for transfers between devices: none -> 96.5 us  [on_device(): lax.all_to_all(jnp.broadcast_to(piece, (nseq,) + piece.shape[1:]), SEQ, 0...]
    ppermute x13 -> x0, starting transfers between devices: 51.5 us -> none  [the longest x4 24.9 us: ring_gather(): b = lax.ppermute(b, name, ccw)]
    ppermute x13 -> x0, waiting for transfers between devices: 21.8 us -> none  [the longest x4 9.5 us: ring_gather(): b = lax.ppermute(b, name, ccw)]
    all_to_all x0 -> x1, starting transfers between devices: none -> 14.5 us  [on_device(): lax.all_to_all(jnp.broadcast_to(piece, (nseq,) + piece.shape[1:]), SEQ, 0...]
    unnamed x24 -> x10, local copies, waits for them, and re-layouts: 10.6 us -> 0.03 us
    broadcast_in_dim x0 -> x1, local copies, waits for them, and re-layouts: none -> 2.48 us  [on_device(): jnp.broadcast_to(piece, (nseq,) + piece.shape[1:])]
  transfers between devices with their start and end apart: 14 -> 2, of which waited for: 7 -> 2; matrix products, arithmetic and copies ran while one was open for 11% -> 3% of each run, Pallas kernels for 0% -> 0%
where the time goes in v10:
time: 175 us; the launch traced here: 174 us
  waiting for transfers between devices  108 us (62%)
  blocking collectives  22.6 us (13%)
  starting transfers between devices  20.3 us (12%)
  matrix products  10.2 us (6%)
  other arithmetic  9.83 us (6%)
  local copies, waits for them, and re-layouts  2.8 us (2%)
    all_to_all x1, waiting for transfers between devices, on_device(): lax.all_to_all(jnp.broadcast_to(piece, (nseq,) + piece.shape[1:]), SEQ, 0...  96.5 us
    all_gather x1, blocking collectives, on_device(): piece = lax.all_gather(hidden_in, TEN, axis=1, tiled=True)  18.4 us
    all_to_all x1, starting transfers between devices, on_device(): lax.all_to_all(jnp.broadcast_to(piece, (nseq,) + piece.shape[1:]), SEQ, 0...  14.5 us
    all_to_all x1, waiting for transfers between devices, on_device(): part = lax.all_to_all(part, 'yhi', 0, 0, tiled=True)  11 us
    all_to_all x1, starting transfers between devices, on_device(): part = lax.all_to_all(part, 'yhi', 0, 0, tiled=True)  5.81 us
    all_to_all x1, blocking collectives, on_device(): part = lax.all_to_all(part, 'core', 0, 0, tiled=True)  4.26 us
    and x1, other arithmetic, on_device(): (key_pos[None, :] >= seg_start[:, None]) & (key_pos[None, :] <= token_pos...  3.73 us
  transfers between devices with their start and end apart: 2, of which 2 were waited for; matrix products, arithmetic and copies ran while one was open for 3% of the time, Pallas kernels for 0%

profile of v10, /device:TPU:6, one launch (start us, length us, event | category | flops | bytes accessed | tf_op | source)
XLA Modules:
  0.0 174.1 jit_solution(12909427560523905352)
XLA Ops:
  0.7 18.4 %all_gather.3 = bf16[128,2560]{0,1:T(8,128)(2,1)S(1)} all-gather(bf16[128,320]{0,1:T(8,128)(2,1)} %param.9), channel_id=1, replica_groups=mesh['z'=8,'x'=4,'ylo'=2,'yhi'=4,'core'=2] {'yhi','core'}, dimensions={1}, use_global_device_ids=true | all-gather | bytes 737280 | tf_op jit(solution)/shard_map/all_gather | solution.py:76
  19.0 0.4 fusion.17
  19.4 3.1 %fusion.18 = f32[128,512]{1,0:T(8,128)S(1)} fusion(bf16[2560,128]{1,0:T(8,128)(2,1)} %param.13, bf16[2560,128]{1,0:T(8,128)(2,1)} %param.12, bf16[2560,256]{1,0:T(8,128)(2,1)} %param.11, bf16[128,2560]{0,1:T(8,128)(2,1)S(1)} %all_gather.3, f32[2560]{0:T(1024)} %param.10, f32[128]{0:T(128)S(1)} %add_rsqrt_fusion.2), kind=kOutput, calls=%fused_computation.25 | convolution fusion | flops 344457216 | bytes 3549696 | tf_op jit(solution)/shard_map/dot_general | solution.py:79
  22.5 0.1 multiply_reduce_fusion.1
  22.6 0.1 copy.32
  22.8 0.1 reduce.6
  22.9 0.1 convert_reduce_fusion
  23.0 0.1 select_reduce_fusion
  23.1 0.1 multiply_bitcast_fusion
  23.2 0.3 fusion.42
  23.5 0.1 pad_maximum_fusion
  23.6 2.5 %broadcast_in_dim.31 = bf16[64,128,256]{2,1,0:T(8,128)(2,1)} broadcast(bf16[128,256]{1,0:T(8,128)(2,1)S(1)} %pad_maximum_fusion), dimensions={1,2} | broadcast | bytes 4259840 | tf_op jit(solution)/shard_map/broadcast_in_dim | solution.py:97
  26.1 14.5 %all-to-all-start = ((bf16[64,128,256]{2,1,0:T(8,128)(2,1)}), bf16[64,128,256]{2,1,0:T(8,128)(2,1)}, u32[]{:S(2)}, u32[]{:S(2)}) async-start(bf16[64,128,256]{2,1,0:T(8,128)(2,1)} %broadcast_in_dim.31), calls=%async_computation | async-start | bytes 8388608 | tf_op jit(solution)/shard_map/all_to_all | solution.py:97
  40.6 0.1 reshape.312
  40.7 0.2 multiply_reduce_fusion
  40.9 0.1 copy.33
  41.0 0.1 add_bitcast_fusion
  41.1 0.3 multiply_cosine_fusion
  41.4 0.1 fusion.29
  41.5 0.1 subtract_convert_fusion
  41.6 3.7 %compare_and_fusion = pred[128,8192]{0,1:T(8,128)(4,1)S(1)} fusion(s32[128]{0:T(128)S(1)} %iota_add_fusion, s32[128]{0:T(128)S(1)} %select_reduce_fusion, s32[8192]{0:T(1024)S(1)} %add_bitcast_fusion), kind=kLoop, calls=%fused_computation.11 | loop fusion | flops 3145728 | bytes 1082368 | tf_op jit(solution)/shard_map/and | solution.py:110
  45.3 96.5 %all-to-all-done = bf16[64,128,256]{2,1,0:T(8,128)(2,1)} async-done(((bf16[64,128,256]{2,1,0:T(8,128)(2,1)}), bf16[64,128,256]{2,1,0:T(8,128)(2,1)}, u32[]{:S(2)}, u32[]{:S(2)}) %all-to-all-start) | async-done | bytes 4194336 | tf_op jit(solution)/shard_map/all_to_all | solution.py:97
  141.9 3.4 %fusion.47 = (f32[2,128]{1,0:T(2,128)S(1)}, f32[1,2,128,8192]{2,3,1,0:T(8,128)S(1)}) fusion(bf16[128,2,64]{2,0,1:T(8,128)(2,1)S(1)} %get-tuple-element.4, bf16[128,2,64]{2,0,1:T(8,128)(2,1)S(1)} %get-tuple-element.3, bf16[8192,256]{1,0:T(8,128)(2,1)} %bitcast.5, pred[128,8192]{0,1:T(8,128)(4,1)S(1)} %compare_and_fusion), kind=kOutput, calls=%fused_computation.73 | convolution fusion | flops 543293184 | bytes 11600896 | tf_op jit(solution)/shard_map/qhgd,khd->hgqk/dot_general | solution.py:107
  145.3 1.7 fusion.2
  147.0 3.4 %fusion.24 = bf16[2,128,128]{1,2,0:T(8,128)(2,1)S(1)} fusion(bf16[8192,256]{1,0:T(8,128)(2,1)} %bitcast.5, f32[1,2,128,8192]{2,3,1,0:T(8,128)S(1)} %get-tuple-element.12, f32[2,128]{1,0:T(2,128)S(1)} %get-tuple-element.11, pred[128,8192]{0,1:T(8,128)(4,1)S(1)} %compare_and_fusion, f32[2,128]{1,0:T(2,128)S(1)} %fusion.2), kind=kOutput, calls=%fused_computation.27 | convolution fusion | flops 543227904 | bytes 11601920 | tf_op jit(solution)/shard_map/hgqk,khd->hgqd/dot_general | solution.py:115
  150.4 0.4 convolution_convert_fusion
  150.8 4.3 %all_to_all.15 = bf16[2,4,16,2560]{3,2,1,0:T(8,128)(2,1)S(1)} all-to-all(bf16[2,4,16,2560]{3,2,1,0:T(8,128)(2,1)S(1)} %bitcast.53), channel_id=1, replica_groups=mesh['z'=8,'x'=4,'ylo'=2,'yhi'=4,'core'=2] {'core'}, dimensions={0} | all-to-all | bytes 1310720 | tf_op jit(solution)/shard_map/all_to_all | solution.py:128
  155.0 0.9 reduce_sum.84
  155.9 5.8 %all-to-all-start.2 = ((bf16[4,16,2560]{2,1,0:T(8,128)(2,1)}), bf16[4,16,2560]{2,1,0:T(8,128)(2,1)S(1)}, u32[]{:S(2)}, u32[]{:S(2)}) async-start(bf16[4,16,2560]{2,1,0:T(8,128)(2,1)} %reduce_sum.84), calls=%async_computation.2 | async-start | bytes 655360 | tf_op jit(solution)/shard_map/all_to_all | solution.py:130
  161.7 0.7 pad_maximum_fusion.1
  162.4 11.0 %all-to-all-done.2 = bf16[4,16,2560]{2,1,0:T(8,128)(2,1)S(1)} async-done(((bf16[4,16,2560]{2,1,0:T(8,128)(2,1)}), bf16[4,16,2560]{2,1,0:T(8,128)(2,1)S(1)}, u32[]{:S(2)}, u32[]{:S(2)}) %all-to-all-start.2) | async-done | bytes 327712 | tf_op jit(solution)/shard_map/all_to_all | solution.py:130
  173.4 0.7 reduce_sum.85
  (22 shorter events, 0.2 us)
Async XLA Ops:
  0.6 149.7 %copy-start = (bf16[256,2560]{1,0:T(8,128)(2,1)S(1)}, bf16[256,2560]{1,0:T(8,128)(2,1)}, u32[]{:S(2)}) copy-start(bf16[256,2560]{1,0:T(8,128)(2,1)} %param.14) | copy-start | bytes 3932164
  19.0 3.6 %copy-start.4 = (s32[16]{0:T(128)S(1)}, s32[16]{0:T(128)}, u32[]{:S(2)}) copy-start(s32[16]{0:T(128)} %param.17) | copy-start | bytes 196
  19.0 4.1 %copy-start.2 = (f32[128]{0:T(128)S(1)}, f32[128]{0:T(128)}, u32[]{:S(2)}) copy-start(f32[128]{0:T(128)} %param.16) | copy-start | bytes 1540
  22.6 3.5 %copy-start.1 = (bf16[128,128]{1,0:T(8,128)(2,1)}, bf16[128,128]{1,0:T(8,128)(2,1)S(1)}, u32[]{:S(2)}) copy-start(bf16[128,128]{1,0:T(8,128)(2,1)S(1)} %slice.74) | copy-start | bytes 98308
  26.1 15.3 %copy-start.3 = (f32[128]{0:T(128)S(1)}, f32[128]{0:T(128)}, u32[]{:S(2)}) copy-start(f32[128]{0:T(128)} %param.15) | copy-start | bytes 1540
  26.1 115.8 %all-to-all-start = ((bf16[64,128,256]{2,1,0:T(8,128)(2,1)}), bf16[64,128,256]{2,1,0:T(8,128)(2,1)}, u32[]{:S(2)}, u32[]{:S(2)}) async-start(bf16[64,128,256]{2,1,0:T(8,128)(2,1)} %broadcast_in_dim.31), calls=%async_computation | async-start | bytes 8388608 | tf_op jit(solution)/shard_map/all_to_all | solution.py:97
  155.9 17.5 %all-to-all-start.2 = ((bf16[4,16,2560]{2,1,0:T(8,128)(2,1)}), bf16[4,16,2560]{2,1,0:T(8,128)(2,1)S(1)}, u32[]{:S(2)}, u32[]{:S(2)}) async-start(bf16[4,16,2560]{2,1,0:T(8,128)(2,1)} %reduce_sum.84), calls=%async_computation.2 | async-start | bytes 655360 | tf_op jit(solution)/shard_map/all_to_all | solution.py:130

commit v11 on v5

--- a/solution.py
+++ b/solution.py
@@ -98,12 +98,15 @@
     plane = nx * nlo
     piece = lax.all_to_all(jnp.broadcast_to(piece, (plane,) + piece.shape[1:]), ("x", "ylo"), 0, 0, tiled=True)
     block_ids = jnp.arange(plane, dtype=jnp.int32)
-    piece, block_ids = ring_gather(piece, block_ids, "z", nx * nlo)
-    span = piece.shape[0] * tokens
-    kv_all = piece.reshape(span, 2 * kv_cols)
-    key_pos = (block_ids[:, None] * tokens + jnp.arange(tokens, dtype=jnp.int32)[None, :]).reshape(span)
-    key_heads = kv_all[:, :kv_cols].reshape(span, kv_local, head_dim)
-    value_heads = kv_all[:, kv_cols:].reshape(span, kv_local, head_dim)
+    nz = lax.axis_size("z")
+    kz = lax.all_gather(piece[..., :kv_cols], "z", axis=0, tiled=True)
+    vz, vids = ring_gather(piece[..., kv_cols:], block_ids, "z", plane)
+    slot_of = jnp.zeros((nz,), jnp.int32).at[vids[::plane] // plane].set(jnp.arange(nz, dtype=jnp.int32))
+    vz = jnp.take(vz.reshape(nz, plane, tokens, kv_cols), slot_of, axis=0)
+    span = nz * plane * tokens
+    key_pos = jnp.arange(span, dtype=jnp.int32)
+    key_heads = kz.reshape(span, kv_local, head_dim)
+    value_heads = vz.reshape(span, kv_local, head_dim)
     query_grid = queries.reshape(tokens, kv_local, group, head_dim)
     inv_root = 1.0 / math.sqrt(head_dim)
     score = (

time: 135 us -> 155 us (1.15)
  between operations: 1.1 us -> 14.6 us
  local copies, waits for them, and re-layouts: 5.14 us -> 8.67 us
  waiting for transfers between devices: 39.6 us -> 42.7 us
  matrix products: 7.1 us -> 8.94 us
  starting transfers between devices: 44.9 us -> 43.3 us
    ppermute x3, waiting for transfers between devices: 4.47 us -> 15.1 us  [ring_gather(): b = lax.ppermute(b, name, ccw)]
    ppermute x3, waiting for transfers between devices: 11.3 us -> 3.45 us  [ring_gather(): a = lax.ppermute(a, name, cw)]
    ppermute x1, waiting for transfers between devices: 0.01 us -> 6.06 us  [ring_gather(): lax.ppermute(a[:m // 2], name, cw)]
    ppermute x1, waiting for transfers between devices: 3.74 us -> 0.01 us  [ring_gather(): lax.ppermute(b[m // 2:], name, ccw)]
    gather x0 -> x1, local copies, waits for them, and re-layouts: none -> 2.54 us  [on_device(): vz = jnp.take(vz.reshape(nz, plane, tokens, kv_cols), slot_of, axis=0)]
    slice x0 -> x2, local copies, waits for them, and re-layouts: none -> 2.07 us  [the longest x1 1.97 us: on_device(): kz = lax.all_gather(piece[..., :kv_cols], 'z', axis=0, tiled=True)]
    all_to_all x1, waiting for transfers between devices: 8.13 us -> 6.07 us  [on_device(): lax.all_to_all(jnp.broadcast_to(piece, (plane,) + piece.shape[1:]), ('x',...]
    dot_general x1, matrix products: 1.88 us -> 3.76 us  [on_device(): jnp.einsum('qhgd,khd->hgqk', query_grid, key_heads, preferred_element_typ...]
  transfers between devices with their start and end apart: 10 -> 11, of which waited for: 9 -> 8; matrix products, arithmetic and copies ran while one was open for 9% -> 7% of each run, Pallas kernels for 0% -> 0%
where the time goes in v11:
time: 155 us; the launch traced here: 153 us
  starting transfers between devices  43.3 us (28%)
  waiting for transfers between devices  42.7 us (28%)
  blocking collectives  22.6 us (15%)
  between operations  14.6 us (9%)
  other arithmetic  11.8 us (8%)
  matrix products  8.94 us (6%)
  local copies, waits for them, and re-layouts  8.67 us (6%)
    ppermute x3, starting transfers between devices, ring_gather(): b = lax.ppermute(b, name, ccw)  19.5 us
    all_gather x1, blocking collectives, on_device(): piece = lax.all_gather(hidden_in, TEN, axis=1, tiled=True)  18.4 us
    ppermute x3, waiting for transfers between devices, ring_gather(): b = lax.ppermute(b, name, ccw)  15.1 us
    all_to_all x1, waiting for transfers between devices, on_device(): part = lax.all_to_all(part, 'yhi', 0, 0, tiled=True)  12 us
    all_to_all x1, starting transfers between devices, on_device(): lax.all_to_all(jnp.broadcast_to(piece, (plane,) + piece.shape[1:]), ('x',...  7.04 us
    all_to_all x1, waiting for transfers between devices, on_device(): lax.all_to_all(jnp.broadcast_to(piece, (plane,) + piece.shape[1:]), ('x',...  6.07 us
    ppermute x1, waiting for transfers between devices, ring_gather(): lax.ppermute(a[:m // 2], name, cw)  6.06 us
    ppermute x3, starting transfers between devices, ring_gather(): a = lax.ppermute(a, name, cw)  5.74 us
  transfers between devices with their start and end apart: 11, of which 8 were waited for; matrix products, arithmetic and copies ran while one was open for 7% of the time, Pallas kernels for 0%

profile of v11, /device:TPU:6, one launch (start us, length us, event | category | flops | bytes accessed | tf_op | source)
XLA Modules:
  0.0 152.7 jit_solution(4708145503223270065)
XLA Ops:
  7.2 18.4 %all_gather.6 = bf16[128,2560]{0,1:T(8,128)(2,1)S(1)} all-gather(bf16[128,320]{0,1:T(8,128)(2,1)} %param.9), channel_id=1, replica_groups=mesh['z'=8,'x'=4,'ylo'=2,'yhi'=4,'core'=2] {'yhi','core'}, dimensions={1}, use_global_device_ids=true | all-gather | bytes 737280 | tf_op jit(solution)/shard_map/all_gather | solution.py:76
  25.9 3.1 %fusion.19 = f32[128,512]{1,0:T(8,128)S(1)} fusion(bf16[2560,128]{1,0:T(8,128)(2,1)} %param.13, bf16[2560,128]{1,0:T(8,128)(2,1)} %param.12, bf16[2560,256]{1,0:T(8,128)(2,1)} %param.11, bf16[128,2560]{0,1:T(8,128)(2,1)S(1)} %all_gather.6, f32[2560]{0:T(1024)} %param.10, f32[128]{0:T(128)S(1)} %add_rsqrt_fusion.2), kind=kOutput, calls=%fused_computation.28 | convolution fusion | flops 344457216 | bytes 3549696 | tf_op jit(solution)/shard_map/dot_general | solution.py:79
  31.6 7.0 %all-to-all-start = ((bf16[8,128,256]{2,1,0:T(8,128)(2,1)}), bf16[8,128,256]{2,1,0:T(8,128)(2,1)}, u32[]{:S(2)}, u32[]{:S(2)}) async-start(bf16[8,128,256]{2,1,0:T(8,128)(2,1)} %broadcast_in_dim.45), calls=%async_computation | async-start | bytes 1048576 | tf_op jit(solution)/shard_map/all_to_all | solution.py:99
  40.1 1.0 multiply_cosine_fusion
  41.2 6.1 %all-to-all-done = bf16[8,128,256]{2,1,0:T(8,128)(2,1)} async-done(((bf16[8,128,256]{2,1,0:T(8,128)(2,1)}), bf16[8,128,256]{2,1,0:T(8,128)(2,1)}, u32[]{:S(2)}, u32[]{:S(2)}) %all-to-all-start) | async-done | bytes 524320 | tf_op jit(solution)/shard_map/all_to_all | solution.py:99
  47.3 2.0 %fusion.49 = (bf16[8,128,128]{2,1,0:T(8,128)(2,1)}, bf16[64,128,128]{2,1,0:T(8,128)(2,1)S(1)}, bf16[8,128,128]{2,1,0:T(8,128)(2,1)}) fusion(bf16[8,128,256]{2,1,0:T(8,128)(2,1)} %all-to-all-done), kind=kLoop, calls=%fused_computation.101 | loop fusion | bytes 1310720 | tf_op jit(solution)/shard_map/slice | solution.py:102
  49.2 1.9 %fusion.9 = pred[128,8192]{0,1:T(8,128)(4,1)} fusion(s32[128]{0:T(128)S(1)} %iota_add_fusion.7, s32[128]{0:T(128)S(1)} %select_reduce_fusion), kind=kLoop, calls=%fused_computation.14 | loop fusion | flops 3145728 | bytes 1049600 | tf_op jit(solution)/shard_map/and | solution.py:116
  51.2 8.4 %collective-permute-start.1 = (bf16[8,128,128]{2,1,0:T(8,128)(2,1)}, bf16[8,128,128]{2,1,0:T(8,128)(2,1)S(1)}, u32[]{:S(2)}, u32[]{:S(2)}) collective-permute-start(bf16[8,128,128]{2,1,0:T(8,128)(2,1)} %get-tuple-element.5), channel_id=1, source_target_pairs={{0,448},{64,0},{128,64},{192,128},{256,192},{320,256},{384,320},{4... | collective-permute-start | bytes 786440 | tf_op jit(solution)/shard_map/ppermute | solution.py:52
  59.6 1.9 %collective-permute-start = (bf16[8,128,128]{2,1,0:T(8,128)(2,1)}, bf16[8,128,128]{2,1,0:T(8,128)(2,1)S(1)}, u32[]{:S(2)}, u32[]{:S(2)}) collective-permute-start(bf16[8,128,128]{2,1,0:T(8,128)(2,1)} %get-tuple-element.5), channel_id=1, source_target_pairs={{0,64},{64,128},{128,192},{192,256},{256,320},{320,384},{384,448},... | collective-permute-start | bytes 786440 | tf_op jit(solution)/shard_map/ppermute | solution.py:51
  61.6 1.6 %subtract_convert_fusion = (bf16[128,2,64]{2,0,1:T(8,128)(2,1)}, bf16[128,2,64]{2,0,1:T(8,128)(2,1)}) fusion(f32[128,2,128]{2,0,1:T(8,128)S(1)} %fusion.30, f32[128,64]{1,0:T(8,128)} %get-tuple-element.13, f32[128,64]{1,0:T(8,128)} %get-tuple-element.12), kind=kLoop, calls=%fused_computation.36 | loop fusion | flops 131072 | bytes 262144 | tf_op jit(solution)/shard_map/convert.2
  63.2 4.5 %collective-permute-done.1 = bf16[8,128,128]{2,1,0:T(8,128)(2,1)S(1)} collective-permute-done((bf16[8,128,128]{2,1,0:T(8,128)(2,1)}, bf16[8,128,128]{2,1,0:T(8,128)(2,1)S(1)}, u32[]{:S(2)}, u32[]{:S(2)}) %collective-permute-start.1) | collective-permute-done | bytes 262176 | tf_op jit(solution)/shard_map/ppermute | solution.py:52
  67.7 5.5 %collective-permute-start.3 = (bf16[8,128,128]{2,1,0:T(8,128)(2,1)S(1)}, bf16[8,128,128]{2,1,0:T(8,128)(2,1)S(1)}, u32[]{:S(2)}, u32[]{:S(2)}) collective-permute-start(bf16[8,128,128]{2,1,0:T(8,128)(2,1)S(1)} %collective-permute-done.1), channel_id=1, source_target_pairs={{0,448},{64,0},{128,64},{192,128},{256,192},{320,256},{384,320},{4... | collective-permute-start | bytes 786440 | tf_op jit(solution)/shard_map/ppermute | solution.py:52
  73.2 1.6 %collective-permute-done = bf16[8,128,128]{2,1,0:T(8,128)(2,1)S(1)} collective-permute-done((bf16[8,128,128]{2,1,0:T(8,128)(2,1)}, bf16[8,128,128]{2,1,0:T(8,128)(2,1)S(1)}, u32[]{:S(2)}, u32[]{:S(2)}) %collective-permute-start) | collective-permute-done | bytes 262176 | tf_op jit(solution)/shard_map/ppermute | solution.py:51
  74.8 1.9 %collective-permute-start.2 = (bf16[8,128,128]{2,1,0:T(8,128)(2,1)S(1)}, bf16[8,128,128]{2,1,0:T(8,128)(2,1)S(1)}, u32[]{:S(2)}, u32[]{:S(2)}) collective-permute-start(bf16[8,128,128]{2,1,0:T(8,128)(2,1)S(1)} %collective-permute-done), channel_id=1, source_target_pairs={{0,64},{64,128},{128,192},{192,256},{256,320},{320,384},{384,448},... | collective-permute-start | bytes 786440 | tf_op jit(solution)/shard_map/ppermute | solution.py:51
  76.8 6.4 %collective-permute-done.3 = bf16[8,128,128]{2,1,0:T(8,128)(2,1)S(1)} collective-permute-done((bf16[8,128,128]{2,1,0:T(8,128)(2,1)S(1)}, bf16[8,128,128]{2,1,0:T(8,128)(2,1)S(1)}, u32[]{:S(2)}, u32[]{:S(2)}) %collective-permute-start.3) | collective-permute-done | bytes 262176 | tf_op jit(solution)/shard_map/ppermute | solution.py:52
  83.2 5.6 %collective-permute-start.5 = (bf16[8,128,128]{2,1,0:T(8,128)(2,1)S(1)}, bf16[8,128,128]{2,1,0:T(8,128)(2,1)S(1)}, u32[]{:S(2)}, u32[]{:S(2)}) collective-permute-start(bf16[8,128,128]{2,1,0:T(8,128)(2,1)S(1)} %collective-permute-done.3), channel_id=1, source_target_pairs={{0,448},{64,0},{128,64},{192,128},{256,192},{320,256},{384,320},{4... | collective-permute-start | bytes 786440 | tf_op jit(solution)/shard_map/ppermute | solution.py:52
  88.8 1.8 %collective-permute-done.2 = bf16[8,128,128]{2,1,0:T(8,128)(2,1)S(1)} collective-permute-done((bf16[8,128,128]{2,1,0:T(8,128)(2,1)S(1)}, bf16[8,128,128]{2,1,0:T(8,128)(2,1)S(1)}, u32[]{:S(2)}, u32[]{:S(2)}) %collective-permute-start.2) | collective-permute-done | bytes 262176 | tf_op jit(solution)/shard_map/ppermute | solution.py:51
  90.7 1.9 %collective-permute-start.4 = (bf16[8,128,128]{2,1,0:T(8,128)(2,1)S(1)}, bf16[8,128,128]{2,1,0:T(8,128)(2,1)S(1)}, u32[]{:S(2)}, u32[]{:S(2)}) collective-permute-start(bf16[8,128,128]{2,1,0:T(8,128)(2,1)S(1)} %collective-permute-done.2), channel_id=1, source_target_pairs={{0,64},{64,128},{128,192},{192,256},{256,320},{320,384},{384,448},... | collective-permute-start | bytes 786440 | tf_op jit(solution)/shard_map/ppermute | solution.py:51
  92.7 4.2 %collective-permute-done.5 = bf16[8,128,128]{2,1,0:T(8,128)(2,1)S(1)} collective-permute-done((bf16[8,128,128]{2,1,0:T(8,128)(2,1)S(1)}, bf16[8,128,128]{2,1,0:T(8,128)(2,1)S(1)}, u32[]{:S(2)}, u32[]{:S(2)}) %collective-permute-start.5) | collective-permute-done | bytes 262176 | tf_op jit(solution)/shard_map/ppermute | solution.py:52
  96.9 5.6 %collective-permute-start.7 = (bf16[4,128,128]{2,1,0:T(8,128)(2,1)S(1)}, bf16[4,128,128]{2,1,0:T(8,128)(2,1)S(1)}, u32[]{:S(2)}, u32[]{:S(2)}) collective-permute-start(bf16[4,128,128]{2,1,0:T(8,128)(2,1)S(1)} %slice.69), channel_id=1, source_target_pairs={{0,448},{64,0},{128,64},{192,128},{256,192},{320,256},{384,320},{4... | collective-permute-start | bytes 393224 | tf_op jit(solution)/shard_map/ppermute | solution.py:59
  102.6 1.9 %collective-permute-start.6 = (bf16[4,128,128]{2,1,0:T(8,128)(2,1)S(1)}, bf16[4,128,128]{2,1,0:T(8,128)(2,1)S(1)}, u32[]{:S(2)}, u32[]{:S(2)}) collective-permute-start(bf16[4,128,128]{2,1,0:T(8,128)(2,1)S(1)} %slice.68), channel_id=1, source_target_pairs={{0,64},{64,128},{128,192},{192,256},{256,320},{320,384},{384,448},... | collective-permute-start | bytes 393224 | tf_op jit(solution)/shard_map/ppermute | solution.py:59
  104.6 6.1 %collective-permute-done.6 = bf16[4,128,128]{2,1,0:T(8,128)(2,1)S(1)} collective-permute-done((bf16[4,128,128]{2,1,0:T(8,128)(2,1)S(1)}, bf16[4,128,128]{2,1,0:T(8,128)(2,1)S(1)}, u32[]{:S(2)}, u32[]{:S(2)}) %collective-permute-start.6) | collective-permute-done | bytes 131104 | tf_op jit(solution)/shard_map/ppermute | solution.py:59
  110.7 1.3 copy-done.2
  112.0 2.5 %gather_fusion = bf16[8,8,128,128]{3,2,1,0:T(8,128)(2,1)S(1)} fusion(bf16[8,8,128,128]{3,2,1,0:T(8,128)(2,1)} %bitcast.47, s32[1024]{0:T(1024)S(1)} %pad_clamp_fusion), kind=kCustom, calls=%fused_computation | custom fusion | bytes 4194336 | tf_op jit(solution)/shard_map/jit(_take)/gather | solution.py:105
  114.6 1.6 %broadcast_select_fusion = bf16[8,8,128,128]{3,2,1,0:T(8,128)(2,1)} fusion(bf16[8,8,128,128]{3,2,1,0:T(8,128)(2,1)S(1)} %gather_fusion, pred[8]{0:T(512)(128)(4,1)S(1)} %compare_and_fusion), kind=kLoop, calls=%fused_computation.23 | loop fusion | flops 1048576 | bytes 4194312 | tf_op jit(solution)/shard_map/jit(_take)/select_n | solution.py:105
  116.2 3.8 %fusion.51 = (f32[2,128]{1,0:T(2,128)S(1)}, f32[1,2,128,8192]{2,3,1,0:T(8,128)S(1)}) fusion(bf16[8192,128,1]{1,0,2:T(8,128)(2,1)} %bitcast.53, bf16[128,2,64]{2,0,1:T(8,128)(2,1)S(1)} %copy-done.10, bf16[128,2,64]{2,0,1:T(8,128)(2,1)S(1)} %copy-done.9, pred[128,8192]{0,1:T(8,128)(4,1)} %fusion.9), kind=kOutput, calls=%fused_computation.103 | convolution fusion | flops 543293184 | bytes 11600896 | tf_op jit(solution)/shard_map/qhgd,khd->hgqk/dot_general | solution.py:113
  119.9 1.7 %fusion.2 = f32[2,128]{1,0:T(2,128)S(1)} fusion(f32[1,2,128,8192]{2,3,1,0:T(8,128)S(1)} %get-tuple-element.15, f32[2,128]{1,0:T(2,128)S(1)} %get-tuple-element.14, pred[128,8192]{0,1:T(8,128)(4,1)S(1)} %copy-done.1), kind=kLoop, calls=%fused_computation.6 | loop fusion | flops 6291200 | bytes 9439232 | tf_op jit(solution)/shard_map/reduce_sum | solution.py:120
  121.6 1.7 %fusion.25 = bf16[2,128,128]{1,2,0:T(8,128)(2,1)S(1)} fusion(bf16[8192,128,1]{1,0,2:T(8,128)(2,1)S(1)} %bitcast.50, f32[1,2,128,8192]{2,3,1,0:T(8,128)S(1)} %get-tuple-element.15, f32[2,128]{1,0:T(2,128)S(1)} %get-tuple-element.14, pred[128,8192]{0,1:T(8,128)(4,1)S(1)} %copy-done.1, f32[2,128]{1,0:T(2,128)S(1)} %fusion.2), kind=kOutput, calls=%fused_computation.30 | convolution fusion | flops 543227904 | bytes 11601920 | tf_op jit(solution)/shard_map/hgqk,khd->hgqd/dot_general | solution.py:121
  123.8 4.3 %all_to_all.15 = bf16[2,4,16,2560]{3,2,1,0:T(8,128)(2,1)S(1)} all-to-all(bf16[2,4,16,2560]{3,2,1,0:T(8,128)(2,1)S(1)} %bitcast.49), channel_id=1, replica_groups=mesh['z'=8,'x'=4,'ylo'=2,'yhi'=4,'core'=2] {'core'}, dimensions={0} | all-to-all | bytes 1310720 | tf_op jit(solution)/shard_map/all_to_all | solution.py:134
  128.1 0.9 reduce_sum.84
  129.0 3.5 %all-to-all-start.2 = ((bf16[4,16,2560]{2,1,0:T(8,128)(2,1)}), bf16[4,16,2560]{2,1,0:T(8,128)(2,1)S(1)}, u32[]{:S(2)}, u32[]{:S(2)}) async-start(bf16[4,16,2560]{2,1,0:T(8,128)(2,1)} %reduce_sum.84), calls=%async_computation.2 | async-start | bytes 655360 | tf_op jit(solution)/shard_map/all_to_all | solution.py:136
  133.2 12.0 %all-to-all-done.2 = bf16[4,16,2560]{2,1,0:T(8,128)(2,1)S(1)} async-done(((bf16[4,16,2560]{2,1,0:T(8,128)(2,1)}), bf16[4,16,2560]{2,1,0:T(8,128)(2,1)S(1)}, u32[]{:S(2)}, u32[]{:S(2)}) %all-to-all-start.2) | async-done | bytes 327712 | tf_op jit(solution)/shard_map/all_to_all | solution.py:136
  (85 shorter events, 6.4 us)
Async XLA Ops:
  7.2 116.2 %copy-start = (bf16[256,2560]{1,0:T(8,128)(2,1)S(1)}, bf16[256,2560]{1,0:T(8,128)(2,1)}, u32[]{:S(2)}) copy-start(bf16[256,2560]{1,0:T(8,128)(2,1)} %param.14) | copy-start | bytes 3932164
  25.9 3.3 %copy-start.13 = (s32[16]{0:T(128)S(1)}, s32[16]{0:T(128)}, u32[]{:S(2)}) copy-start(s32[16]{0:T(128)} %param.17) | copy-start | bytes 196
  25.9 3.7 %copy-start.11 = (f32[128]{0:T(128)S(1)}, f32[128]{0:T(128)}, u32[]{:S(2)}) copy-start(f32[128]{0:T(128)} %param.16) | copy-start | bytes 1540
  29.0 12.1 %copy-start.12 = (f32[128]{0:T(128)S(1)}, f32[128]{0:T(128)}, u32[]{:S(2)}) copy-start(f32[128]{0:T(128)} %param.15) | copy-start | bytes 1540
  29.2 9.5 %copy-start.8 = (bf16[128,128]{1,0:T(8,128)(2,1)}, bf16[128,128]{1,0:T(8,128)(2,1)S(1)}, u32[]{:S(2)}) copy-start(bf16[128,128]{1,0:T(8,128)(2,1)S(1)} %slice.93) | copy-start | bytes 98308
  30.1 0.6 copy-start.4
  30.1 0.6 copy-start.6
  31.6 15.6 %all-to-all-start = ((bf16[8,128,256]{2,1,0:T(8,128)(2,1)}), bf16[8,128,256]{2,1,0:T(8,128)(2,1)}, u32[]{:S(2)}, u32[]{:S(2)}) async-start(bf16[8,128,256]{2,1,0:T(8,128)(2,1)} %broadcast_in_dim.45), calls=%async_computation | async-start | bytes 1048576 | tf_op jit(solution)/shard_map/all_to_all | solution.py:99
  38.7 77.5 %all-gather.2.cloned.1.call-start = ((), (), s32[]{:S(2)}) async-start(), calls=%async_computation.3 | async-start | bytes 2359296 | tf_op jit(solution)/shard_map/all_gather | solution.py:102
  51.2 16.5 %collective-permute-start.1 = (bf16[8,128,128]{2,1,0:T(8,128)(2,1)}, bf16[8,128,128]{2,1,0:T(8,128)(2,1)S(1)}, u32[]{:S(2)}, u32[]{:S(2)}) collective-permute-start(bf16[8,128,128]{2,1,0:T(8,128)(2,1)} %get-tuple-element.5), channel_id=1, source_target_pairs={{0,448},{64,0},{128,64},{192,128},{256,192},{320,256},{384,320},{4... | collective-permute-start | bytes 786440 | tf_op jit(solution)/shard_map/ppermute | solution.py:52
  59.6 15.2 %collective-permute-start = (bf16[8,128,128]{2,1,0:T(8,128)(2,1)}, bf16[8,128,128]{2,1,0:T(8,128)(2,1)S(1)}, u32[]{:S(2)}, u32[]{:S(2)}) collective-permute-start(bf16[8,128,128]{2,1,0:T(8,128)(2,1)} %get-tuple-element.5), channel_id=1, source_target_pairs={{0,64},{64,128},{128,192},{192,256},{256,320},{320,384},{384,448},... | collective-permute-start | bytes 786440 | tf_op jit(solution)/shard_map/ppermute | solution.py:51
  67.7 15.6 %collective-permute-start.3 = (bf16[8,128,128]{2,1,0:T(8,128)(2,1)S(1)}, bf16[8,128,128]{2,1,0:T(8,128)(2,1)S(1)}, u32[]{:S(2)}, u32[]{:S(2)}) collective-permute-start(bf16[8,128,128]{2,1,0:T(8,128)(2,1)S(1)} %collective-permute-done.1), channel_id=1, source_target_pairs={{0,448},{64,0},{128,64},{192,128},{256,192},{320,256},{384,320},{4... | collective-permute-start | bytes 786440 | tf_op jit(solution)/shard_map/ppermute | solution.py:52
  74.8 15.8 %collective-permute-start.2 = (bf16[8,128,128]{2,1,0:T(8,128)(2,1)S(1)}, bf16[8,128,128]{2,1,0:T(8,128)(2,1)S(1)}, u32[]{:S(2)}, u32[]{:S(2)}) collective-permute-start(bf16[8,128,128]{2,1,0:T(8,128)(2,1)S(1)} %collective-permute-done), channel_id=1, source_target_pairs={{0,64},{64,128},{128,192},{192,256},{256,320},{320,384},{384,448},... | collective-permute-start | bytes 786440 | tf_op jit(solution)/shard_map/ppermute | solution.py:51
  83.2 13.7 %collective-permute-start.5 = (bf16[8,128,128]{2,1,0:T(8,128)(2,1)S(1)}, bf16[8,128,128]{2,1,0:T(8,128)(2,1)S(1)}, u32[]{:S(2)}, u32[]{:S(2)}) collective-permute-start(bf16[8,128,128]{2,1,0:T(8,128)(2,1)S(1)} %collective-permute-done.3), channel_id=1, source_target_pairs={{0,448},{64,0},{128,64},{192,128},{256,192},{320,256},{384,320},{4... | collective-permute-start | bytes 786440 | tf_op jit(solution)/shard_map/ppermute | solution.py:52
  90.7 11.9 %collective-permute-start.4 = (bf16[8,128,128]{2,1,0:T(8,128)(2,1)S(1)}, bf16[8,128,128]{2,1,0:T(8,128)(2,1)S(1)}, u32[]{:S(2)}, u32[]{:S(2)}) collective-permute-start(bf16[8,128,128]{2,1,0:T(8,128)(2,1)S(1)} %collective-permute-done.2), channel_id=1, source_target_pairs={{0,64},{64,128},{128,192},{192,256},{256,320},{320,384},{384,448},... | collective-permute-start | bytes 786440 | tf_op jit(solution)/shard_map/ppermute | solution.py:51
  96.9 13.7 %collective-permute-start.7 = (bf16[4,128,128]{2,1,0:T(8,128)(2,1)S(1)}, bf16[4,128,128]{2,1,0:T(8,128)(2,1)S(1)}, u32[]{:S(2)}, u32[]{:S(2)}) collective-permute-start(bf16[4,128,128]{2,1,0:T(8,128)(2,1)S(1)} %slice.69), channel_id=1, source_target_pairs={{0,448},{64,0},{128,64},{192,128},{256,192},{320,256},{384,320},{4... | collective-permute-start | bytes 393224 | tf_op jit(solution)/shard_map/ppermute | solution.py:59
  102.6 8.1 %collective-permute-start.6 = (bf16[4,128,128]{2,1,0:T(8,128)(2,1)S(1)}, bf16[4,128,128]{2,1,0:T(8,128)(2,1)S(1)}, u32[]{:S(2)}, u32[]{:S(2)}) collective-permute-start(bf16[4,128,128]{2,1,0:T(8,128)(2,1)S(1)} %slice.68), channel_id=1, source_target_pairs={{0,64},{64,128},{128,192},{192,256},{256,320},{320,384},{384,448},... | collective-permute-start | bytes 393224 | tf_op jit(solution)/shard_map/ppermute | solution.py:59
  110.7 1.3 copy-start.2
  114.6 1.6 %copy-start.9 = (bf16[128,2,64]{2,0,1:T(8,128)(2,1)S(1)}, bf16[128,2,64]{2,0,1:T(8,128)(2,1)}, u32[]{:S(2)}) copy-start(bf16[128,2,64]{2,0,1:T(8,128)(2,1)} %get-tuple-element.6) | copy-start | bytes 98308
  114.6 1.6 %copy-start.10 = (bf16[128,2,64]{2,0,1:T(8,128)(2,1)S(1)}, bf16[128,2,64]{2,0,1:T(8,128)(2,1)}, u32[]{:S(2)}) copy-start(bf16[128,2,64]{2,0,1:T(8,128)(2,1)} %get-tuple-element.7) | copy-start | bytes 98308
  116.2 3.8 %copy-start.1 = (pred[128,8192]{0,1:T(8,128)(4,1)S(1)}, pred[128,8192]{0,1:T(8,128)(4,1)}, u32[]{:S(2)}) copy-start(pred[128,8192]{0,1:T(8,128)(4,1)} %fusion.9) | copy-start | bytes 3145732
  119.9 1.7 %copy-start.3 = (bf16[8,8,128,128]{3,2,1,0:T(8,128)(2,1)S(1)}, bf16[8,8,128,128]{3,2,1,0:T(8,128)(2,1)}, u32[]{:S(2)}) copy-start(bf16[8,8,128,128]{3,2,1,0:T(8,128)(2,1)} %broadcast_select_fusion) | copy-start | bytes 6291460
  123.8 8.7 %copy-start.5 = (bf16[128,64]{1,0:T(8,128)(2,1)S(1)}, bf16[128,64]{1,0:T(8,128)(2,1)}, u32[]{:S(2)}) copy-start(bf16[128,64]{1,0:T(8,128)(2,1)} %copy-done.4) | copy-start | bytes 49156
  123.8 8.7 %copy-start.7 = (bf16[128,64]{1,0:T(8,128)(2,1)S(1)}, bf16[128,64]{1,0:T(8,128)(2,1)}, u32[]{:S(2)}) copy-start(bf16[128,64]{1,0:T(8,128)(2,1)} %copy-done.6) | copy-start | bytes 49156
  129.0 16.2 %all-to-all-start.2 = ((bf16[4,16,2560]{2,1,0:T(8,128)(2,1)}), bf16[4,16,2560]{2,1,0:T(8,128)(2,1)S(1)}, u32[]{:S(2)}, u32[]{:S(2)}) async-start(bf16[4,16,2560]{2,1,0:T(8,128)(2,1)} %reduce_sum.84), calls=%async_computation.2 | async-start | bytes 655360 | tf_op jit(solution)/shard_map/all_to_all | solution.py:136
Sparse Core Ops, SparseCore 0:
  49.4 50.7 all-gather.1

commit v12 on v5

--- a/solution.py
+++ b/solution.py
@@ -40,26 +40,42 @@
     )
 
 
-def ring_gather(piece, inner, name, stride):
+def ring_pairs(n, k, forward, needed):
+    out = []
+    for src in range(n):
+        if forward:
+            start, dst = (src - (k - 1)) % n, (src + 1) % n
+            reach = [(start + j) % n for j in range(k, n // 2 + 1)]
+        else:
+            start, dst = (src + (k - 1)) % n, (src - 1) % n
+            reach = [(start - j) % n for j in range(k, n // 2 + 1)]
+        if any(needed(start, d) for d in reach):
+            out.append((src, dst))
+    return out
+
+
+def ring_gather(piece, inner, name, stride, needed=lambda p, d: True):
     n = lax.axis_size(name)
     c = lax.axis_index(name)
-    cw = [(i, (i + 1) % n) for i in range(n)]
-    ccw = [(i, (i - 1) % n) for i in range(n)]
     pieces, ids = [piece], [c * stride + inner]
     a = b = piece
     for s in range(1, (n - 1) // 2 + 1):
-        a = lax.ppermute(a, name, cw)
-        b = lax.ppermute(b, name, ccw)
+        a = lax.ppermute(a, name, ring_pairs(n, s, True, needed))
+        b = lax.ppermute(b, name, ring_pairs(n, s, False, needed))
         pieces += [a, b]
         ids += [((c - s) % n) * stride + inner, ((c + s) % n) * stride + inner]
     if n % 2 == 0:
-        far = ((c + n // 2) % n) * stride
+        s = n // 2
+        far = ((c + s) % n) * stride
         m = piece.shape[0]
         if m % 2 == 0:
-            pieces += [lax.ppermute(a[: m // 2], name, cw), lax.ppermute(b[m // 2 :], name, ccw)]
+            pieces += [
+                lax.ppermute(a[: m // 2], name, ring_pairs(n, s, True, needed)),
+                lax.ppermute(b[m // 2 :], name, ring_pairs(n, s, False, needed)),
+            ]
             ids += [far + inner[: m // 2], far + inner[m // 2 :]]
         else:
-            pieces += [lax.ppermute(a, name, cw)]
+            pieces += [lax.ppermute(a, name, ring_pairs(n, s, True, needed))]
             ids += [far + inner]
     return jnp.concatenate(pieces, axis=0), jnp.concatenate(ids, axis=0)
 
@@ -98,7 +114,8 @@
     plane = nx * nlo
     piece = lax.all_to_all(jnp.broadcast_to(piece, (plane,) + piece.shape[1:]), ("x", "ylo"), 0, 0, tiled=True)
     block_ids = jnp.arange(plane, dtype=jnp.int32)
-    piece, block_ids = ring_gather(piece, block_ids, "z", nx * nlo)
+    back = -(-(-(-(max_len - 1) // tokens)) // plane)
+    piece, block_ids = ring_gather(piece, block_ids, "z", plane, lambda p, d: 1 <= d - p <= back)
     span = piece.shape[0] * tokens
     kv_all = piece.reshape(span, 2 * kv_cols)
     key_pos = (block_ids[:, None] * tokens + jnp.arange(tokens, dtype=jnp.int32)[None, :]).reshape(span)

time: 135 us -> 134 us (level)
  starting transfers between devices: 44.9 us -> 40.6 us
  waiting for transfers between devices: 39.6 us -> 43.3 us
    ppermute x8, starting transfers between devices: 33.8 us -> 29.5 us  [the longest x3 18.7 us: ring_gather(): b = lax.ppermute(b, name, ring_pairs(n, s, False, needed))]
    ppermute x8, waiting for transfers between devices: 19.5 us -> 23.2 us  [the longest x3 19.4 us: ring_gather(): b = lax.ppermute(b, name, ring_pairs(n, s, False, needed))]
  transfers between devices with their start and end apart: 10 -> 10, of which waited for: 9 -> 6; matrix products, arithmetic and copies ran while one was open for 9% -> 9% of each run, Pallas kernels for 0% -> 0%
where the time goes in v12:
time: 134 us; the launch traced here: 133 us
  waiting for transfers between devices  43.3 us (32%)
  starting transfers between devices  40.6 us (30%)
  blocking collectives  22.6 us (17%)
  other arithmetic  13 us (10%)
  matrix products  7.09 us (5%)
  local copies, waits for them, and re-layouts  5.14 us (4%)
    ppermute x3, waiting for transfers between devices, ring_gather(): b = lax.ppermute(b, name, ring_pairs(n, s, False, needed))  19.4 us
    ppermute x3, starting transfers between devices, ring_gather(): b = lax.ppermute(b, name, ring_pairs(n, s, False, needed))  18.7 us
    all_gather x1, blocking collectives, on_device(): piece = lax.all_gather(hidden_in, TEN, axis=1, tiled=True)  18.4 us
    all_to_all x1, waiting for transfers between devices, on_device(): part = lax.all_to_all(part, 'yhi', 0, 0, tiled=True)  12 us
    all_to_all x1, waiting for transfers between devices, on_device(): lax.all_to_all(jnp.broadcast_to(piece, (plane,) + piece.shape[1:]), ('x',...  8.13 us
    all_to_all x1, starting transfers between devices, on_device(): lax.all_to_all(jnp.broadcast_to(piece, (plane,) + piece.shape[1:]), ('x',...  6.41 us
    ppermute x1, starting transfers between devices, ring_gather(): lax.ppermute(b[m // 2:], name, ring_pairs(n, s, False, needed))  5.61 us
    all_to_all x1, starting transfers between devices, on_device(): part = lax.all_to_all(part, 'yhi', 0, 0, tiled=True)  4.66 us
  transfers between devices with their start and end apart: 10, of which 6 were waited for; matrix products, arithmetic and copies ran while one was open for 9% of the time, Pallas kernels for 0%

profile of v12, /device:TPU:6, one launch (start us, length us, event | category | flops | bytes accessed | tf_op | source)
XLA Modules:
  0.0 132.8 jit_solution(17906826244866942987)
XLA Ops:
  0.7 18.4 %all_gather.3 = bf16[128,2560]{0,1:T(8,128)(2,1)S(1)} all-gather(bf16[128,320]{0,1:T(8,128)(2,1)} %param.9), channel_id=1, replica_groups=mesh['z'=8,'x'=4,'ylo'=2,'yhi'=4,'core'=2] {'yhi','core'}, dimensions={1}, use_global_device_ids=true | all-gather | bytes 737280 | tf_op jit(solution)/shard_map/all_gather | solution.py:92
  19.4 3.1 %fusion.18 = f32[128,512]{1,0:T(8,128)S(1)} fusion(bf16[2560,128]{1,0:T(8,128)(2,1)} %param.13, bf16[2560,128]{1,0:T(8,128)(2,1)} %param.12, bf16[2560,256]{1,0:T(8,128)(2,1)} %param.11, bf16[128,2560]{0,1:T(8,128)(2,1)S(1)} %all_gather.3, f32[2560]{0:T(1024)} %param.10, f32[128]{0:T(128)S(1)} %add_rsqrt_fusion.2), kind=kOutput, calls=%fused_computation.25 | convolution fusion | flops 344457216 | bytes 3549696 | tf_op jit(solution)/shard_map/dot_general | solution.py:95
  23.6 0.8 broadcast_in_dim.31
  24.5 6.4 %all-to-all-start = ((bf16[8,128,256]{2,1,0:T(8,128)(2,1)}), bf16[8,128,256]{2,1,0:T(8,128)(2,1)S(1)}, u32[]{:S(2)}, u32[]{:S(2)}) async-start(bf16[8,128,256]{2,1,0:T(8,128)(2,1)} %broadcast_in_dim.31), calls=%async_computation | async-start | bytes 1048576 | tf_op jit(solution)/shard_map/all_to_all | solution.py:115
  31.2 8.1 %all-to-all-done = bf16[8,128,256]{2,1,0:T(8,128)(2,1)S(1)} async-done(((bf16[8,128,256]{2,1,0:T(8,128)(2,1)}), bf16[8,128,256]{2,1,0:T(8,128)(2,1)S(1)}, u32[]{:S(2)}, u32[]{:S(2)}) %all-to-all-start) | async-done | bytes 524320 | tf_op jit(solution)/shard_map/all_to_all | solution.py:115
  39.4 3.2 %collective-permute-start = (bf16[8,128,256]{2,1,0:T(8,128)(2,1)S(1)}, bf16[8,128,256]{2,1,0:T(8,128)(2,1)}, u32[]{:S(2)}, u32[]{:S(2)}) collective-permute-start(bf16[8,128,256]{2,1,0:T(8,128)(2,1)S(1)} %all-to-all-done), channel_id=1, source_target_pairs={{0,64},{64,128},{128,192},{192,256},{256,320},{320,384},{384,448},... | collective-permute-start | bytes 1572872 | tf_op jit(solution)/shard_map/ppermute | solution.py:63
  42.5 3.7 %compare_and_fusion = pred[128,8192]{0,1:T(8,128)(4,1)S(1)} fusion(s32[128]{0:T(128)S(1)} %iota_add_fusion, s32[128]{0:T(128)S(1)} %select_reduce_fusion, s32[8192]{0:T(1024)S(1)} %add_bitcast_fusion), kind=kLoop, calls=%fused_computation.11 | loop fusion | flops 3145728 | bytes 1082368 | tf_op jit(solution)/shard_map/and | solution.py:130
  46.2 7.5 %collective-permute-start.1 = (bf16[8,128,256]{2,1,0:T(8,128)(2,1)S(1)}, bf16[8,128,256]{2,1,0:T(8,128)(2,1)}, u32[]{:S(2)}, u32[]{:S(2)}) collective-permute-start(bf16[8,128,256]{2,1,0:T(8,128)(2,1)S(1)} %all-to-all-done), channel_id=1, source_target_pairs={{0,448},{64,0},{128,64},{192,128},{1,449},{65,1},{129,65},{193,129... | collective-permute-start | bytes 1572872 | tf_op jit(solution)/shard_map/ppermute | solution.py:64
  53.8 0.7 reshape.365
  54.5 1.0 multiply_cosine_fusion
  56.2 1.7 %multiply_reduce_fusion = f32[128,2]{1,0:T(8,128)} fusion(f32[128,2,128]{2,1,0:T(2,128)} %reshape.365), kind=kLoop, calls=%fused_computation.34 | loop fusion | flops 65280 | bytes 132096 | tf_op jit(solution)/shard_map/reduce_sum | solution.py:30
  57.9 0.9 copy.33
  58.8 5.5 %collective-permute-done.1 = bf16[8,128,256]{2,1,0:T(8,128)(2,1)} collective-permute-done((bf16[8,128,256]{2,1,0:T(8,128)(2,1)S(1)}, bf16[8,128,256]{2,1,0:T(8,128)(2,1)}, u32[]{:S(2)}, u32[]{:S(2)}) %collective-permute-start.1) | collective-permute-done | bytes 524320 | tf_op jit(solution)/shard_map/ppermute | solution.py:64
  64.3 5.7 %collective-permute-start.3 = (bf16[8,128,256]{2,1,0:T(8,128)(2,1)}, bf16[8,128,256]{2,1,0:T(8,128)(2,1)S(1)}, u32[]{:S(2)}, u32[]{:S(2)}) collective-permute-start(bf16[8,128,256]{2,1,0:T(8,128)(2,1)} %collective-permute-done.1), channel_id=1, source_target_pairs={{0,448},{64,0},{128,64},{448,384},{1,449},{65,1},{129,65},{449,385... | collective-permute-start | bytes 1572872 | tf_op jit(solution)/shard_map/ppermute | solution.py:64
  70.2 0.7 collective-permute-start.4
  70.9 1.0 subtract_convert_fusion
  71.9 8.2 %collective-permute-done.3 = bf16[8,128,256]{2,1,0:T(8,128)(2,1)S(1)} collective-permute-done((bf16[8,128,256]{2,1,0:T(8,128)(2,1)}, bf16[8,128,256]{2,1,0:T(8,128)(2,1)S(1)}, u32[]{:S(2)}, u32[]{:S(2)}) %collective-permute-start.3) | collective-permute-done | bytes 524320 | tf_op jit(solution)/shard_map/ppermute | solution.py:64
  80.0 5.5 %collective-permute-start.5 = (bf16[8,128,256]{2,1,0:T(8,128)(2,1)S(1)}, bf16[8,128,256]{2,1,0:T(8,128)(2,1)S(1)}, u32[]{:S(2)}, u32[]{:S(2)}) collective-permute-start(bf16[8,128,256]{2,1,0:T(8,128)(2,1)S(1)} %collective-permute-done.3), channel_id=1, source_target_pairs={{0,448},{64,0},{384,320},{448,384},{1,449},{65,1},{385,321},{449,3... | collective-permute-start | bytes 1572872 | tf_op jit(solution)/shard_map/ppermute | solution.py:64
  85.6 1.1 constant_dynamic-update-slice_fusion.7
  86.6 1.1 constant_dynamic-update-slice_fusion.6
  88.5 5.8 %collective-permute-done.5 = bf16[8,128,256]{2,1,0:T(8,128)(2,1)S(1)} collective-permute-done((bf16[8,128,256]{2,1,0:T(8,128)(2,1)S(1)}, bf16[8,128,256]{2,1,0:T(8,128)(2,1)S(1)}, u32[]{:S(2)}, u32[]{:S(2)}) %collective-permute-start.5) | collective-permute-done | bytes 524320 | tf_op jit(solution)/shard_map/ppermute | solution.py:64
  94.4 5.6 %collective-permute-start.7 = (bf16[4,128,256]{2,1,0:T(8,128)(2,1)S(1)}, bf16[4,128,256]{2,1,0:T(8,128)(2,1)S(1)}, u32[]{:S(2)}, u32[]{:S(2)}) collective-permute-start(bf16[4,128,256]{2,1,0:T(8,128)(2,1)S(1)} %slice.58), channel_id=1, source_target_pairs={{0,448},{320,256},{384,320},{448,384},{1,449},{321,257},{385,321},... | collective-permute-start | bytes 786440 | tf_op jit(solution)/shard_map/ppermute | solution.py:74
  100.1 3.7 %collective-permute-done.7 = bf16[4,128,256]{2,1,0:T(8,128)(2,1)S(1)} collective-permute-done((bf16[4,128,256]{2,1,0:T(8,128)(2,1)S(1)}, bf16[4,128,256]{2,1,0:T(8,128)(2,1)S(1)}, u32[]{:S(2)}, u32[]{:S(2)}) %collective-permute-start.7) | collective-permute-done | bytes 262176 | tf_op jit(solution)/shard_map/ppermute | solution.py:74
  103.9 1.9 %fusion.47 = (f32[2,128]{1,0:T(2,128)S(1)}, f32[1,2,128,8192]{2,3,1,0:T(8,128)S(1)}) fusion(bf16[128,2,64]{2,0,1:T(8,128)(2,1)S(1)} %get-tuple-element.4, bf16[128,2,64]{2,0,1:T(8,128)(2,1)S(1)} %get-tuple-element.3, bf16[8192,256]{1,0:T(8,128)(2,1)S(1)} %bitcast.55, pred[128,8192]{0,1:T(8,128)(4,1)S(1)} %compare_and_fusion), kind=kOutput, calls=%fused_computation.91 | convolution fusion | flops 543293184 | bytes 11666432 | tf_op jit(solution)/shard_map/qhgd,khd->hgqk/dot_general | solution.py:127
  105.7 1.7 %fusion.2 = f32[2,128]{1,0:T(2,128)S(1)} fusion(f32[1,2,128,8192]{2,3,1,0:T(8,128)S(1)} %get-tuple-element.12, f32[2,128]{1,0:T(2,128)S(1)} %get-tuple-element.11, pred[128,8192]{0,1:T(8,128)(4,1)S(1)} %compare_and_fusion), kind=kLoop, calls=%fused_computation.4 | loop fusion | flops 6291200 | bytes 9439232 | tf_op jit(solution)/shard_map/reduce_sum | solution.py:134
  107.4 1.8 %fusion.24 = bf16[2,128,128]{1,2,0:T(8,128)(2,1)S(1)} fusion(bf16[8192,256]{1,0:T(8,128)(2,1)S(1)} %bitcast.56, f32[1,2,128,8192]{2,3,1,0:T(8,128)S(1)} %get-tuple-element.12, f32[2,128]{1,0:T(2,128)S(1)} %get-tuple-element.11, pred[128,8192]{0,1:T(8,128)(4,1)S(1)} %compare_and_fusion, f32[2,128]{1,0:T(2,128)S(1)} %fusion.2), kind=kOutput, calls=%fused_computation.27 | convolution fusion | flops 543227904 | bytes 11601920 | tf_op jit(solution)/shard_map/hgqk,khd->hgqd/dot_general | solution.py:135
  109.7 4.3 %all_to_all.15 = bf16[2,4,16,2560]{3,2,1,0:T(8,128)(2,1)S(1)} all-to-all(bf16[2,4,16,2560]{3,2,1,0:T(8,128)(2,1)S(1)} %bitcast.53), channel_id=1, replica_groups=mesh['z'=8,'x'=4,'ylo'=2,'yhi'=4,'core'=2] {'core'}, dimensions={0} | all-to-all | bytes 1310720 | tf_op jit(solution)/shard_map/all_to_all | solution.py:148
  113.9 0.9 reduce_sum.84
  114.8 4.7 %all-to-all-start.2 = ((bf16[4,16,2560]{2,1,0:T(8,128)(2,1)}), bf16[4,16,2560]{2,1,0:T(8,128)(2,1)S(1)}, u32[]{:S(2)}, u32[]{:S(2)}) async-start(bf16[4,16,2560]{2,1,0:T(8,128)(2,1)} %reduce_sum.84), calls=%async_computation.2 | async-start | bytes 655360 | tf_op jit(solution)/shard_map/all_to_all | solution.py:150
  119.5 0.7 pad_maximum_fusion.1
  120.2 12.0 %all-to-all-done.2 = bf16[4,16,2560]{2,1,0:T(8,128)(2,1)S(1)} async-done(((bf16[4,16,2560]{2,1,0:T(8,128)(2,1)}), bf16[4,16,2560]{2,1,0:T(8,128)(2,1)S(1)}, u32[]{:S(2)}, u32[]{:S(2)}) %all-to-all-start.2) | async-done | bytes 327712 | tf_op jit(solution)/shard_map/all_to_all | solution.py:150
  132.1 0.7 reduce_sum.85
  (65 shorter events, 3.9 us)
Async XLA Ops:
  0.6 108.6 %copy-start = (bf16[256,2560]{1,0:T(8,128)(2,1)S(1)}, bf16[256,2560]{1,0:T(8,128)(2,1)}, u32[]{:S(2)}) copy-start(bf16[256,2560]{1,0:T(8,128)(2,1)} %param.14) | copy-start | bytes 3932164
  19.0 3.6 %copy-start.8 = (s32[16]{0:T(128)S(1)}, s32[16]{0:T(128)}, u32[]{:S(2)}) copy-start(s32[16]{0:T(128)} %param.17) | copy-start | bytes 196
  19.0 4.1 %copy-start.6 = (f32[128]{0:T(128)S(1)}, f32[128]{0:T(128)}, u32[]{:S(2)}) copy-start(f32[128]{0:T(128)} %param.16) | copy-start | bytes 1540
  22.5 47.6 %copy-start.7 = (f32[128]{0:T(128)S(1)}, f32[128]{0:T(128)}, u32[]{:S(2)}) copy-start(f32[128]{0:T(128)} %param.15) | copy-start | bytes 1540
  22.6 1.9 %copy-start.5 = (bf16[128,128]{1,0:T(8,128)(2,1)}, bf16[128,128]{1,0:T(8,128)(2,1)S(1)}, u32[]{:S(2)}) copy-start(bf16[128,128]{1,0:T(8,128)(2,1)S(1)} %slice.94) | copy-start | bytes 98308
  23.5 0.9 copy-start.1
  23.5 0.9 copy-start.3
  24.5 14.9 %all-to-all-start = ((bf16[8,128,256]{2,1,0:T(8,128)(2,1)}), bf16[8,128,256]{2,1,0:T(8,128)(2,1)S(1)}, u32[]{:S(2)}, u32[]{:S(2)}) async-start(bf16[8,128,256]{2,1,0:T(8,128)(2,1)} %broadcast_in_dim.31), calls=%async_computation | async-start | bytes 1048576 | tf_op jit(solution)/shard_map/all_to_all | solution.py:115
  39.4 16.1 %collective-permute-start = (bf16[8,128,256]{2,1,0:T(8,128)(2,1)S(1)}, bf16[8,128,256]{2,1,0:T(8,128)(2,1)}, u32[]{:S(2)}, u32[]{:S(2)}) collective-permute-start(bf16[8,128,256]{2,1,0:T(8,128)(2,1)S(1)} %all-to-all-done), channel_id=1, source_target_pairs={{0,64},{64,128},{128,192},{192,256},{256,320},{320,384},{384,448},... | collective-permute-start | bytes 1572872 | tf_op jit(solution)/shard_map/ppermute | solution.py:63
  46.2 18.1 %collective-permute-start.1 = (bf16[8,128,256]{2,1,0:T(8,128)(2,1)S(1)}, bf16[8,128,256]{2,1,0:T(8,128)(2,1)}, u32[]{:S(2)}, u32[]{:S(2)}) collective-permute-start(bf16[8,128,256]{2,1,0:T(8,128)(2,1)S(1)} %all-to-all-done), channel_id=1, source_target_pairs={{0,448},{64,0},{128,64},{192,128},{1,449},{65,1},{129,65},{193,129... | collective-permute-start | bytes 1572872 | tf_op jit(solution)/shard_map/ppermute | solution.py:64
  55.5 14.7 %collective-permute-start.2 = (bf16[8,128,256]{2,1,0:T(8,128)(2,1)}, bf16[8,128,256]{2,1,0:T(8,128)(2,1)S(1)}, u32[]{:S(2)}, u32[]{:S(2)}) collective-permute-start(bf16[8,128,256]{2,1,0:T(8,128)(2,1)} %collective-permute-done), channel_id=1, source_target_pairs={{64,128},{128,192},{192,256},{256,320},{320,384},{384,448},{65,129... | collective-permute-start | bytes 1572872 | tf_op jit(solution)/shard_map/ppermute | solution.py:63
  64.3 15.7 %collective-permute-start.3 = (bf16[8,128,256]{2,1,0:T(8,128)(2,1)}, bf16[8,128,256]{2,1,0:T(8,128)(2,1)S(1)}, u32[]{:S(2)}, u32[]{:S(2)}) collective-permute-start(bf16[8,128,256]{2,1,0:T(8,128)(2,1)} %collective-permute-done.1), channel_id=1, source_target_pairs={{0,448},{64,0},{128,64},{448,384},{1,449},{65,1},{129,65},{449,385... | collective-permute-start | bytes 1572872 | tf_op jit(solution)/shard_map/ppermute | solution.py:64
  70.2 17.6 %collective-permute-start.4 = (bf16[8,128,256]{2,1,0:T(8,128)(2,1)S(1)}, bf16[8,128,256]{2,1,0:T(8,128)(2,1)S(1)}, u32[]{:S(2)}, u32[]{:S(2)}) collective-permute-start(bf16[8,128,256]{2,1,0:T(8,128)(2,1)S(1)} %collective-permute-done.2), channel_id=1, source_target_pairs={{128,192},{192,256},{256,320},{320,384},{384,448},{129,193},{193,2... | collective-permute-start | bytes 1572872 | tf_op jit(solution)/shard_map/ppermute | solution.py:63
  80.0 14.3 %collective-permute-start.5 = (bf16[8,128,256]{2,1,0:T(8,128)(2,1)S(1)}, bf16[8,128,256]{2,1,0:T(8,128)(2,1)S(1)}, u32[]{:S(2)}, u32[]{:S(2)}) collective-permute-start(bf16[8,128,256]{2,1,0:T(8,128)(2,1)S(1)} %collective-permute-done.3), channel_id=1, source_target_pairs={{0,448},{64,0},{384,320},{448,384},{1,449},{65,1},{385,321},{449,3... | collective-permute-start | bytes 1572872 | tf_op jit(solution)/shard_map/ppermute | solution.py:64
  87.8 12.3 %collective-permute-start.6 = (bf16[4,128,256]{2,1,0:T(8,128)(2,1)S(1)}, bf16[4,128,256]{2,1,0:T(8,128)(2,1)S(1)}, u32[]{:S(2)}, u32[]{:S(2)}) collective-permute-start(bf16[4,128,256]{2,1,0:T(8,128)(2,1)S(1)} %slice.57), channel_id=1, source_target_pairs={{192,256},{256,320},{320,384},{384,448},{193,257},{257,321},{321,3... | collective-permute-start | bytes 786440 | tf_op jit(solution)/shard_map/ppermute | solution.py:73
  94.4 9.5 %collective-permute-start.7 = (bf16[4,128,256]{2,1,0:T(8,128)(2,1)S(1)}, bf16[4,128,256]{2,1,0:T(8,128)(2,1)S(1)}, u32[]{:S(2)}, u32[]{:S(2)}) collective-permute-start(bf16[4,128,256]{2,1,0:T(8,128)(2,1)S(1)} %slice.58), channel_id=1, source_target_pairs={{0,448},{320,256},{384,320},{448,384},{1,449},{321,257},{385,321},... | collective-permute-start | bytes 786440 | tf_op jit(solution)/shard_map/ppermute | solution.py:74
  109.2 10.3 %copy-start.2 = (bf16[128,64]{1,0:T(8,128)(2,1)S(1)}, bf16[128,64]{1,0:T(8,128)(2,1)}, u32[]{:S(2)}) copy-start(bf16[128,64]{1,0:T(8,128)(2,1)} %copy-done.1) | copy-start | bytes 49156
  109.2 10.3 %copy-start.4 = (bf16[128,64]{1,0:T(8,128)(2,1)S(1)}, bf16[128,64]{1,0:T(8,128)(2,1)}, u32[]{:S(2)}) copy-start(bf16[128,64]{1,0:T(8,128)(2,1)} %copy-done.3) | copy-start | bytes 49156
  114.8 17.3 %all-to-all-start.2 = ((bf16[4,16,2560]{2,1,0:T(8,128)(2,1)}), bf16[4,16,2560]{2,1,0:T(8,128)(2,1)S(1)}, u32[]{:S(2)}, u32[]{:S(2)}) async-start(bf16[4,16,2560]{2,1,0:T(8,128)(2,1)} %reduce_sum.84), calls=%async_computation.2 | async-start | bytes 655360 | tf_op jit(solution)/shard_map/all_to_all | solution.py:150

commit v13 on v12

--- a/solution.py
+++ b/solution.py
@@ -59,6 +59,20 @@
     c = lax.axis_index(name)
     pieces, ids = [piece], [c * stride + inner]
     a = b = piece
+    if n % 2 == 0 and n >= 4:
+        last = n // 2 - 1
+        held = a
+        for s in range(1, last + 1):
+            if s == last:
+                hop2 = [(src, (src + 2) % n) for src in range(n) if needed((src - (last - 1)) % n, (src + 2) % n)]
+                pieces.append(lax.ppermute(held, name, hop2))
+                ids.append(((c + n // 2) % n) * stride + inner)
+            a = lax.ppermute(a, name, ring_pairs(n, s, True, needed))
+            b = lax.ppermute(b, name, ring_pairs(n, s, False, needed))
+            held = a
+            pieces += [a, b]
+            ids += [((c - s) % n) * stride + inner, ((c + s) % n) * stride + inner]
+        return jnp.concatenate(pieces, axis=0), jnp.concatenate(ids, axis=0)
     for s in range(1, (n - 1) // 2 + 1):
         a = lax.ppermute(a, name, ring_pairs(n, s, True, needed))
         b = lax.ppermute(b, name, ring_pairs(n, s, False, needed))

time: 134 us -> 136 us (1.015)
  the two profiles are of different devices: /device:TPU:6 before, /device:TPU:264 now
where the time goes in v13:
time: 136 us; the launch traced here: 135 us
  waiting for transfers between devices  66 us (49%)
  starting transfers between devices  24 us (18%)
  blocking collectives  21.6 us (16%)
  other arithmetic  11.4 us (8%)
  matrix products  7.09 us (5%)
  local copies, waits for them, and re-layouts  4.06 us (3%)
    ppermute x3, waiting for transfers between devices, ring_gather(): a = lax.ppermute(a, name, ring_pairs(n, s, True, needed))  37 us
    all_gather x1, blocking collectives, on_device(): piece = lax.all_gather(hidden_in, TEN, axis=1, tiled=True)  17.3 us
    all_to_all x1, waiting for transfers between devices, on_device(): part = lax.all_to_all(part, 'yhi', 0, 0, tiled=True)  12.3 us
    ppermute x1, waiting for transfers between devices, ring_gather(): pieces.append(lax.ppermute(held, name, hop2))  11.2 us
    ppermute x3, starting transfers between devices, ring_gather(): a = lax.ppermute(a, name, ring_pairs(n, s, True, needed))  9.18 us
    all_to_all x1, starting transfers between devices, on_device(): lax.all_to_all(jnp.broadcast_to(piece, (plane,) + piece.shape[1:]), ('x',...  5.79 us
    all_to_all x1, waiting for transfers between devices, on_device(): lax.all_to_all(jnp.broadcast_to(piece, (plane,) + piece.shape[1:]), ('x',...  5.51 us
    all_to_all x1, starting transfers between devices, on_device(): part = lax.all_to_all(part, 'yhi', 0, 0, tiled=True)  5.02 us
  transfers between devices with their start and end apart: 9, of which 6 were waited for; matrix products, arithmetic and copies ran while one was open for 7% of the time, Pallas kernels for 0%

profile of v13, /device:TPU:264, one launch (start us, length us, event | category | flops | bytes accessed | tf_op | source)
XLA Modules:
  0.0 135.1 jit_solution(6527316639384123122)
XLA Ops:
  0.7 17.3 %all_gather.3 = bf16[128,2560]{0,1:T(8,128)(2,1)S(1)} all-gather(bf16[128,320]{0,1:T(8,128)(2,1)} %param.9), channel_id=1, replica_groups=mesh['z'=8,'x'=4,'ylo'=2,'yhi'=4,'core'=2] {'yhi','core'}, dimensions={1}, use_global_device_ids=true | all-gather | bytes 737280 | tf_op jit(solution)/shard_map/all_gather | solution.py:106
  18.0 0.4 fusion.17
  18.3 3.1 %fusion.18 = f32[128,512]{1,0:T(8,128)S(1)} fusion(bf16[2560,128]{1,0:T(8,128)(2,1)} %param.13, bf16[2560,128]{1,0:T(8,128)(2,1)} %param.12, bf16[2560,256]{1,0:T(8,128)(2,1)} %param.11, bf16[128,2560]{0,1:T(8,128)(2,1)S(1)} %all_gather.3, f32[2560]{0:T(1024)} %param.10, f32[128]{0:T(128)S(1)} %add_rsqrt_fusion.2), kind=kOutput, calls=%fused_computation.25 | convolution fusion | flops 344457216 | bytes 3549696 | tf_op jit(solution)/shard_map/dot_general | solution.py:109
  22.6 0.8 broadcast_in_dim.31
  23.4 5.8 %all-to-all-start = ((bf16[8,128,256]{2,1,0:T(8,128)(2,1)}), bf16[8,128,256]{2,1,0:T(8,128)(2,1)S(1)}, u32[]{:S(2)}, u32[]{:S(2)}) async-start(bf16[8,128,256]{2,1,0:T(8,128)(2,1)} %broadcast_in_dim.31), calls=%async_computation | async-start | bytes 1048576 | tf_op jit(solution)/shard_map/all_to_all | solution.py:129
  29.4 3.7 %compare_and_fusion = pred[128,8192]{0,1:T(8,128)(4,1)S(1)} fusion(s32[128]{0:T(128)S(1)} %iota_add_fusion, s32[128]{0:T(128)S(1)} %select_reduce_fusion, s32[8192]{0:T(1024)S(1)} %add_bitcast_fusion), kind=kLoop, calls=%fused_computation.11 | loop fusion | flops 3145728 | bytes 1082368 | tf_op jit(solution)/shard_map/and | solution.py:144
  33.1 5.5 %all-to-all-done = bf16[8,128,256]{2,1,0:T(8,128)(2,1)S(1)} async-done(((bf16[8,128,256]{2,1,0:T(8,128)(2,1)}), bf16[8,128,256]{2,1,0:T(8,128)(2,1)S(1)}, u32[]{:S(2)}, u32[]{:S(2)}) %all-to-all-start) | async-done | bytes 524320 | tf_op jit(solution)/shard_map/all_to_all | solution.py:129
  38.7 3.4 %collective-permute-start = (bf16[8,128,256]{2,1,0:T(8,128)(2,1)S(1)}, bf16[8,128,256]{2,1,0:T(8,128)(2,1)}, u32[]{:S(2)}, u32[]{:S(2)}) collective-permute-start(bf16[8,128,256]{2,1,0:T(8,128)(2,1)S(1)} %all-to-all-done), channel_id=1, source_target_pairs={{0,64},{64,128},{128,192},{192,256},{256,320},{320,384},{384,448},... | collective-permute-start | bytes 1572872 | tf_op jit(solution)/shard_map/ppermute | solution.py:70
  42.1 0.7 reshape.357
  42.8 0.7 collective-permute-start.1
  43.5 1.7 %multiply_reduce_fusion = f32[128,2]{1,0:T(8,128)} fusion(f32[128,2,128]{2,1,0:T(2,128)} %reshape.357), kind=kLoop, calls=%fused_computation.34 | loop fusion | flops 65280 | bytes 132096 | tf_op jit(solution)/shard_map/reduce_sum | solution.py:30
  45.2 0.9 copy.33
  46.1 8.6 %collective-permute-done = bf16[8,128,256]{2,1,0:T(8,128)(2,1)} collective-permute-done((bf16[8,128,256]{2,1,0:T(8,128)(2,1)S(1)}, bf16[8,128,256]{2,1,0:T(8,128)(2,1)}, u32[]{:S(2)}, u32[]{:S(2)}) %collective-permute-start) | collective-permute-done | bytes 524320 | tf_op jit(solution)/shard_map/ppermute | solution.py:70
  54.7 2.1 %collective-permute-start.2 = (bf16[8,128,256]{2,1,0:T(8,128)(2,1)}, bf16[8,128,256]{2,1,0:T(8,128)(2,1)S(1)}, u32[]{:S(2)}, u32[]{:S(2)}) collective-permute-start(bf16[8,128,256]{2,1,0:T(8,128)(2,1)} %collective-permute-done), channel_id=1, source_target_pairs={{64,128},{128,192},{192,256},{256,320},{320,384},{384,448},{65,129... | collective-permute-start | bytes 1572872 | tf_op jit(solution)/shard_map/ppermute | solution.py:70
  57.0 0.7 collective-permute-start.3
  58.1 11.9 %collective-permute-done.2 = bf16[8,128,256]{2,1,0:T(8,128)(2,1)S(1)} collective-permute-done((bf16[8,128,256]{2,1,0:T(8,128)(2,1)}, bf16[8,128,256]{2,1,0:T(8,128)(2,1)S(1)}, u32[]{:S(2)}, u32[]{:S(2)}) %collective-permute-start.2) | collective-permute-done | bytes 524320 | tf_op jit(solution)/shard_map/ppermute | solution.py:70
  70.0 1.9 %collective-permute-start.4 = (bf16[8,128,256]{2,1,0:T(8,128)(2,1)S(1)}, bf16[8,128,256]{2,1,0:T(8,128)(2,1)S(1)}, u32[]{:S(2)}, u32[]{:S(2)}) collective-permute-start(bf16[8,128,256]{2,1,0:T(8,128)(2,1)S(1)} %collective-permute-done.2), channel_id=1, source_target_pairs={{128,256},{192,320},{256,384},{320,448},{129,257},{193,321},{257,3... | collective-permute-start | bytes 1572872 | tf_op jit(solution)/shard_map/ppermute | solution.py:68
  71.9 3.7 %collective-permute-start.5 = (bf16[8,128,256]{2,1,0:T(8,128)(2,1)S(1)}, bf16[8,128,256]{2,1,0:T(8,128)(2,1)S(1)}, u32[]{:S(2)}, u32[]{:S(2)}) collective-permute-start(bf16[8,128,256]{2,1,0:T(8,128)(2,1)S(1)} %collective-permute-done.2), channel_id=1, source_target_pairs={{128,192},{192,256},{256,320},{320,384},{384,448},{129,193},{193,2... | collective-permute-start | bytes 1572872 | tf_op jit(solution)/shard_map/ppermute | solution.py:70
  75.6 1.1 constant_dynamic-update-slice_fusion.6
  76.7 0.7 collective-permute-start.6
  77.5 11.2 %collective-permute-done.4 = bf16[8,128,256]{2,1,0:T(8,128)(2,1)S(1)} collective-permute-done((bf16[8,128,256]{2,1,0:T(8,128)(2,1)S(1)}, bf16[8,128,256]{2,1,0:T(8,128)(2,1)S(1)}, u32[]{:S(2)}, u32[]{:S(2)}) %collective-permute-start.4) | collective-permute-done | bytes 524320 | tf_op jit(solution)/shard_map/ppermute | solution.py:68
  88.8 16.5 %collective-permute-done.5 = bf16[8,128,256]{2,1,0:T(8,128)(2,1)S(1)} collective-permute-done((bf16[8,128,256]{2,1,0:T(8,128)(2,1)S(1)}, bf16[8,128,256]{2,1,0:T(8,128)(2,1)S(1)}, u32[]{:S(2)}, u32[]{:S(2)}) %collective-permute-start.5) | collective-permute-done | bytes 524320 | tf_op jit(solution)/shard_map/ppermute | solution.py:70
  105.4 1.9 %fusion.47 = (f32[2,128]{1,0:T(2,128)S(1)}, f32[1,2,128,8192]{2,3,1,0:T(8,128)S(1)}) fusion(bf16[128,2,64]{2,0,1:T(8,128)(2,1)S(1)} %get-tuple-element.4, bf16[128,2,64]{2,0,1:T(8,128)(2,1)S(1)} %get-tuple-element.3, bf16[8192,256]{1,0:T(8,128)(2,1)S(1)} %bitcast.55, pred[128,8192]{0,1:T(8,128)(4,1)S(1)} %compare_and_fusion), kind=kOutput, calls=%fused_computation.89 | convolution fusion | flops 543293184 | bytes 11666432 | tf_op jit(solution)/shard_map/qhgd,khd->hgqk/dot_general | solution.py:141
  107.3 1.7 %fusion.2 = f32[2,128]{1,0:T(2,128)S(1)} fusion(f32[1,2,128,8192]{2,3,1,0:T(8,128)S(1)} %get-tuple-element.12, f32[2,128]{1,0:T(2,128)S(1)} %get-tuple-element.11, pred[128,8192]{0,1:T(8,128)(4,1)S(1)} %compare_and_fusion), kind=kLoop, calls=%fused_computation.4 | loop fusion | flops 6291200 | bytes 9439232 | tf_op jit(solution)/shard_map/reduce_sum | solution.py:148
  109.0 1.8 %fusion.24 = bf16[2,128,128]{1,2,0:T(8,128)(2,1)S(1)} fusion(bf16[8192,256]{1,0:T(8,128)(2,1)S(1)} %bitcast.56, f32[1,2,128,8192]{2,3,1,0:T(8,128)S(1)} %get-tuple-element.12, f32[2,128]{1,0:T(2,128)S(1)} %get-tuple-element.11, pred[128,8192]{0,1:T(8,128)(4,1)S(1)} %compare_and_fusion, f32[2,128]{1,0:T(2,128)S(1)} %fusion.2), kind=kOutput, calls=%fused_computation.27 | convolution fusion | flops 543227904 | bytes 11601920 | tf_op jit(solution)/shard_map/hgqk,khd->hgqd/dot_general | solution.py:149
  110.8 0.4 convolution_convert_fusion
  111.2 4.3 %all_to_all.15 = bf16[2,4,16,2560]{3,2,1,0:T(8,128)(2,1)S(1)} all-to-all(bf16[2,4,16,2560]{3,2,1,0:T(8,128)(2,1)S(1)} %bitcast.53), channel_id=1, replica_groups=mesh['z'=8,'x'=4,'ylo'=2,'yhi'=4,'core'=2] {'core'}, dimensions={0} | all-to-all | bytes 1310720 | tf_op jit(solution)/shard_map/all_to_all | solution.py:162
  115.5 0.9 reduce_sum.84
  116.4 5.0 %all-to-all-start.2 = ((bf16[4,16,2560]{2,1,0:T(8,128)(2,1)}), bf16[4,16,2560]{2,1,0:T(8,128)(2,1)S(1)}, u32[]{:S(2)}, u32[]{:S(2)}) async-start(bf16[4,16,2560]{2,1,0:T(8,128)(2,1)} %reduce_sum.84), calls=%async_computation.2 | async-start | bytes 655360 | tf_op jit(solution)/shard_map/all_to_all | solution.py:164
  121.4 0.7 pad_maximum_fusion.1
  122.1 12.3 %all-to-all-done.2 = bf16[4,16,2560]{2,1,0:T(8,128)(2,1)S(1)} async-done(((bf16[4,16,2560]{2,1,0:T(8,128)(2,1)}), bf16[4,16,2560]{2,1,0:T(8,128)(2,1)S(1)}, u32[]{:S(2)}, u32[]{:S(2)}) %all-to-all-start.2) | async-done | bytes 327712 | tf_op jit(solution)/shard_map/all_to_all | solution.py:164
  134.4 0.7 reduce_sum.85
  (57 shorter events, 2.1 us)
Async XLA Ops:
  0.6 110.2 %copy-start = (bf16[256,2560]{1,0:T(8,128)(2,1)S(1)}, bf16[256,2560]{1,0:T(8,128)(2,1)}, u32[]{:S(2)}) copy-start(bf16[256,2560]{1,0:T(8,128)(2,1)} %param.14) | copy-start | bytes 3932164
  18.0 3.6 %copy-start.8 = (s32[16]{0:T(128)S(1)}, s32[16]{0:T(128)}, u32[]{:S(2)}) copy-start(s32[16]{0:T(128)} %param.17) | copy-start | bytes 196
  18.0 4.1 %copy-start.6 = (f32[128]{0:T(128)S(1)}, f32[128]{0:T(128)}, u32[]{:S(2)}) copy-start(f32[128]{0:T(128)} %param.16) | copy-start | bytes 1540
  21.4 35.4 %copy-start.7 = (f32[128]{0:T(128)S(1)}, f32[128]{0:T(128)}, u32[]{:S(2)}) copy-start(f32[128]{0:T(128)} %param.15) | copy-start | bytes 1540
  21.6 1.9 %copy-start.5 = (bf16[128,128]{1,0:T(8,128)(2,1)}, bf16[128,128]{1,0:T(8,128)(2,1)S(1)}, u32[]{:S(2)}) copy-start(bf16[128,128]{1,0:T(8,128)(2,1)S(1)} %slice.74) | copy-start | bytes 98308
  22.5 0.9 copy-start.1
  22.5 0.9 copy-start.3
  23.4 15.2 %all-to-all-start = ((bf16[8,128,256]{2,1,0:T(8,128)(2,1)}), bf16[8,128,256]{2,1,0:T(8,128)(2,1)S(1)}, u32[]{:S(2)}, u32[]{:S(2)}) async-start(bf16[8,128,256]{2,1,0:T(8,128)(2,1)} %broadcast_in_dim.31), calls=%async_computation | async-start | bytes 1048576 | tf_op jit(solution)/shard_map/all_to_all | solution.py:129
  38.7 16.0 %collective-permute-start = (bf16[8,128,256]{2,1,0:T(8,128)(2,1)S(1)}, bf16[8,128,256]{2,1,0:T(8,128)(2,1)}, u32[]{:S(2)}, u32[]{:S(2)}) collective-permute-start(bf16[8,128,256]{2,1,0:T(8,128)(2,1)S(1)} %all-to-all-done), channel_id=1, source_target_pairs={{0,64},{64,128},{128,192},{192,256},{256,320},{320,384},{384,448},... | collective-permute-start | bytes 1572872 | tf_op jit(solution)/shard_map/ppermute | solution.py:70
  42.8 14.2 %collective-permute-start.1 = (bf16[8,128,256]{2,1,0:T(8,128)(2,1)S(1)}, bf16[8,128,256]{2,1,0:T(8,128)(2,1)S(1)}, u32[]{:S(2)}, u32[]{:S(2)}) collective-permute-start(bf16[8,128,256]{2,1,0:T(8,128)(2,1)S(1)} %all-to-all-done), channel_id=1, source_target_pairs={{0,448},{64,0},{128,64},{192,128},{1,449},{65,1},{129,65},{193,129... | collective-permute-start | bytes 1572872 | tf_op jit(solution)/shard_map/ppermute | solution.py:71
  54.7 15.3 %collective-permute-start.2 = (bf16[8,128,256]{2,1,0:T(8,128)(2,1)}, bf16[8,128,256]{2,1,0:T(8,128)(2,1)S(1)}, u32[]{:S(2)}, u32[]{:S(2)}) collective-permute-start(bf16[8,128,256]{2,1,0:T(8,128)(2,1)} %collective-permute-done), channel_id=1, source_target_pairs={{64,128},{128,192},{192,256},{256,320},{320,384},{384,448},{65,129... | collective-permute-start | bytes 1572872 | tf_op jit(solution)/shard_map/ppermute | solution.py:70
  57.0 19.7 %collective-permute-start.3 = (bf16[8,128,256]{2,1,0:T(8,128)(2,1)S(1)}, bf16[8,128,256]{2,1,0:T(8,128)(2,1)S(1)}, u32[]{:S(2)}, u32[]{:S(2)}) collective-permute-start(bf16[8,128,256]{2,1,0:T(8,128)(2,1)S(1)} %collective-permute-done.1), channel_id=1, source_target_pairs={{0,448},{64,0},{128,64},{448,384},{1,449},{65,1},{129,65},{449,385... | collective-permute-start | bytes 1572872 | tf_op jit(solution)/shard_map/ppermute | solution.py:71
  70.0 18.8 %collective-permute-start.4 = (bf16[8,128,256]{2,1,0:T(8,128)(2,1)S(1)}, bf16[8,128,256]{2,1,0:T(8,128)(2,1)S(1)}, u32[]{:S(2)}, u32[]{:S(2)}) collective-permute-start(bf16[8,128,256]{2,1,0:T(8,128)(2,1)S(1)} %collective-permute-done.2), channel_id=1, source_target_pairs={{128,256},{192,320},{256,384},{320,448},{129,257},{193,321},{257,3... | collective-permute-start | bytes 1572872 | tf_op jit(solution)/shard_map/ppermute | solution.py:68
  71.9 33.4 %collective-permute-start.5 = (bf16[8,128,256]{2,1,0:T(8,128)(2,1)S(1)}, bf16[8,128,256]{2,1,0:T(8,128)(2,1)S(1)}, u32[]{:S(2)}, u32[]{:S(2)}) collective-permute-start(bf16[8,128,256]{2,1,0:T(8,128)(2,1)S(1)} %collective-permute-done.2), channel_id=1, source_target_pairs={{128,192},{192,256},{256,320},{320,384},{384,448},{129,193},{193,2... | collective-permute-start | bytes 1572872 | tf_op jit(solution)/shard_map/ppermute | solution.py:70
  76.7 28.7 %collective-permute-start.6 = (bf16[8,128,256]{2,1,0:T(8,128)(2,1)S(1)}, bf16[8,128,256]{2,1,0:T(8,128)(2,1)S(1)}, u32[]{:S(2)}, u32[]{:S(2)}) collective-permute-start(bf16[8,128,256]{2,1,0:T(8,128)(2,1)S(1)} %collective-permute-done.3), channel_id=1, source_target_pairs={{0,448},{64,0},{384,320},{448,384},{1,449},{65,1},{385,321},{449,3... | collective-permute-start | bytes 1572872 | tf_op jit(solution)/shard_map/ppermute | solution.py:71
  110.8 10.6 %copy-start.2 = (bf16[128,64]{1,0:T(8,128)(2,1)S(1)}, bf16[128,64]{1,0:T(8,128)(2,1)}, u32[]{:S(2)}) copy-start(bf16[128,64]{1,0:T(8,128)(2,1)} %copy-done.1) | copy-start | bytes 49156
  110.8 10.6 %copy-start.4 = (bf16[128,64]{1,0:T(8,128)(2,1)S(1)}, bf16[128,64]{1,0:T(8,128)(2,1)}, u32[]{:S(2)}) copy-start(bf16[128,64]{1,0:T(8,128)(2,1)} %copy-done.3) | copy-start | bytes 49156
  116.4 18.0 %all-to-all-start.2 = ((bf16[4,16,2560]{2,1,0:T(8,128)(2,1)}), bf16[4,16,2560]{2,1,0:T(8,128)(2,1)S(1)}, u32[]{:S(2)}, u32[]{:S(2)}) async-start(bf16[4,16,2560]{2,1,0:T(8,128)(2,1)} %reduce_sum.84), calls=%async_computation.2 | async-start | bytes 655360 | tf_op jit(solution)/shard_map/all_to_all | solution.py:164

commit v14 on v13

--- a/solution.py
+++ b/solution.py
@@ -61,15 +61,20 @@
     a = b = piece
     if n % 2 == 0 and n >= 4:
         last = n // 2 - 1
-        held = a
+        m = piece.shape[0]
+        half = m // 2 if m % 2 == 0 else m
         for s in range(1, last + 1):
             if s == last:
-                hop2 = [(src, (src + 2) % n) for src in range(n) if needed((src - (last - 1)) % n, (src + 2) % n)]
-                pieces.append(lax.ppermute(held, name, hop2))
-                ids.append(((c + n // 2) % n) * stride + inner)
+                far = ((c + n // 2) % n) * stride
+                ahead = [(src, (src + 2) % n) for src in range(n) if needed((src - (last - 1)) % n, (src + 2) % n)]
+                pieces.append(lax.ppermute(a[:half], name, ahead))
+                ids.append(far + inner[:half])
+                if half < m:
+                    behind = [(src, (src - 2) % n) for src in range(n) if needed((src + (last - 1)) % n, (src - 2) % n)]
+                    pieces.append(lax.ppermute(b[half:], name, behind))
+                    ids.append(far + inner[half:])
             a = lax.ppermute(a, name, ring_pairs(n, s, True, needed))
             b = lax.ppermute(b, name, ring_pairs(n, s, False, needed))
-            held = a
             pieces += [a, b]
             ids += [((c - s) % n) * stride + inner, ((c + s) % n) * stride + inner]
         return jnp.concatenate(pieces, axis=0), jnp.concatenate(ids, axis=0)

time: 136 us -> 134 us (0.985)
  the two profiles are of different devices: /device:TPU:264 before, /device:TPU:6 now
where the time goes in v14:
time: 134 us; the launch traced here: 132 us
  waiting for transfers between devices  49.3 us (37%)
  starting transfers between devices  37.4 us (28%)
  blocking collectives  22.6 us (17%)
  other arithmetic  11.4 us (9%)
  matrix products  7.1 us (5%)
  local copies, waits for them, and re-layouts  3.07 us (2%)
    ppermute x3, waiting for transfers between devices, ring_gather(): b = lax.ppermute(b, name, ring_pairs(n, s, False, needed))  26.3 us
    all_gather x1, blocking collectives, on_device(): piece = lax.all_gather(hidden_in, TEN, axis=1, tiled=True)  18.4 us
    ppermute x3, starting transfers between devices, ring_gather(): b = lax.ppermute(b, name, ring_pairs(n, s, False, needed))  17.7 us
    all_to_all x1, waiting for transfers between devices, on_device(): part = lax.all_to_all(part, 'yhi', 0, 0, tiled=True)  12 us
    ppermute x1, waiting for transfers between devices, ring_gather(): pieces.append(lax.ppermute(b[half:], name, behind))  7.3 us
    all_to_all x1, starting transfers between devices, on_device(): lax.all_to_all(jnp.broadcast_to(piece, (plane,) + piece.shape[1:]), ('x',...  6.41 us
    all_to_all x1, starting transfers between devices, on_device(): part = lax.all_to_all(part, 'yhi', 0, 0, tiled=True)  4.66 us
    all_to_all x1, blocking collectives, on_device(): part = lax.all_to_all(part, 'core', 0, 0, tiled=True)  4.26 us
  transfers between devices with their start and end apart: 10, of which 6 were waited for; matrix products, arithmetic and copies ran while one was open for 7% of the time, Pallas kernels for 0%

profile of v14, /device:TPU:6, one launch (start us, length us, event | category | flops | bytes accessed | tf_op | source)
XLA Modules:
  0.0 132.0 jit_solution(4842833008063111337)
XLA Ops:
  0.7 18.4 %all_gather.3 = bf16[128,2560]{0,1:T(8,128)(2,1)S(1)} all-gather(bf16[128,320]{0,1:T(8,128)(2,1)} %param.9), channel_id=1, replica_groups=mesh['z'=8,'x'=4,'ylo'=2,'yhi'=4,'core'=2] {'yhi','core'}, dimensions={1}, use_global_device_ids=true | all-gather | bytes 737280 | tf_op jit(solution)/shard_map/all_gather | solution.py:111
  19.0 0.4 fusion.17
  19.4 3.1 %fusion.18 = f32[128,512]{1,0:T(8,128)S(1)} fusion(bf16[2560,128]{1,0:T(8,128)(2,1)} %param.13, bf16[2560,128]{1,0:T(8,128)(2,1)} %param.12, bf16[2560,256]{1,0:T(8,128)(2,1)} %param.11, bf16[128,2560]{0,1:T(8,128)(2,1)S(1)} %all_gather.3, f32[2560]{0:T(1024)} %param.10, f32[128]{0:T(128)S(1)} %add_rsqrt_fusion.2), kind=kOutput, calls=%fused_computation.25 | convolution fusion | flops 344457216 | bytes 3549696 | tf_op jit(solution)/shard_map/dot_general | solution.py:114
  23.6 0.8 broadcast_in_dim.31
  24.5 6.4 %all-to-all-start = ((bf16[8,128,256]{2,1,0:T(8,128)(2,1)}), bf16[8,128,256]{2,1,0:T(8,128)(2,1)S(1)}, u32[]{:S(2)}, u32[]{:S(2)}) async-start(bf16[8,128,256]{2,1,0:T(8,128)(2,1)} %broadcast_in_dim.31), calls=%async_computation | async-start | bytes 1048576 | tf_op jit(solution)/shard_map/all_to_all | solution.py:134
  31.3 0.7 reshape.365
  32.0 3.7 %compare_and_fusion = pred[128,8192]{0,1:T(8,128)(4,1)S(1)} fusion(s32[128]{0:T(128)S(1)} %iota_add_fusion, s32[128]{0:T(128)S(1)} %select_reduce_fusion, s32[8192]{0:T(1024)S(1)} %add_bitcast_fusion), kind=kLoop, calls=%fused_computation.11 | loop fusion | flops 3145728 | bytes 1082368 | tf_op jit(solution)/shard_map/and | solution.py:149
  35.7 3.6 %all-to-all-done = bf16[8,128,256]{2,1,0:T(8,128)(2,1)S(1)} async-done(((bf16[8,128,256]{2,1,0:T(8,128)(2,1)}), bf16[8,128,256]{2,1,0:T(8,128)(2,1)S(1)}, u32[]{:S(2)}, u32[]{:S(2)}) %all-to-all-start) | async-done | bytes 524320 | tf_op jit(solution)/shard_map/all_to_all | solution.py:134
  39.4 2.4 %collective-permute-start = (bf16[8,128,256]{2,1,0:T(8,128)(2,1)S(1)}, bf16[8,128,256]{2,1,0:T(8,128)(2,1)S(1)}, u32[]{:S(2)}, u32[]{:S(2)}) collective-permute-start(bf16[8,128,256]{2,1,0:T(8,128)(2,1)S(1)} %all-to-all-done), channel_id=1, source_target_pairs={{0,64},{64,128},{128,192},{192,256},{256,320},{320,384},{384,448},... | collective-permute-start | bytes 1572872 | tf_op jit(solution)/shard_map/ppermute | solution.py:76
  41.8 1.7 %multiply_reduce_fusion = f32[128,2]{1,0:T(8,128)} fusion(f32[128,2,128]{2,1,0:T(2,128)} %reshape.365), kind=kLoop, calls=%fused_computation.34 | loop fusion | flops 65280 | bytes 132096 | tf_op jit(solution)/shard_map/reduce_sum | solution.py:30
  43.5 0.9 copy.33
  44.4 8.3 %collective-permute-start.1 = (bf16[8,128,256]{2,1,0:T(8,128)(2,1)S(1)}, bf16[8,128,256]{2,1,0:T(8,128)(2,1)S(1)}, u32[]{:S(2)}, u32[]{:S(2)}) collective-permute-start(bf16[8,128,256]{2,1,0:T(8,128)(2,1)S(1)} %all-to-all-done), channel_id=1, source_target_pairs={{0,448},{64,0},{128,64},{192,128},{1,449},{65,1},{129,65},{193,129... | collective-permute-start | bytes 1572872 | tf_op jit(solution)/shard_map/ppermute | solution.py:77
  52.8 0.7 collective-permute-start.2
  53.9 9.4 %collective-permute-done.1 = bf16[8,128,256]{2,1,0:T(8,128)(2,1)S(1)} collective-permute-done((bf16[8,128,256]{2,1,0:T(8,128)(2,1)S(1)}, bf16[8,128,256]{2,1,0:T(8,128)(2,1)S(1)}, u32[]{:S(2)}, u32[]{:S(2)}) %collective-permute-start.1) | collective-permute-done | bytes 524320 | tf_op jit(solution)/shard_map/ppermute | solution.py:77
  63.2 5.6 %collective-permute-start.3 = (bf16[8,128,256]{2,1,0:T(8,128)(2,1)S(1)}, bf16[8,128,256]{2,1,0:T(8,128)(2,1)S(1)}, u32[]{:S(2)}, u32[]{:S(2)}) collective-permute-start(bf16[8,128,256]{2,1,0:T(8,128)(2,1)S(1)} %collective-permute-done.1), channel_id=1, source_target_pairs={{0,448},{64,0},{128,64},{448,384},{1,449},{65,1},{129,65},{449,385... | collective-permute-start | bytes 1572872 | tf_op jit(solution)/shard_map/ppermute | solution.py:77
  69.1 0.7 collective-permute-start.4
  69.8 0.7 collective-permute-start.6
  70.5 8.0 %collective-permute-done.3 = bf16[8,128,256]{2,1,0:T(8,128)(2,1)S(1)} collective-permute-done((bf16[8,128,256]{2,1,0:T(8,128)(2,1)S(1)}, bf16[8,128,256]{2,1,0:T(8,128)(2,1)S(1)}, u32[]{:S(2)}, u32[]{:S(2)}) %collective-permute-start.3) | collective-permute-done | bytes 524320 | tf_op jit(solution)/shard_map/ppermute | solution.py:77
  78.5 4.1 %collective-permute-start.5 = (bf16[4,128,256]{2,1,0:T(8,128)(2,1)S(1)}, bf16[4,128,256]{2,1,0:T(8,128)(2,1)S(1)}, u32[]{:S(2)}, u32[]{:S(2)}) collective-permute-start(bf16[4,128,256]{2,1,0:T(8,128)(2,1)S(1)} %slice.58), channel_id=1, source_target_pairs={{0,384},{64,448},{384,256},{448,320},{1,385},{65,449},{385,257},{4... | collective-permute-start | bytes 786440 | tf_op jit(solution)/shard_map/ppermute | solution.py:74
  82.7 3.9 %collective-permute-start.7 = (bf16[8,128,256]{2,1,0:T(8,128)(2,1)S(1)}, bf16[8,128,256]{2,1,0:T(8,128)(2,1)S(1)}, u32[]{:S(2)}, u32[]{:S(2)}) collective-permute-start(bf16[8,128,256]{2,1,0:T(8,128)(2,1)S(1)} %collective-permute-done.3), channel_id=1, source_target_pairs={{0,448},{64,0},{384,320},{448,384},{1,449},{65,1},{385,321},{449,3... | collective-permute-start | bytes 1572872 | tf_op jit(solution)/shard_map/ppermute | solution.py:77
  86.7 7.3 %collective-permute-done.5 = bf16[4,128,256]{2,1,0:T(8,128)(2,1)S(1)} collective-permute-done((bf16[4,128,256]{2,1,0:T(8,128)(2,1)S(1)}, bf16[4,128,256]{2,1,0:T(8,128)(2,1)S(1)}, u32[]{:S(2)}, u32[]{:S(2)}) %collective-permute-start.5) | collective-permute-done | bytes 262176 | tf_op jit(solution)/shard_map/ppermute | solution.py:74
  94.0 9.0 %collective-permute-done.7 = bf16[8,128,256]{2,1,0:T(8,128)(2,1)S(1)} collective-permute-done((bf16[8,128,256]{2,1,0:T(8,128)(2,1)S(1)}, bf16[8,128,256]{2,1,0:T(8,128)(2,1)S(1)}, u32[]{:S(2)}, u32[]{:S(2)}) %collective-permute-start.7) | collective-permute-done | bytes 524320 | tf_op jit(solution)/shard_map/ppermute | solution.py:77
  103.0 1.9 %fusion.47 = (f32[2,128]{1,0:T(2,128)S(1)}, f32[1,2,128,8192]{2,3,1,0:T(8,128)S(1)}) fusion(bf16[128,2,64]{2,0,1:T(8,128)(2,1)S(1)} %get-tuple-element.4, bf16[128,2,64]{2,0,1:T(8,128)(2,1)S(1)} %get-tuple-element.3, bf16[8192,256]{1,0:T(8,128)(2,1)S(1)} %bitcast.55, pred[128,8192]{0,1:T(8,128)(4,1)S(1)} %compare_and_fusion), kind=kOutput, calls=%fused_computation.91 | convolution fusion | flops 543293184 | bytes 11666432 | tf_op jit(solution)/shard_map/qhgd,khd->hgqk/dot_general | solution.py:146
  104.9 1.7 %fusion.2 = f32[2,128]{1,0:T(2,128)S(1)} fusion(f32[1,2,128,8192]{2,3,1,0:T(8,128)S(1)} %get-tuple-element.12, f32[2,128]{1,0:T(2,128)S(1)} %get-tuple-element.11, pred[128,8192]{0,1:T(8,128)(4,1)S(1)} %compare_and_fusion), kind=kLoop, calls=%fused_computation.4 | loop fusion | flops 6291200 | bytes 9439232 | tf_op jit(solution)/shard_map/reduce_sum | solution.py:153
  106.6 1.8 %fusion.24 = bf16[2,128,128]{1,2,0:T(8,128)(2,1)S(1)} fusion(bf16[8192,256]{1,0:T(8,128)(2,1)S(1)} %bitcast.56, f32[1,2,128,8192]{2,3,1,0:T(8,128)S(1)} %get-tuple-element.12, f32[2,128]{1,0:T(2,128)S(1)} %get-tuple-element.11, pred[128,8192]{0,1:T(8,128)(4,1)S(1)} %compare_and_fusion, f32[2,128]{1,0:T(2,128)S(1)} %fusion.2), kind=kOutput, calls=%fused_computation.27 | convolution fusion | flops 543227904 | bytes 11601920 | tf_op jit(solution)/shard_map/hgqk,khd->hgqd/dot_general | solution.py:154
  108.4 0.4 convolution_convert_fusion
  108.8 4.3 %all_to_all.15 = bf16[2,4,16,2560]{3,2,1,0:T(8,128)(2,1)S(1)} all-to-all(bf16[2,4,16,2560]{3,2,1,0:T(8,128)(2,1)S(1)} %bitcast.53), channel_id=1, replica_groups=mesh['z'=8,'x'=4,'ylo'=2,'yhi'=4,'core'=2] {'core'}, dimensions={0} | all-to-all | bytes 1310720 | tf_op jit(solution)/shard_map/all_to_all | solution.py:167
  113.1 0.9 reduce_sum.84
  114.0 4.7 %all-to-all-start.2 = ((bf16[4,16,2560]{2,1,0:T(8,128)(2,1)}), bf16[4,16,2560]{2,1,0:T(8,128)(2,1)S(1)}, u32[]{:S(2)}, u32[]{:S(2)}) async-start(bf16[4,16,2560]{2,1,0:T(8,128)(2,1)} %reduce_sum.84), calls=%async_computation.2 | async-start | bytes 655360 | tf_op jit(solution)/shard_map/all_to_all | solution.py:169
  118.7 0.7 pad_maximum_fusion.1
  119.3 12.0 %all-to-all-done.2 = bf16[4,16,2560]{2,1,0:T(8,128)(2,1)S(1)} async-done(((bf16[4,16,2560]{2,1,0:T(8,128)(2,1)}), bf16[4,16,2560]{2,1,0:T(8,128)(2,1)S(1)}, u32[]{:S(2)}, u32[]{:S(2)}) %all-to-all-start.2) | async-done | bytes 327712 | tf_op jit(solution)/shard_map/all_to_all | solution.py:169
  131.3 0.7 reduce_sum.85
  (65 shorter events, 2.3 us)
Async XLA Ops:
  0.6 107.8 %copy-start = (bf16[256,2560]{1,0:T(8,128)(2,1)S(1)}, bf16[256,2560]{1,0:T(8,128)(2,1)}, u32[]{:S(2)}) copy-start(bf16[256,2560]{1,0:T(8,128)(2,1)} %param.14) | copy-start | bytes 3932164
  19.0 3.6 %copy-start.8 = (s32[16]{0:T(128)S(1)}, s32[16]{0:T(128)}, u32[]{:S(2)}) copy-start(s32[16]{0:T(128)} %param.17) | copy-start | bytes 196
  19.0 4.1 %copy-start.6 = (f32[128]{0:T(128)S(1)}, f32[128]{0:T(128)}, u32[]{:S(2)}) copy-start(f32[128]{0:T(128)} %param.16) | copy-start | bytes 1540
  22.5 30.2 %copy-start.7 = (f32[128]{0:T(128)S(1)}, f32[128]{0:T(128)}, u32[]{:S(2)}) copy-start(f32[128]{0:T(128)} %param.15) | copy-start | bytes 1540
  22.6 8.3 %copy-start.5 = (bf16[128,128]{1,0:T(8,128)(2,1)}, bf16[128,128]{1,0:T(8,128)(2,1)S(1)}, u32[]{:S(2)}) copy-start(bf16[128,128]{1,0:T(8,128)(2,1)S(1)} %slice.94) | copy-start | bytes 98308
  23.5 0.9 copy-start.1
  23.5 0.9 copy-start.3
  24.5 14.9 %all-to-all-start = ((bf16[8,128,256]{2,1,0:T(8,128)(2,1)}), bf16[8,128,256]{2,1,0:T(8,128)(2,1)S(1)}, u32[]{:S(2)}, u32[]{:S(2)}) async-start(bf16[8,128,256]{2,1,0:T(8,128)(2,1)} %broadcast_in_dim.31), calls=%async_computation | async-start | bytes 1048576 | tf_op jit(solution)/shard_map/all_to_all | solution.py:134
  39.4 13.5 %collective-permute-start = (bf16[8,128,256]{2,1,0:T(8,128)(2,1)S(1)}, bf16[8,128,256]{2,1,0:T(8,128)(2,1)S(1)}, u32[]{:S(2)}, u32[]{:S(2)}) collective-permute-start(bf16[8,128,256]{2,1,0:T(8,128)(2,1)S(1)} %all-to-all-done), channel_id=1, source_target_pairs={{0,64},{64,128},{128,192},{192,256},{256,320},{320,384},{384,448},... | collective-permute-start | bytes 1572872 | tf_op jit(solution)/shard_map/ppermute | solution.py:76
  44.4 18.8 %collective-permute-start.1 = (bf16[8,128,256]{2,1,0:T(8,128)(2,1)S(1)}, bf16[8,128,256]{2,1,0:T(8,128)(2,1)S(1)}, u32[]{:S(2)}, u32[]{:S(2)}) collective-permute-start(bf16[8,128,256]{2,1,0:T(8,128)(2,1)S(1)} %all-to-all-done), channel_id=1, source_target_pairs={{0,448},{64,0},{128,64},{192,128},{1,449},{65,1},{129,65},{193,129... | collective-permute-start | bytes 1572872 | tf_op jit(solution)/shard_map/ppermute | solution.py:77
  52.8 16.2 %collective-permute-start.2 = (bf16[8,128,256]{2,1,0:T(8,128)(2,1)S(1)}, bf16[8,128,256]{2,1,0:T(8,128)(2,1)S(1)}, u32[]{:S(2)}, u32[]{:S(2)}) collective-permute-start(bf16[8,128,256]{2,1,0:T(8,128)(2,1)S(1)} %collective-permute-done), channel_id=1, source_target_pairs={{64,128},{128,192},{192,256},{256,320},{320,384},{384,448},{65,129... | collective-permute-start | bytes 1572872 | tf_op jit(solution)/shard_map/ppermute | solution.py:76
  63.2 15.3 %collective-permute-start.3 = (bf16[8,128,256]{2,1,0:T(8,128)(2,1)S(1)}, bf16[8,128,256]{2,1,0:T(8,128)(2,1)S(1)}, u32[]{:S(2)}, u32[]{:S(2)}) collective-permute-start(bf16[8,128,256]{2,1,0:T(8,128)(2,1)S(1)} %collective-permute-done.1), channel_id=1, source_target_pairs={{0,448},{64,0},{128,64},{448,384},{1,449},{65,1},{129,65},{449,385... | collective-permute-start | bytes 1572872 | tf_op jit(solution)/shard_map/ppermute | solution.py:77
  69.1 17.5 %collective-permute-start.4 = (bf16[4,128,256]{2,1,0:T(8,128)(2,1)S(1)}, bf16[4,128,256]{2,1,0:T(8,128)(2,1)S(1)}, u32[]{:S(2)}, u32[]{:S(2)}) collective-permute-start(bf16[4,128,256]{2,1,0:T(8,128)(2,1)S(1)} %slice.57), channel_id=1, source_target_pairs={{128,256},{192,320},{256,384},{320,448},{129,257},{193,321},{257,3... | collective-permute-start | bytes 786440 | tf_op jit(solution)/shard_map/ppermute | solution.py:70
  69.8 24.2 %collective-permute-start.6 = (bf16[8,128,256]{2,1,0:T(8,128)(2,1)S(1)}, bf16[8,128,256]{2,1,0:T(8,128)(2,1)S(1)}, u32[]{:S(2)}, u32[]{:S(2)}) collective-permute-start(bf16[8,128,256]{2,1,0:T(8,128)(2,1)S(1)} %collective-permute-done.2), channel_id=1, source_target_pairs={{128,192},{192,256},{256,320},{320,384},{384,448},{129,193},{193,2... | collective-permute-start | bytes 1572872 | tf_op jit(solution)/shard_map/ppermute | solution.py:76
  78.5 15.4 %collective-permute-start.5 = (bf16[4,128,256]{2,1,0:T(8,128)(2,1)S(1)}, bf16[4,128,256]{2,1,0:T(8,128)(2,1)S(1)}, u32[]{:S(2)}, u32[]{:S(2)}) collective-permute-start(bf16[4,128,256]{2,1,0:T(8,128)(2,1)S(1)} %slice.58), channel_id=1, source_target_pairs={{0,384},{64,448},{384,256},{448,320},{1,385},{65,449},{385,257},{4... | collective-permute-start | bytes 786440 | tf_op jit(solution)/shard_map/ppermute | solution.py:74
  82.7 20.3 %collective-permute-start.7 = (bf16[8,128,256]{2,1,0:T(8,128)(2,1)S(1)}, bf16[8,128,256]{2,1,0:T(8,128)(2,1)S(1)}, u32[]{:S(2)}, u32[]{:S(2)}) collective-permute-start(bf16[8,128,256]{2,1,0:T(8,128)(2,1)S(1)} %collective-permute-done.3), channel_id=1, source_target_pairs={{0,448},{64,0},{384,320},{448,384},{1,449},{65,1},{385,321},{449,3... | collective-permute-start | bytes 1572872 | tf_op jit(solution)/shard_map/ppermute | solution.py:77
  108.4 10.3 %copy-start.2 = (bf16[128,64]{1,0:T(8,128)(2,1)S(1)}, bf16[128,64]{1,0:T(8,128)(2,1)}, u32[]{:S(2)}) copy-start(bf16[128,64]{1,0:T(8,128)(2,1)} %copy-done.1) | copy-start | bytes 49156
  108.4 10.3 %copy-start.4 = (bf16[128,64]{1,0:T(8,128)(2,1)S(1)}, bf16[128,64]{1,0:T(8,128)(2,1)}, u32[]{:S(2)}) copy-start(bf16[128,64]{1,0:T(8,128)(2,1)} %copy-done.3) | copy-start | bytes 49156
  114.0 17.3 %all-to-all-start.2 = ((bf16[4,16,2560]{2,1,0:T(8,128)(2,1)}), bf16[4,16,2560]{2,1,0:T(8,128)(2,1)S(1)}, u32[]{:S(2)}, u32[]{:S(2)}) async-start(bf16[4,16,2560]{2,1,0:T(8,128)(2,1)} %reduce_sum.84), calls=%async_computation.2 | async-start | bytes 655360 | tf_op jit(solution)/shard_map/all_to_all | solution.py:169
